TPU v7x, 512 devices: a whole 4x4x16 slice. The times are simulated.
512 devices in a mesh: tok: 64 (over z, x), head: 8 (over y, core).
Axes of the slice: x: 4, y: 4, z: 16, core: 2. Of those that a mesh axis runs over, the one named last changes fastest.
Arguments:
- tokens: bfloat16 [32768, 2560], P('tok', 'head'), may hold values from -6 to 6
- query_weight: bfloat16 [2560, 2560], P('tok'), may hold values from -0.125 to 0.125
- keyvalue_weight: bfloat16 [2560, 512], P('tok'), may hold values from -0.125 to 0.125
- output_weight: bfloat16 [2560, 2560], P(None, ('head', 'tok')), may hold values from -0.125 to 0.125
- cache: bfloat16 [2048, 2, 128, 256], P(('tok', 'head')), may hold values from -460 to 460
- page_table: int32 [512, 4], P('tok'), may hold values from 0 to 2047, as said below
- parents: int32 [512, 64], P('tok'), may hold values from 0 to 62, as said below
- cache_len: int32 [512], P('tok'), may hold values from 1 to 448, as said below
- accepted_leaf: int32 [512], P('tok'), may hold values from 0 to 63
Outputs:
- attended: bfloat16 [32768, 2560], P('tok', 'head')
- cache_out: bfloat16 [2048, 2, 128, 256], P(('tok', 'head'))
Inputs may be any that keep to these rules, and one draw needn't show every extreme that they name: `page_table`: for every d, row d names each of the pages d * 4 to d * 4 + 3 exactly once, so request d's pages all lie on device d (devices counted tok-major, head-minor). parents[r, 0] = 0, and parents[r, i] < i for i >= 1. `cache_len`: roughly half of the requests hold at most 128 cached positions, the others more than 320.
All inputs are finite; a program needn't handle non-finite values.
Results may differ from a plain program's by a relative error of at most 0.014.
The roundings to bfloat16 on the way count: a program that leaves them out, or rounds other values in their place, can miss the bound.
Values may be sent and summed in bfloat16 or wider, within the bound.
No kernel may reach another device: no remote copies, remote signals or barrier semaphores. Data moves between devices by JAX's collectives and lax.ppermute only.
A program may use at most 64 MiB of HBM per device.

v0:
```python
import math

import jax
import jax.numpy as jnp
from jax import lax
from jax.sharding import Mesh, PartitionSpec as P

HQ = 10
HD = 256
DRAFT = 64
PAGE = 128
NPR = 4
WINDOW = 256


def ancestry(parent_row):
    node_ids = jnp.arange(DRAFT, dtype=jnp.int32)
    link = (parent_row[:, None] == node_ids[None, :]).astype(jnp.float32)
    reach = jnp.minimum(link + jnp.eye(DRAFT, dtype=jnp.float32), 1.0)
    for sweep in range((DRAFT - 1).bit_length()):
        reach = jnp.minimum(jnp.dot(reach, reach, precision=lax.Precision.HIGHEST), 1.0)
    depth = (jnp.sum(reach, axis=1) - 1.0).astype(jnp.int32)
    return (reach, depth)


def rotate(values, position):
    half = HD // 4
    freq = jnp.exp(jnp.arange(half, dtype=jnp.float32) * (-2.0 * math.log(10000.0) / (HD // 2)))
    angle = position.astype(jnp.float32)[..., None] * freq
    cosine = jnp.cos(angle)
    sine = jnp.sin(angle)
    first = values[..., :half]
    second = values[..., half : 2 * half]
    return jnp.concatenate(
        [first * cosine - second * sine, second * cosine + first * sine, values[..., 2 * half :]],
        axis=-1,
    )


def attend(queries, cache_keys, cache_values, tree_keys, tree_values, lengths, position, reach):
    window_span = cache_keys.shape[1]
    slot_ids = jnp.arange(window_span, dtype=jnp.int32)
    visible = (slot_ids[None, None, :] < lengths[:, None, None]) & (
        slot_ids[None, None, :] > position[:, :, None] - WINDOW
    )
    cache_scores = jnp.einsum(
        "rnhd,rcd->rhnc", queries, cache_keys, preferred_element_type=jnp.float32
    )
    tree_scores = jnp.einsum(
        "rnhd,rmd->rhnm", queries, tree_keys, preferred_element_type=jnp.float32
    )
    cache_scores = jnp.where(visible[:, None], cache_scores, -1e30)
    tree_scores = jnp.where(reach[:, None] > 0.5, tree_scores, -1e30)
    row_peak = jnp.maximum(jnp.max(cache_scores, axis=-1), jnp.max(tree_scores, axis=-1))[..., None]
    cache_weights = jnp.exp(cache_scores - row_peak)
    tree_weights = jnp.exp(tree_scores - row_peak)
    denominator = jnp.sum(cache_weights, axis=-1, keepdims=True) + jnp.sum(
        tree_weights, axis=-1, keepdims=True
    )
    cache_weights = (cache_weights / denominator).astype(jnp.bfloat16)
    tree_weights = (tree_weights / denominator).astype(jnp.bfloat16)
    result = jnp.einsum(
        "rhnc,rcd->rnhd", cache_weights, cache_values, preferred_element_type=jnp.float32
    )
    result = result + jnp.einsum(
        "rhnm,rmd->rnhd", tree_weights, tree_values, preferred_element_type=jnp.float32
    )
    return result.astype(jnp.bfloat16)


def refresh(logical_pages, length, leaf, reach, depth, new_keys, new_values):
    count = logical_pages.shape[0] * logical_pages.shape[2]
    logical = jnp.transpose(logical_pages, (1, 0, 2, 3)).reshape(2, count, HD)
    slot_ids = jnp.arange(count, dtype=jnp.int32)
    on_path = reach[leaf]
    selector = ((on_path[None, :] > 0.5) & (depth[None, :] == slot_ids[:, None] - length)).astype(
        jnp.float32
    )
    placed_keys = jnp.dot(selector, new_keys.astype(jnp.float32), precision=lax.Precision.HIGHEST)
    placed_values = jnp.dot(
        selector, new_values.astype(jnp.float32), precision=lax.Precision.HIGHEST
    )
    placed = jnp.stack([placed_keys, placed_values]).astype(jnp.bfloat16)
    written = jnp.sum(selector, axis=1) > 0.5
    logical = jnp.where(written[None, :, None], placed, logical)
    return jnp.transpose(
        logical.reshape(2, logical_pages.shape[0], logical_pages.shape[2], HD), (1, 0, 2, 3)
    )


def ring_gather(piece, axis):
    size = lax.axis_size(axis)
    if size == 1:
        return piece[None]
    index = lax.axis_index(axis)
    by_offset = {0: piece}
    ahead = piece
    behind = piece
    for step in range(1, size // 2 + 1):
        ahead = lax.ppermute(ahead, axis, [(i, (i + 1) % size) for i in range(size)])
        by_offset[size - step] = ahead
        if step <= (size - 1) // 2:
            behind = lax.ppermute(behind, axis, [(i, (i - 1) % size) for i in range(size)])
            by_offset[step] = behind
    placed = jnp.zeros((size,) + piece.shape, piece.dtype)
    for offset in range(size):
        placed = lax.dynamic_update_slice_in_dim(
            placed, by_offset[offset][None], (index + offset) % size, axis=0
        )
    return placed


def grid_gather(piece):
    lanes = 128
    inner = ring_gather(piece.reshape(-1, lanes), "tx")
    outer = ring_gather(inner.reshape(-1, lanes), "tz")
    return outer.reshape(-1, piece.shape[0])


def shards(
    tokens,
    query_weight,
    keyvalue_weight,
    output_weight,
    cache,
    page_table,
    parents,
    cache_len,
    accepted_leaf,
):
    head_count = lax.axis_size("head")
    head_index = lax.axis_index("head")
    tok_index = lax.axis_index("tz") * lax.axis_size("tx") + lax.axis_index("tx")
    requests = parents.shape[0]
    assert requests == head_count
    pages_dev = cache.shape[0]
    part_rows = query_weight.shape[0]
    q_cols = (HQ * HD) // head_count
    kv_cols = (2 * HD) // head_count
    out_cols = output_weight.shape[1]
    wq_piece = lax.dynamic_slice_in_dim(query_weight, head_index * q_cols, q_cols, axis=1)
    wkv_piece = lax.dynamic_slice_in_dim(keyvalue_weight, head_index * kv_cols, kv_cols, axis=1)
    flat = jnp.concatenate(
        [wq_piece.reshape(-1), wkv_piece.reshape(-1), output_weight.reshape(-1)]
    )
    stacked = grid_gather(flat)
    tok_count = stacked.shape[0]
    n_q = part_rows * q_cols
    n_kv = part_rows * kv_cols
    wq_cols = stacked[:, :n_q].reshape(tok_count * part_rows, q_cols)
    wkv_cols = stacked[:, n_q : n_q + n_kv].reshape(tok_count * part_rows, kv_cols)
    wo_cols = (
        stacked[:, n_q + n_kv :]
        .reshape(tok_count, HQ * HD, out_cols)
        .transpose(1, 0, 2)
        .reshape(HQ * HD, tok_count * out_cols)
    )
    gathered = lax.all_gather(tokens, "head", axis=1, tiled=True)
    wide = gathered.astype(jnp.float32)
    mean_square = jnp.mean(wide * wide, axis=1, keepdims=True)
    normed = (wide * lax.rsqrt(mean_square + 1e-06)).astype(jnp.bfloat16)
    q_part = jnp.dot(normed, wq_cols, preferred_element_type=jnp.float32)
    kv_part = jnp.dot(normed, wkv_cols, preferred_element_type=jnp.float32)
    both = jnp.concatenate([q_part, kv_part], axis=1)
    mine = lax.all_to_all(both, "head", 0, 1, tiled=True)
    mine = mine.reshape(DRAFT, head_count, q_cols + kv_cols)
    q_pre = mine[:, :, :q_cols].reshape(DRAFT, HQ, HD)
    kv_pre = mine[:, :, q_cols:].reshape(DRAFT, 2 * HD)
    parent_row = lax.dynamic_index_in_dim(parents, head_index, 0, keepdims=False)
    length = lax.dynamic_index_in_dim(cache_len, head_index, 0, keepdims=False)
    leaf = lax.dynamic_index_in_dim(accepted_leaf, head_index, 0, keepdims=False)
    reach, depth = ancestry(parent_row)
    position = length + depth
    queries = (rotate(q_pre, position[:, None]) * HD ** (-0.5)).astype(jnp.bfloat16)
    tree_keys = rotate(kv_pre[:, :HD], position).astype(jnp.bfloat16)
    tree_values = kv_pre[:, HD:].astype(jnp.bfloat16)
    device = tok_index * head_count + head_index
    own_table = (
        lax.dynamic_index_in_dim(page_table, head_index, 0, keepdims=False) - device * pages_dev
    )
    own_pages = jnp.take(cache, own_table, axis=0)
    cache_keys = own_pages[:, 0].reshape(NPR * PAGE, HD)
    cache_values = own_pages[:, 1].reshape(NPR * PAGE, HD)
    result = attend(
        queries[None],
        cache_keys[None],
        cache_values[None],
        tree_keys[None],
        tree_values[None],
        length[None],
        position[None],
        reach[None],
    )
    mixed = lax.all_gather(result.reshape(DRAFT, HQ * HD), "head", axis=0, tiled=True)
    summed = jnp.zeros((mixed.shape[0], wo_cols.shape[1]), jnp.float32)
    for group in range(head_count):
        head_ids = [k for k in range(group, HQ, head_count)]
        if not head_ids:
            continue
        partial_value = None
        for k in head_ids:
            term = jnp.dot(
                mixed[:, k * HD : (k + 1) * HD],
                wo_cols[k * HD : (k + 1) * HD],
                preferred_element_type=jnp.float32,
            )
            partial_value = term if partial_value is None else partial_value + term
        summed = summed + partial_value.astype(jnp.bfloat16).astype(jnp.float32)
    attended = summed.astype(jnp.bfloat16)
    new_pages = refresh(own_pages, length, leaf, reach, depth, tree_keys, tree_values)
    matches = (own_table[:, None] == jnp.arange(pages_dev, dtype=jnp.int32)[None, :]).astype(
        jnp.int32
    )
    inverse = jnp.sum(matches * jnp.arange(pages_dev, dtype=jnp.int32)[:, None], axis=0)
    cache_out = jnp.take(new_pages, inverse, axis=0)
    return (attended, cache_out)


def solution(mesh):
    tok_size = mesh.shape["tok"]
    tx_size = 4 if tok_size % 4 == 0 else tok_size
    grid = Mesh(
        mesh.devices.reshape(tok_size // tx_size, tx_size, mesh.shape["head"]),
        ("tz", "tx", "head"),
    )
    tok = ("tz", "tx")
    in_specs = (
        P(tok, "head"),
        P(tok, None),
        P(tok, None),
        P(None, ("head",) + tok),
        P(tok + ("head",), None, None, None),
        P(tok, None),
        P(tok, None),
        P(tok),
        P(tok),
    )
    out_specs = (P(tok, "head"), P(tok + ("head",), None, None, None))
    return jax.shard_map(shards, mesh=grid, in_specs=in_specs, out_specs=out_specs, check_vma=False)
```

profile of v0, /device:TPU:1, one launch (start us, length us, event | category | flops | bytes accessed | tf_op | source)
XLA Modules:
  0.0 223.0 jit_solution(783145941364720500)
XLA Ops:
  7.2 0.9 constant_dynamic-slice_fusion.2
  8.3 0.8 constant_dynamic-slice_fusion.1
  9.1 1.2 copy.63
  10.3 1.0 reshape.343
  12.1 5.2 %collective-permute-start = (bf16[220,128]{1,0:T(8,128)(2,1)S(1)}, bf16[220,128]{1,0:T(8,128)(2,1)S(1)}, u32[]{:S(2)}, u32[]{:S(2)}) collective-permute-start(bf16[220,128]{1,0:T(8,128)(2,1)S(1)} %bitcast.160), channel_id=1, source_target_pairs={{0,24},{8,0},{16,8},{24,16},{1,25},{9,1},{17,9},{25,17},{2,26},{10... | collective-permute-start | bytes 168968 | tf_op jit(solution)/shard_map/ppermute | solution.py:103
  17.3 1.9 collective-permute-start.1
  19.5 1.2 dynamic_slice.29
  22.1 0.9 fusion.67
  24.8 1.2 dynamic_slice.25
  27.9 2.1 collective-permute-start.2
  30.0 4.0 %collective-permute-done.2 = bf16[220,128]{1,0:T(8,128)(2,1)S(1)} collective-permute-done((bf16[220,128]{1,0:T(8,128)(2,1)S(1)}, bf16[220,128]{1,0:T(8,128)(2,1)S(1)}, u32[]{:S(2)}, u32[]{:S(2)}) %collective-permute-start.2) | collective-permute-done | bytes 56352 | tf_op jit(solution)/shard_map/ppermute | solution.py:100
  34.1 11.1 %collective-permute-start.3 = (bf16[880,128]{1,0:T(8,128)(2,1)S(1)}, bf16[880,128]{1,0:T(8,128)(2,1)S(1)}, u32[]{:S(2)}, u32[]{:S(2)}) collective-permute-start(bf16[880,128]{1,0:T(8,128)(2,1)S(1)} %reshape.345), channel_id=1, source_target_pairs={{0,480},{32,0},{64,32},{96,64},{128,96},{160,128},{192,160},{224,1... | collective-permute-start | bytes 675848 | tf_op jit(solution)/shard_map/ppermute | solution.py:103
  45.2 1.9 collective-permute-start.10
  47.2 2.3 %broadcast_in_dim.125 = bf16[16,880,128]{2,1,0:T(8,128)(2,1)} broadcast(bf16[]{:T(256)} %constant.175.clone.1), dimensions={} | broadcast | bytes 3604482 | tf_op jit(solution)/shard_map/broadcast_in_dim | solution.py:105
  50.2 4.6 %collective-permute-start.4 = (bf16[880,128]{1,0:T(8,128)(2,1)S(1)}, bf16[880,128]{1,0:T(8,128)(2,1)S(1)}, u32[]{:S(2)}, u32[]{:S(2)}) collective-permute-start(bf16[880,128]{1,0:T(8,128)(2,1)S(1)} %collective-permute-done.3), channel_id=1, source_target_pairs={{0,480},{32,0},{64,32},{96,64},{128,96},{160,128},{192,160},{224,1... | collective-permute-start | bytes 675848 | tf_op jit(solution)/shard_map/ppermute | solution.py:103
  54.8 1.9 collective-permute-start.11
  57.7 5.0 %collective-permute-start.5 = (bf16[880,128]{1,0:T(8,128)(2,1)S(1)}, bf16[880,128]{1,0:T(8,128)(2,1)S(1)}, u32[]{:S(2)}, u32[]{:S(2)}) collective-permute-start(bf16[880,128]{1,0:T(8,128)(2,1)S(1)} %collective-permute-done.4), channel_id=1, source_target_pairs={{0,480},{32,0},{64,32},{96,64},{128,96},{160,128},{192,160},{224,1... | collective-permute-start | bytes 675848 | tf_op jit(solution)/shard_map/ppermute | solution.py:103
  62.7 1.9 collective-permute-start.12
  65.6 5.0 %collective-permute-start.6 = (bf16[880,128]{1,0:T(8,128)(2,1)S(1)}, bf16[880,128]{1,0:T(8,128)(2,1)S(1)}, u32[]{:S(2)}, u32[]{:S(2)}) collective-permute-start(bf16[880,128]{1,0:T(8,128)(2,1)S(1)} %collective-permute-done.5), channel_id=1, source_target_pairs={{0,480},{32,0},{64,32},{96,64},{128,96},{160,128},{192,160},{224,1... | collective-permute-start | bytes 675848 | tf_op jit(solution)/shard_map/ppermute | solution.py:103
  70.6 1.9 collective-permute-start.13
  73.5 5.0 %collective-permute-start.7 = (bf16[880,128]{1,0:T(8,128)(2,1)S(1)}, bf16[880,128]{1,0:T(8,128)(2,1)S(1)}, u32[]{:S(2)}, u32[]{:S(2)}) collective-permute-start(bf16[880,128]{1,0:T(8,128)(2,1)S(1)} %collective-permute-done.6), channel_id=1, source_target_pairs={{0,480},{32,0},{64,32},{96,64},{128,96},{160,128},{192,160},{224,1... | collective-permute-start | bytes 675848 | tf_op jit(solution)/shard_map/ppermute | solution.py:103
  78.6 1.9 collective-permute-start.14
  81.4 5.0 %collective-permute-start.8 = (bf16[880,128]{1,0:T(8,128)(2,1)S(1)}, bf16[880,128]{1,0:T(8,128)(2,1)S(1)}, u32[]{:S(2)}, u32[]{:S(2)}) collective-permute-start(bf16[880,128]{1,0:T(8,128)(2,1)S(1)} %collective-permute-done.7), channel_id=1, source_target_pairs={{0,480},{32,0},{64,32},{96,64},{128,96},{160,128},{192,160},{224,1... | collective-permute-start | bytes 675848 | tf_op jit(solution)/shard_map/ppermute | solution.py:103
  86.7 1.9 collective-permute-start.15
  89.3 1.1 collective-permute-done.8
  90.4 5.0 %collective-permute-start.9 = (bf16[880,128]{1,0:T(8,128)(2,1)S(1)}, bf16[880,128]{1,0:T(8,128)(2,1)S(1)}, u32[]{:S(2)}, u32[]{:S(2)}) collective-permute-start(bf16[880,128]{1,0:T(8,128)(2,1)S(1)} %collective-permute-done.8), channel_id=1, source_target_pairs={{0,480},{32,0},{64,32},{96,64},{128,96},{160,128},{192,160},{224,1... | collective-permute-start | bytes 675848 | tf_op jit(solution)/shard_map/ppermute | solution.py:103
  95.9 1.9 collective-permute-start.16
  97.9 0.7 bitcast_dynamic-update-slice_fusion.9
  98.6 7.9 %collective-permute-done.16 = bf16[880,128]{1,0:T(8,128)(2,1)S(1)} collective-permute-done((bf16[880,128]{1,0:T(8,128)(2,1)S(1)}, bf16[880,128]{1,0:T(8,128)(2,1)S(1)}, u32[]{:S(2)}, u32[]{:S(2)}) %collective-permute-start.16) | collective-permute-done | bytes 225312 | tf_op jit(solution)/shard_map/ppermute | solution.py:100
  106.5 1.9 collective-permute-start.17
  109.1 7.1 %collective-permute-done.17 = bf16[880,128]{1,0:T(8,128)(2,1)S(1)} collective-permute-done((bf16[880,128]{1,0:T(8,128)(2,1)S(1)}, bf16[880,128]{1,0:T(8,128)(2,1)S(1)}, u32[]{:S(2)}, u32[]{:S(2)}) %collective-permute-start.17) | collective-permute-done | bytes 225312 | tf_op jit(solution)/shard_map/ppermute | solution.py:100
  120.4 0.7 bitcast_dynamic-update-slice_fusion.1
  121.9 6.6 %reshape.346 = bf16[64,28160]{1,0:T(8,128)(2,1)} reshape(bf16[16,880,128]{2,1,0:T(8,128)(2,1)} %bitcast_dynamic-update-slice_fusion) | data formatting | bytes 7208960 | tf_op jit(solution)/shard_map/reshape | solution.py:117
  128.5 3.4 %fusion.75 = (bf16[64,12800]{1,0:T(8,128)(2,1)S(1)}, bf16[64,12800]{1,0:T(8,128)(2,1)}) fusion(bf16[64,28160]{1,0:T(8,128)(2,1)} %reshape.346), kind=kLoop, calls=%fused_computation.159 | loop fusion | bytes 6553600 | tf_op jit(solution)/shard_map/slice | solution.py:150
  131.9 2.5 %reshape.347 = bf16[2560,320]{1,0:T(8,128)(2,1)} reshape(bf16[64,12800]{1,0:T(8,128)(2,1)S(1)} %get-tuple-element.15) | data formatting | bytes 3276800 | tf_op jit(solution)/shard_map/reshape | solution.py:150
  134.7 2.5 %fusion = f32[512]{0:T(512)S(1)} fusion(bf16[512,2560]{0,1:T(8,128)(2,1)} %all-gather.3.cloned.1.call-done), kind=kLoop, calls=%fused_computation.4 | loop fusion | flops 3931648 | bytes 2623488 | tf_op jit(solution)/shard_map/reduce_sum | solution.py:160
  137.3 3.0 %fusion.4 = f32[512,320]{0,1:T(8,128)S(1)} fusion(bf16[2560,320]{1,0:T(8,128)(2,1)S(1)} %copy-done.5, bf16[512,2560]{0,1:T(8,128)(2,1)} %all-gather.3.cloned.1.call-done, f32[512]{0:T(512)S(1)} %add_rsqrt_fusion), kind=kOutput, calls=%fused_computation.7 | convolution fusion | flops 842792960 | bytes 4917248 | tf_op jit(solution)/shard_map/dot_general | solution.py:162
  141.1 1.2 copy.64
  142.3 14.9 %all-to-all-start = ((f32[8,64,384]{2,1,0:T(8,128)}), f32[8,64,384]{2,1,0:T(8,128)S(1)}, u32[]{:S(2)}, u32[]{:S(2)}) async-start(f32[8,64,384]{2,1,0:T(8,128)} %bitcast.26), calls=%async_computation | async-start | bytes 1572864 | tf_op jit(solution)/shard_map/all_to_all | solution.py:165
  159.3 10.0 %all-to-all-done = f32[8,64,384]{2,1,0:T(8,128)S(1)} async-done(((f32[8,64,384]{2,1,0:T(8,128)}), f32[8,64,384]{2,1,0:T(8,128)S(1)}, u32[]{:S(2)}, u32[]{:S(2)}) %all-to-all-start) | async-done | bytes 786464 | tf_op jit(solution)/shard_map/all_to_all | solution.py:165
  171.8 1.0 fusion.32
  175.3 0.7 copy.90
  176.3 2.9 %copy.73 = bf16[64,12800]{0,1:T(8,128)(2,1)} copy(bf16[64,12800]{1,0:T(8,128)(2,1)S(1)} %copy-done.1) | data formatting | bytes 3276800 | tf_op jit(solution)/shard_map/slice | solution.py:153
  179.3 7.1 %reshape.354 = bf16[64,2560,5]{0,2,1:T(8,128)(2,1)} reshape(bf16[64,12800]{0,1:T(8,128)(2,1)} %copy.73) | data formatting | bytes 3276800 | tf_op jit(solution)/shard_map/reshape | solution.py:154
  186.4 4.6 %fusion.74 = (bf16[256,64,5]{1,2,0:T(8,128)(2,1)S(1)}, bf16[256,64,5]{1,2,0:T(8,128)(2,1)S(1)}, bf16[256,64,5]{1,2,0:T(8,128)(2,1)S(1)}, bf16[256,64,5]{1,2,0:T(...) fusion(bf16[2560,64,5]{1,2,0:T(8,128)(2,1)} %bitcast.152), kind=kLoop, calls=%fused_computation.158 | loop fusion | bytes 3276800 | tf_op jit(solution)/shard_map/slice | solution.py:204
  191.0 1.5 copy.74
  192.5 0.7 slice.154
  193.2 1.5 copy.76
  194.7 0.7 slice.160
  195.5 1.5 copy.77
  196.9 0.7 slice.163
  197.7 1.5 copy.78
  199.2 0.7 slice.166
  199.9 1.5 copy.79
  201.4 0.7 slice.169
  202.6 0.8 slice.172
  203.8 0.7 slice.175
  205.6 0.7 slice.181
  207.5 0.9 broadcast_select_fusion
  208.4 1.4 fusion.44
  209.8 1.3 fusion.41
  211.1 1.2 fusion.25
  212.3 1.2 fusion.24
  215.0 1.2 fusion.16
  (142 shorter events, 28.5 us)
Async XLA Ops:
  7.2 150.8 %copy-start = (bf16[4,2,128,256]{3,2,1,0:T(8,128)(2,1)S(1)}, bf16[4,2,128,256]{3,2,1,0:T(8,128)(2,1)}, u32[]{:S(2)}) copy-start(bf16[4,2,128,256]{3,2,1,0:T(8,128)(2,1)} %param.15) | copy-start | bytes 1572868
  7.2 127.5 %all-gather.3.cloned.1.call-start = ((), (), s32[]{:S(2)}) async-start(), calls=%async_computation.1 | async-start | bytes 2949120 | tf_op jit(solution)/shard_map/all_gather | solution.py:158
  12.1 17.9 %collective-permute-start = (bf16[220,128]{1,0:T(8,128)(2,1)S(1)}, bf16[220,128]{1,0:T(8,128)(2,1)S(1)}, u32[]{:S(2)}, u32[]{:S(2)}) collective-permute-start(bf16[220,128]{1,0:T(8,128)(2,1)S(1)} %bitcast.160), channel_id=1, source_target_pairs={{0,24},{8,0},{16,8},{24,16},{1,25},{9,1},{17,9},{25,17},{2,26},{10... | collective-permute-start | bytes 168968 | tf_op jit(solution)/shard_map/ppermute | solution.py:103
  17.3 10.5 %collective-permute-start.1 = (bf16[220,128]{1,0:T(8,128)(2,1)S(1)}, bf16[220,128]{1,0:T(8,128)(2,1)S(1)}, u32[]{:S(2)}, u32[]{:S(2)}) collective-permute-start(bf16[220,128]{1,0:T(8,128)(2,1)S(1)} %bitcast.161), channel_id=1, source_target_pairs={{0,8},{8,16},{16,24},{24,0},{1,9},{9,17},{17,25},{25,1},{2,10},{10... | collective-permute-start | bytes 168968 | tf_op jit(solution)/shard_map/ppermute | solution.py:100
  27.9 6.1 %collective-permute-start.2 = (bf16[220,128]{1,0:T(8,128)(2,1)S(1)}, bf16[220,128]{1,0:T(8,128)(2,1)S(1)}, u32[]{:S(2)}, u32[]{:S(2)}) collective-permute-start(bf16[220,128]{1,0:T(8,128)(2,1)S(1)} %collective-permute-done.1), channel_id=1, source_target_pairs={{0,8},{8,16},{16,24},{24,0},{1,9},{9,17},{17,25},{25,1},{2,10},{10... | collective-permute-start | bytes 168968 | tf_op jit(solution)/shard_map/ppermute | solution.py:100
  34.1 16.1 %collective-permute-start.3 = (bf16[880,128]{1,0:T(8,128)(2,1)S(1)}, bf16[880,128]{1,0:T(8,128)(2,1)S(1)}, u32[]{:S(2)}, u32[]{:S(2)}) collective-permute-start(bf16[880,128]{1,0:T(8,128)(2,1)S(1)} %reshape.345), channel_id=1, source_target_pairs={{0,480},{32,0},{64,32},{96,64},{128,96},{160,128},{192,160},{224,1... | collective-permute-start | bytes 675848 | tf_op jit(solution)/shard_map/ppermute | solution.py:103
  45.2 9.6 %collective-permute-start.10 = (bf16[880,128]{1,0:T(8,128)(2,1)S(1)}, bf16[880,128]{1,0:T(8,128)(2,1)S(1)}, u32[]{:S(2)}, u32[]{:S(2)}) collective-permute-start(bf16[880,128]{1,0:T(8,128)(2,1)S(1)} %reshape.345), channel_id=1, source_target_pairs={{0,32},{32,64},{64,96},{96,128},{128,160},{160,192},{192,224},{224... | collective-permute-start | bytes 675848 | tf_op jit(solution)/shard_map/ppermute | solution.py:100
  50.2 7.5 %collective-permute-start.4 = (bf16[880,128]{1,0:T(8,128)(2,1)S(1)}, bf16[880,128]{1,0:T(8,128)(2,1)S(1)}, u32[]{:S(2)}, u32[]{:S(2)}) collective-permute-start(bf16[880,128]{1,0:T(8,128)(2,1)S(1)} %collective-permute-done.3), channel_id=1, source_target_pairs={{0,480},{32,0},{64,32},{96,64},{128,96},{160,128},{192,160},{224,1... | collective-permute-start | bytes 675848 | tf_op jit(solution)/shard_map/ppermute | solution.py:103
  54.8 7.9 %collective-permute-start.11 = (bf16[880,128]{1,0:T(8,128)(2,1)S(1)}, bf16[880,128]{1,0:T(8,128)(2,1)S(1)}, u32[]{:S(2)}, u32[]{:S(2)}) collective-permute-start(bf16[880,128]{1,0:T(8,128)(2,1)S(1)} %collective-permute-done.10), channel_id=1, source_target_pairs={{0,32},{32,64},{64,96},{96,128},{128,160},{160,192},{192,224},{224... | collective-permute-start | bytes 675848 | tf_op jit(solution)/shard_map/ppermute | solution.py:100
  57.7 7.9 %collective-permute-start.5 = (bf16[880,128]{1,0:T(8,128)(2,1)S(1)}, bf16[880,128]{1,0:T(8,128)(2,1)S(1)}, u32[]{:S(2)}, u32[]{:S(2)}) collective-permute-start(bf16[880,128]{1,0:T(8,128)(2,1)S(1)} %collective-permute-done.4), channel_id=1, source_target_pairs={{0,480},{32,0},{64,32},{96,64},{128,96},{160,128},{192,160},{224,1... | collective-permute-start | bytes 675848 | tf_op jit(solution)/shard_map/ppermute | solution.py:103
  62.7 7.9 %collective-permute-start.12 = (bf16[880,128]{1,0:T(8,128)(2,1)S(1)}, bf16[880,128]{1,0:T(8,128)(2,1)S(1)}, u32[]{:S(2)}, u32[]{:S(2)}) collective-permute-start(bf16[880,128]{1,0:T(8,128)(2,1)S(1)} %collective-permute-done.11), channel_id=1, source_target_pairs={{0,32},{32,64},{64,96},{96,128},{128,160},{160,192},{192,224},{224... | collective-permute-start | bytes 675848 | tf_op jit(solution)/shard_map/ppermute | solution.py:100
  65.6 7.9 %collective-permute-start.6 = (bf16[880,128]{1,0:T(8,128)(2,1)S(1)}, bf16[880,128]{1,0:T(8,128)(2,1)S(1)}, u32[]{:S(2)}, u32[]{:S(2)}) collective-permute-start(bf16[880,128]{1,0:T(8,128)(2,1)S(1)} %collective-permute-done.5), channel_id=1, source_target_pairs={{0,480},{32,0},{64,32},{96,64},{128,96},{160,128},{192,160},{224,1... | collective-permute-start | bytes 675848 | tf_op jit(solution)/shard_map/ppermute | solution.py:103
  70.6 7.9 %collective-permute-start.13 = (bf16[880,128]{1,0:T(8,128)(2,1)S(1)}, bf16[880,128]{1,0:T(8,128)(2,1)S(1)}, u32[]{:S(2)}, u32[]{:S(2)}) collective-permute-start(bf16[880,128]{1,0:T(8,128)(2,1)S(1)} %collective-permute-done.12), channel_id=1, source_target_pairs={{0,32},{32,64},{64,96},{96,128},{128,160},{160,192},{192,224},{224... | collective-permute-start | bytes 675848 | tf_op jit(solution)/shard_map/ppermute | solution.py:100
  73.5 7.9 %collective-permute-start.7 = (bf16[880,128]{1,0:T(8,128)(2,1)S(1)}, bf16[880,128]{1,0:T(8,128)(2,1)S(1)}, u32[]{:S(2)}, u32[]{:S(2)}) collective-permute-start(bf16[880,128]{1,0:T(8,128)(2,1)S(1)} %collective-permute-done.6), channel_id=1, source_target_pairs={{0,480},{32,0},{64,32},{96,64},{128,96},{160,128},{192,160},{224,1... | collective-permute-start | bytes 675848 | tf_op jit(solution)/shard_map/ppermute | solution.py:103
  78.6 8.1 %collective-permute-start.14 = (bf16[880,128]{1,0:T(8,128)(2,1)S(1)}, bf16[880,128]{1,0:T(8,128)(2,1)S(1)}, u32[]{:S(2)}, u32[]{:S(2)}) collective-permute-start(bf16[880,128]{1,0:T(8,128)(2,1)S(1)} %collective-permute-done.13), channel_id=1, source_target_pairs={{0,32},{32,64},{64,96},{96,128},{128,160},{160,192},{192,224},{224... | collective-permute-start | bytes 675848 | tf_op jit(solution)/shard_map/ppermute | solution.py:100
  81.4 9.0 %collective-permute-start.8 = (bf16[880,128]{1,0:T(8,128)(2,1)S(1)}, bf16[880,128]{1,0:T(8,128)(2,1)S(1)}, u32[]{:S(2)}, u32[]{:S(2)}) collective-permute-start(bf16[880,128]{1,0:T(8,128)(2,1)S(1)} %collective-permute-done.7), channel_id=1, source_target_pairs={{0,480},{32,0},{64,32},{96,64},{128,96},{160,128},{192,160},{224,1... | collective-permute-start | bytes 675848 | tf_op jit(solution)/shard_map/ppermute | solution.py:103
  86.7 9.3 %collective-permute-start.15 = (bf16[880,128]{1,0:T(8,128)(2,1)S(1)}, bf16[880,128]{1,0:T(8,128)(2,1)S(1)}, u32[]{:S(2)}, u32[]{:S(2)}) collective-permute-start(bf16[880,128]{1,0:T(8,128)(2,1)S(1)} %collective-permute-done.14), channel_id=1, source_target_pairs={{0,32},{32,64},{64,96},{96,128},{128,160},{160,192},{192,224},{224... | collective-permute-start | bytes 675848 | tf_op jit(solution)/shard_map/ppermute | solution.py:100
  90.4 18.0 %collective-permute-start.9 = (bf16[880,128]{1,0:T(8,128)(2,1)S(1)}, bf16[880,128]{1,0:T(8,128)(2,1)S(1)}, u32[]{:S(2)}, u32[]{:S(2)}) collective-permute-start(bf16[880,128]{1,0:T(8,128)(2,1)S(1)} %collective-permute-done.8), channel_id=1, source_target_pairs={{0,480},{32,0},{64,32},{96,64},{128,96},{160,128},{192,160},{224,1... | collective-permute-start | bytes 675848 | tf_op jit(solution)/shard_map/ppermute | solution.py:103
  95.9 10.5 %collective-permute-start.16 = (bf16[880,128]{1,0:T(8,128)(2,1)S(1)}, bf16[880,128]{1,0:T(8,128)(2,1)S(1)}, u32[]{:S(2)}, u32[]{:S(2)}) collective-permute-start(bf16[880,128]{1,0:T(8,128)(2,1)S(1)} %collective-permute-done.15), channel_id=1, source_target_pairs={{0,32},{32,64},{64,96},{96,128},{128,160},{160,192},{192,224},{224... | collective-permute-start | bytes 675848 | tf_op jit(solution)/shard_map/ppermute | solution.py:100
  106.5 9.7 %collective-permute-start.17 = (bf16[880,128]{1,0:T(8,128)(2,1)S(1)}, bf16[880,128]{1,0:T(8,128)(2,1)S(1)}, u32[]{:S(2)}, u32[]{:S(2)}) collective-permute-start(bf16[880,128]{1,0:T(8,128)(2,1)S(1)} %collective-permute-done.16), channel_id=1, source_target_pairs={{0,32},{32,64},{64,96},{96,128},{128,160},{160,192},{192,224},{224... | collective-permute-start | bytes 675848 | tf_op jit(solution)/shard_map/ppermute | solution.py:100
  128.5 5.8 %slice-start = ((bf16[64,28160]{1,0:T(8,128)(2,1)}), bf16[64,2560]{1,0:T(8,128)(2,1)S(1)}, s32[]{:S(2)}) async-start(bf16[64,28160]{1,0:T(8,128)(2,1)} %reshape.346), calls=%async_computation.3 | async-start | bytes 655360 | tf_op jit(solution)/shard_map/slice | solution.py:151
  134.3 3.0 %copy-start.5 = (bf16[2560,320]{1,0:T(8,128)(2,1)S(1)}, bf16[2560,320]{1,0:T(8,128)(2,1)}, u32[]{:S(2)}) copy-start(bf16[2560,320]{1,0:T(8,128)(2,1)} %reshape.347) | copy-start | bytes 4915204
  137.3 3.1 %copy-start.2 = (bf16[512,2560]{0,1:T(8,128)(2,1)S(1)}, bf16[512,2560]{0,1:T(8,128)(2,1)}, u32[]{:S(2)}) copy-start(bf16[512,2560]{0,1:T(8,128)(2,1)} %all-gather.3.cloned.1.call-done) | copy-start | bytes 7864324
  142.3 27.0 %all-to-all-start = ((f32[8,64,384]{2,1,0:T(8,128)}), f32[8,64,384]{2,1,0:T(8,128)S(1)}, u32[]{:S(2)}, u32[]{:S(2)}) async-start(f32[8,64,384]{2,1,0:T(8,128)} %bitcast.26), calls=%async_computation | async-start | bytes 1572864 | tf_op jit(solution)/shard_map/all_to_all | solution.py:165
  157.2 51.2 %all-gather.5.cloned.1.call-start = ((), (), s32[]{:S(2)}) async-start(), calls=%async_computation.2 | async-start | bytes 2949120 | tf_op jit(solution)/shard_map/all_gather | solution.py:194
  174.9 1.5 copy-start.1
  202.6 4.2 %copy-start.4 = (bf16[4,2,128,256]{3,2,1,0:T(8,128)(2,1)S(1)}, bf16[4,2,128,256]{3,2,1,0:T(8,128)(2,1)}, u32[]{:S(2)}) copy-start(bf16[4,2,128,256]{3,2,1,0:T(8,128)(2,1)} %get-tuple-element.3) | copy-start | bytes 1572868
  203.8 4.5 %copy-start.7 = (bf16[256,320]{0,1:T(8,128)(2,1)S(1)}, bf16[256,320]{0,1:T(8,128)(2,1)}, u32[]{:S(2)}) copy-start(bf16[256,320]{0,1:T(8,128)(2,1)} %slice.154) | copy-start | bytes 491524
  204.6 5.2 %copy-start.8 = (bf16[256,320]{0,1:T(8,128)(2,1)S(1)}, bf16[256,320]{0,1:T(8,128)(2,1)}, u32[]{:S(2)}) copy-start(bf16[256,320]{0,1:T(8,128)(2,1)} %slice.160) | copy-start | bytes 491524
  205.0 6.0 %copy-start.9 = (bf16[256,320]{0,1:T(8,128)(2,1)S(1)}, bf16[256,320]{0,1:T(8,128)(2,1)}, u32[]{:S(2)}) copy-start(bf16[256,320]{0,1:T(8,128)(2,1)} %slice.166) | copy-start | bytes 491524
  205.6 6.7 %copy-start.10 = (bf16[256,320]{0,1:T(8,128)(2,1)S(1)}, bf16[256,320]{0,1:T(8,128)(2,1)}, u32[]{:S(2)}) copy-start(bf16[256,320]{0,1:T(8,128)(2,1)} %slice.169) | copy-start | bytes 491524
  206.8 6.8 %copy-start.11 = (bf16[256,320]{0,1:T(8,128)(2,1)S(1)}, bf16[256,320]{0,1:T(8,128)(2,1)}, u32[]{:S(2)}) copy-start(bf16[256,320]{0,1:T(8,128)(2,1)} %slice.172) | copy-start | bytes 491524
  206.9 7.0 %copy-start.12 = (bf16[256,320]{0,1:T(8,128)(2,1)S(1)}, bf16[256,320]{0,1:T(8,128)(2,1)}, u32[]{:S(2)}) copy-start(bf16[256,320]{0,1:T(8,128)(2,1)} %slice.175) | copy-start | bytes 491524
  208.4 6.0 %copy-start.13 = (bf16[256,320]{0,1:T(8,128)(2,1)S(1)}, bf16[256,320]{0,1:T(8,128)(2,1)}, u32[]{:S(2)}) copy-start(bf16[256,320]{0,1:T(8,128)(2,1)} %slice.181) | copy-start | bytes 491524
  208.4 5.2 %copy-start.3 = (bf16[512,2560]{1,0:T(8,128)(2,1)S(1)}, bf16[512,2560]{1,0:T(8,128)(2,1)}, u32[]{:S(2)}) copy-start(bf16[512,2560]{1,0:T(8,128)(2,1)} %all-gather.5.cloned.1.call-done) | copy-start | bytes 7864324
  209.8 4.9 %copy-start.6 = (bf16[256,320]{0,1:T(8,128)(2,1)S(1)}, bf16[256,320]{0,1:T(8,128)(2,1)}, u32[]{:S(2)}) copy-start(bf16[256,320]{0,1:T(8,128)(2,1)} %slice.163) | copy-start | bytes 491524
Sparse Core Ops, SparseCore 0:
  19.4 39.0 all-gather.2
  176.2 26.4 all-gather.4
where the time goes:
time: 225 us; the launch traced here: 223 us
  starting transfers between devices  80.2 us (36%)
  local copies, waits for them, and re-layouts  70.2 us (31%)
  waiting for transfers between devices  31.9 us (14%)
  between operations  17.3 us (8%)
  matrix products  14.7 us (7%)
  other arithmetic  8.67 us (4%)
    ppermute x8, starting transfers between devices, ring_gather(): lax.ppermute(behind, axis, [(i, (i - 1) % size) for i in range(size)])  45.9 us
    slice x21, local copies, waits for them, and re-layouts, shards(): wo_cols[k * HD:(k + 1) * HD]  20.3 us
    ppermute x10, waiting for transfers between devices, ring_gather(): lax.ppermute(ahead, axis, [(i, (i + 1) % size) for i in range(size)])  19.7 us
    ppermute x10, starting transfers between devices, ring_gather(): lax.ppermute(ahead, axis, [(i, (i + 1) % size) for i in range(size)])  19.3 us
    all_to_all x1, starting transfers between devices, shards(): mine = lax.all_to_all(both, 'head', 0, 1, tiled=True)  14.9 us
    dynamic_update_slice x20, local copies, waits for them, and re-layouts, ring_gather(): lax.dynamic_update_slice_in_dim(placed, by_offset[offset][None], (index +...  11.5 us
    all_to_all x1, waiting for transfers between devices, shards(): mine = lax.all_to_all(both, 'head', 0, 1, tiled=True)  10 us
    dot_general x10, matrix products, shards(): jnp.dot(mixed[:, k * HD:(k + 1) * HD], wo_cols[k * HD:(k + 1) * HD], pref...  7.63 us
  transfers between devices with their start and end apart: 21, of which 11 were waited for; matrix products, arithmetic and copies ran while one was open for 30% of the time, Pallas kernels for 0%

commit v1 on v0

--- a/solution.py
+++ b/solution.py
@@ -88,11 +88,8 @@
     )
 
 
-def ring_gather(piece, axis):
+def ring_pieces(piece, axis):
     size = lax.axis_size(axis)
-    if size == 1:
-        return piece[None]
-    index = lax.axis_index(axis)
     by_offset = {0: piece}
     ahead = piece
     behind = piece
@@ -102,19 +99,25 @@
         if step <= (size - 1) // 2:
             behind = lax.ppermute(behind, axis, [(i, (i - 1) % size) for i in range(size)])
             by_offset[step] = behind
-    placed = jnp.zeros((size,) + piece.shape, piece.dtype)
-    for offset in range(size):
+    return by_offset
+
+
+def grid_gather(piece):
+    z_size = lax.axis_size("tz")
+    x_size = lax.axis_size("tx")
+    z_index = lax.axis_index("tz")
+    x_index = lax.axis_index("tx")
+    column = jnp.zeros((z_size,) + piece.shape, piece.dtype)
+    for offset, got in ring_pieces(piece, "tz").items():
+        column = lax.dynamic_update_slice_in_dim(
+            column, got[None], (z_index + offset) % z_size, axis=0
+        )
+    placed = jnp.zeros((z_size, x_size) + piece.shape, piece.dtype)
+    for offset, got in ring_pieces(column, "tx").items():
         placed = lax.dynamic_update_slice_in_dim(
-            placed, by_offset[offset][None], (index + offset) % size, axis=0
+            placed, got[:, None], (x_index + offset) % x_size, axis=1
         )
-    return placed
-
-
-def grid_gather(piece):
-    lanes = 128
-    inner = ring_gather(piece.reshape(-1, lanes), "tx")
-    outer = ring_gather(inner.reshape(-1, lanes), "tz")
-    return outer.reshape(-1, piece.shape[0])
+    return placed.reshape((z_size * x_size,) + piece.shape)
 
 
 def shards(
@@ -140,17 +143,19 @@
     out_cols = output_weight.shape[1]
     wq_piece = lax.dynamic_slice_in_dim(query_weight, head_index * q_cols, q_cols, axis=1)
     wkv_piece = lax.dynamic_slice_in_dim(keyvalue_weight, head_index * kv_cols, kv_cols, axis=1)
-    flat = jnp.concatenate(
-        [wq_piece.reshape(-1), wkv_piece.reshape(-1), output_weight.reshape(-1)]
-    )
-    stacked = grid_gather(flat)
+    proj_piece = jnp.concatenate([wq_piece, wkv_piece], axis=1)
+    width = proj_piece.shape[1]
+    wo_flat = output_weight.reshape(-1)
+    wo_rows = -(-wo_flat.shape[0] // width)
+    wo_rows = -(-(part_rows + wo_rows) // 8) * 8 - part_rows
+    wo_block = jnp.pad(wo_flat, (0, wo_rows * width - wo_flat.shape[0])).reshape(wo_rows, width)
+    piece = jnp.concatenate([proj_piece, wo_block], axis=0)
+    stacked = grid_gather(piece)
     tok_count = stacked.shape[0]
-    n_q = part_rows * q_cols
-    n_kv = part_rows * kv_cols
-    wq_cols = stacked[:, :n_q].reshape(tok_count * part_rows, q_cols)
-    wkv_cols = stacked[:, n_q : n_q + n_kv].reshape(tok_count * part_rows, kv_cols)
+    proj_w = stacked[:, :part_rows].reshape(tok_count * part_rows, width)
     wo_cols = (
-        stacked[:, n_q + n_kv :]
+        stacked[:, part_rows:]
+        .reshape(tok_count, -1)[:, : wo_flat.shape[0]]
         .reshape(tok_count, HQ * HD, out_cols)
         .transpose(1, 0, 2)
         .reshape(HQ * HD, tok_count * out_cols)
@@ -159,9 +164,7 @@
     wide = gathered.astype(jnp.float32)
     mean_square = jnp.mean(wide * wide, axis=1, keepdims=True)
     normed = (wide * lax.rsqrt(mean_square + 1e-06)).astype(jnp.bfloat16)
-    q_part = jnp.dot(normed, wq_cols, preferred_element_type=jnp.float32)
-    kv_part = jnp.dot(normed, wkv_cols, preferred_element_type=jnp.float32)
-    both = jnp.concatenate([q_part, kv_part], axis=1)
+    both = jnp.dot(normed, proj_w, preferred_element_type=jnp.float32)
     mine = lax.all_to_all(both, "head", 0, 1, tiled=True)
     mine = mine.reshape(DRAFT, head_count, q_cols + kv_cols)
     q_pre = mine[:, :, :q_cols].reshape(DRAFT, HQ, HD)

time: 225 us -> 210 us (0.933)
  local copies, waits for them, and re-layouts: 70.2 us -> 52.6 us
  waiting for transfers between devices: 31.9 us -> 43.8 us
  starting transfers between devices: 80.2 us -> 75.9 us
  matrix products: 14.7 us -> 12.4 us
    ppermute x18, waiting for transfers between devices: 21.8 us -> 34.5 us  [the longest x10 34.5 us: ring_pieces(): lax.ppermute(ahead, axis, [(i, (i + 1) % size) for i in range(size)])]
    reshape x8 -> x3, local copies, waits for them, and re-layouts: 17.8 us -> 8.15 us  [the longest x1 7.15 us: shards(): wo_cols = stacked[:, part_rows:].reshape(tok_count, -1)[:, :wo_flat.shape...]
    dynamic_update_slice x20 -> x19, local copies, waits for them, and re-layouts: 11.5 us -> 2.29 us  [the longest x4 1.99 us: grid_gather(): lax.dynamic_update_slice_in_dim(placed, got[:, None], (x_index + offset)...]
    slice x21, local copies, waits for them, and re-layouts: 20.3 us -> 16.6 us  [shards(): wo_cols[k * HD:(k + 1) * HD]]
    slice x4 -> x3, local copies, waits for them, and re-layouts: 6.3 us -> 9.41 us  [the longest x2 7.07 us: shards(): stacked[:, part_rows:].reshape(tok_count, -1)[:, :wo_flat.shape[0]]]
    all_gather x0 -> x1, local copies, waits for them, and re-layouts: none -> 2.98 us  [shards(): gathered = lax.all_gather(tokens, 'head', axis=1, tiled=True)]
    unnamed x33 -> x31, local copies, waits for them, and re-layouts: 3.1 us -> 4.63 us
  transfers between devices with their start and end apart: 21 -> 21, of which waited for: 11 -> 4; matrix products, arithmetic and copies ran while one was open for 30% -> 21% of each run, Pallas kernels for 0% -> 0%
where the time goes in v1:
time: 210 us; the launch traced here: 209 us
  starting transfers between devices  75.9 us (36%)
  local copies, waits for them, and re-layouts  52.6 us (25%)
  waiting for transfers between devices  43.8 us (21%)
  between operations  17.4 us (8%)
  matrix products  12.4 us (6%)
  other arithmetic  6.56 us (3%)
    ppermute x8, starting transfers between devices, ring_pieces(): lax.ppermute(behind, axis, [(i, (i - 1) % size) for i in range(size)])  40.3 us
    ppermute x10, waiting for transfers between devices, ring_pieces(): lax.ppermute(ahead, axis, [(i, (i + 1) % size) for i in range(size)])  34.5 us
    ppermute x10, starting transfers between devices, ring_pieces(): lax.ppermute(ahead, axis, [(i, (i + 1) % size) for i in range(size)])  22.8 us
    slice x21, local copies, waits for them, and re-layouts, shards(): wo_cols[k * HD:(k + 1) * HD]  16.6 us
    all_to_all x1, starting transfers between devices, shards(): mine = lax.all_to_all(both, 'head', 0, 1, tiled=True)  12.7 us
    all_to_all x1, waiting for transfers between devices, shards(): mine = lax.all_to_all(both, 'head', 0, 1, tiled=True)  9.21 us
    reshape x1, local copies, waits for them, and re-layouts, shards(): wo_cols = stacked[:, part_rows:].reshape(tok_count, -1)[:, :wo_flat.shape...  7.15 us
    slice x2, local copies, waits for them, and re-layouts, shards(): stacked[:, part_rows:].reshape(tok_count, -1)[:, :wo_flat.shape[0]]  7.07 us
  transfers between devices with their start and end apart: 21, of which 4 were waited for; matrix products, arithmetic and copies ran while one was open for 21% of the time, Pallas kernels for 0%

profile of v1, /device:TPU:1, one launch (start us, length us, event | category | flops | bytes accessed | tf_op | source)
XLA Modules:
  0.0 208.6 jit_solution(8573016834578123282)
XLA Ops:
  7.3 1.2 copy.63
  8.5 1.0 reshape.333
  9.5 0.8 constant_dynamic-slice_fusion.1
  10.3 0.9 constant_dynamic-slice_fusion.2
  11.3 4.4 %collective-permute-start = (bf16[80,384]{1,0:T(8,128)(2,1)S(1)}, bf16[80,384]{1,0:T(8,128)(2,1)S(1)}, u32[]{:S(2)}, u32[]{:S(2)}) collective-permute-start(bf16[80,384]{1,0:T(8,128)(2,1)S(1)} %get-tuple-element.6), channel_id=1, source_target_pairs={{0,32},{32,64},{64,96},{96,128},{128,160},{160,192},{192,224},{224... | collective-permute-start | bytes 184328 | tf_op jit(solution)/shard_map/ppermute | solution.py:97
  15.7 9.5 %collective-permute-start.1 = (bf16[80,384]{1,0:T(8,128)(2,1)S(1)}, bf16[80,384]{1,0:T(8,128)(2,1)S(1)}, u32[]{:S(2)}, u32[]{:S(2)}) collective-permute-start(bf16[80,384]{1,0:T(8,128)(2,1)S(1)} %get-tuple-element.6), channel_id=1, source_target_pairs={{0,480},{32,0},{64,32},{96,64},{128,96},{160,128},{192,160},{224,1... | collective-permute-start | bytes 184328 | tf_op jit(solution)/shard_map/ppermute | solution.py:100
  25.4 0.6 dynamic_slice.29
  27.3 0.6 dynamic_slice.25
  27.9 0.7 fusion.64
  30.8 0.6 iota_subtract_fusion
  31.4 1.9 collective-permute-start.2
  33.4 4.6 %collective-permute-start.3 = (bf16[80,384]{1,0:T(8,128)(2,1)S(1)}, bf16[80,384]{1,0:T(8,128)(2,1)S(1)}, u32[]{:S(2)}, u32[]{:S(2)}) collective-permute-start(bf16[80,384]{1,0:T(8,128)(2,1)S(1)} %collective-permute-done.1), channel_id=1, source_target_pairs={{0,480},{32,0},{64,32},{96,64},{128,96},{160,128},{192,160},{224,1... | collective-permute-start | bytes 184328 | tf_op jit(solution)/shard_map/ppermute | solution.py:100
  38.0 1.9 collective-permute-start.4
  40.0 4.6 %collective-permute-start.5 = (bf16[80,384]{1,0:T(8,128)(2,1)S(1)}, bf16[80,384]{1,0:T(8,128)(2,1)S(1)}, u32[]{:S(2)}, u32[]{:S(2)}) collective-permute-start(bf16[80,384]{1,0:T(8,128)(2,1)S(1)} %collective-permute-done.3), channel_id=1, source_target_pairs={{0,480},{32,0},{64,32},{96,64},{128,96},{160,128},{192,160},{224,1... | collective-permute-start | bytes 184328 | tf_op jit(solution)/shard_map/ppermute | solution.py:100
  44.6 1.9 collective-permute-start.6
  46.5 4.6 %collective-permute-start.7 = (bf16[80,384]{1,0:T(8,128)(2,1)S(1)}, bf16[80,384]{1,0:T(8,128)(2,1)S(1)}, u32[]{:S(2)}, u32[]{:S(2)}) collective-permute-start(bf16[80,384]{1,0:T(8,128)(2,1)S(1)} %collective-permute-done.5), channel_id=1, source_target_pairs={{0,480},{32,0},{64,32},{96,64},{128,96},{160,128},{192,160},{224,1... | collective-permute-start | bytes 184328 | tf_op jit(solution)/shard_map/ppermute | solution.py:100
  51.2 1.9 collective-permute-start.8
  53.1 4.6 %collective-permute-start.9 = (bf16[80,384]{1,0:T(8,128)(2,1)S(1)}, bf16[80,384]{1,0:T(8,128)(2,1)S(1)}, u32[]{:S(2)}, u32[]{:S(2)}) collective-permute-start(bf16[80,384]{1,0:T(8,128)(2,1)S(1)} %collective-permute-done.7), channel_id=1, source_target_pairs={{0,480},{32,0},{64,32},{96,64},{128,96},{160,128},{192,160},{224,1... | collective-permute-start | bytes 184328 | tf_op jit(solution)/shard_map/ppermute | solution.py:100
  57.8 1.9 collective-permute-start.10
  59.7 4.6 %collective-permute-start.11 = (bf16[80,384]{1,0:T(8,128)(2,1)S(1)}, bf16[80,384]{1,0:T(8,128)(2,1)S(1)}, u32[]{:S(2)}, u32[]{:S(2)}) collective-permute-start(bf16[80,384]{1,0:T(8,128)(2,1)S(1)} %collective-permute-done.9), channel_id=1, source_target_pairs={{0,480},{32,0},{64,32},{96,64},{128,96},{160,128},{192,160},{224,1... | collective-permute-start | bytes 184328 | tf_op jit(solution)/shard_map/ppermute | solution.py:100
  64.3 1.9 collective-permute-start.12
  66.3 4.6 %collective-permute-start.13 = (bf16[80,384]{1,0:T(8,128)(2,1)S(1)}, bf16[80,384]{1,0:T(8,128)(2,1)S(1)}, u32[]{:S(2)}, u32[]{:S(2)}) collective-permute-start(bf16[80,384]{1,0:T(8,128)(2,1)S(1)} %collective-permute-done.11), channel_id=1, source_target_pairs={{0,480},{32,0},{64,32},{96,64},{128,96},{160,128},{192,160},{224,1... | collective-permute-start | bytes 184328 | tf_op jit(solution)/shard_map/ppermute | solution.py:100
  70.9 1.9 collective-permute-start.14
  72.9 4.2 %collective-permute-done.14 = bf16[80,384]{1,0:T(8,128)(2,1)S(1)} collective-permute-done((bf16[80,384]{1,0:T(8,128)(2,1)S(1)}, bf16[80,384]{1,0:T(8,128)(2,1)S(1)}, u32[]{:S(2)}, u32[]{:S(2)}) %collective-permute-start.14) | collective-permute-done | bytes 61472 | tf_op jit(solution)/shard_map/ppermute | solution.py:97
  77.1 3.1 %collective-permute-start.15 = (bf16[16,80,384]{2,1,0:T(8,128)(2,1)S(1)}, bf16[16,80,384]{2,1,0:T(8,128)(2,1)S(1)}, u32[]{:S(2)}, u32[]{:S(2)}) collective-permute-start(bf16[16,80,384]{2,1,0:T(8,128)(2,1)S(1)} %bitcast_dynamic-update-slice_fusion.4), channel_id=1, source_target_pairs={{0,8},{8,16},{16,24},{24,0},{1,9},{9,17},{17,25},{25,1},{2,10},{10... | collective-permute-start | bytes 2949128 | tf_op jit(solution)/shard_map/ppermute | solution.py:97
  80.4 3.4 %collective-permute-start.16 = (bf16[16,80,384]{2,1,0:T(8,128)(2,1)S(1)}, bf16[16,80,384]{2,1,0:T(8,128)(2,1)S(1)}, u32[]{:S(2)}, u32[]{:S(2)}) collective-permute-start(bf16[16,80,384]{2,1,0:T(8,128)(2,1)S(1)} %bitcast_dynamic-update-slice_fusion.4), channel_id=1, source_target_pairs={{0,24},{8,0},{16,8},{24,16},{1,25},{9,1},{17,9},{25,17},{2,26},{10... | collective-permute-start | bytes 2949128 | tf_op jit(solution)/shard_map/ppermute | solution.py:100
  83.8 13.3 %collective-permute-done.15 = bf16[16,80,384]{2,1,0:T(8,128)(2,1)S(1)} collective-permute-done((bf16[16,80,384]{2,1,0:T(8,128)(2,1)S(1)}, bf16[16,80,384]{2,1,0:T(8,128)(2,1)S(1)}, u32[]{:S(2)}, u32[]{:S(2)}) %collective-permute-start.15) | collective-permute-done | bytes 983072 | tf_op jit(solution)/shard_map/ppermute | solution.py:97
  97.0 1.9 collective-permute-start.17
  99.1 0.5 broadcast_in_dim.131
  100.3 17.1 %collective-permute-done.17 = bf16[16,80,384]{2,1,0:T(8,128)(2,1)} collective-permute-done((bf16[16,80,384]{2,1,0:T(8,128)(2,1)S(1)}, bf16[16,80,384]{2,1,0:T(8,128)(2,1)}, u32[]{:S(2)}, u32[]{:S(2)}) %collective-permute-start.17) | collective-permute-done | bytes 983072 | tf_op jit(solution)/shard_map/ppermute | solution.py:97
  117.3 1.4 bitcast_dynamic-update-slice_fusion
  118.7 2.3 %fusion.71 = (bf16[64,40,384]{2,1,0:T(8,128)(2,1)}, bf16[64,40,384]{2,1,0:T(8,128)(2,1)}) fusion(bf16[64,80,384]{2,1,0:T(8,128)(2,1)S(1)} %bitcast.159), kind=kLoop, calls=%fused_computation.156 | loop fusion | bytes 7864320 | tf_op jit(solution)/shard_map/slice | solution.py:155
  121.1 3.0 %copy.62 = bf16[512,2560]{1,0:T(8,128)(2,1)S(1)} copy(bf16[512,2560]{0,1:T(8,128)(2,1)} %all-gather.3.cloned.1.call-done) | data formatting | bytes 5242880 | tf_op jit(solution)/shard_map/all_gather | solution.py:163
  124.1 0.6 fusion
  124.7 0.5 fusion.1
  125.2 1.0 copy-done.6
  126.2 2.4 %fusion.79 = f32[8,64,384]{2,1,0:T(8,128)} fusion(bf16[8,64,2560]{2,1,0:T(8,128)(2,1)S(1)} %bitcast.163, bf16[2560,384,1]{1,0,2:T(8,128)(2,1)S(1)} %bitcast.164), kind=kOutput, calls=%fused_computation.162 | convolution fusion | flops 1006632960 | bytes 5373952 | tf_op jit(solution)/shard_map/dot_general | solution.py:167
  128.6 12.7 %all-to-all-start = ((f32[8,64,384]{2,1,0:T(8,128)}), f32[8,64,384]{2,1,0:T(8,128)S(1)}, u32[]{:S(2)}, u32[]{:S(2)}) async-start(f32[8,64,384]{2,1,0:T(8,128)} %fusion.79), calls=%async_computation | async-start | bytes 1572864 | tf_op jit(solution)/shard_map/all_to_all | solution.py:168
  141.3 0.6 iota_compare_fusion.6
  142.1 1.4 gather_fusion
  143.5 0.7 add_add_fusion
  144.3 9.2 %all-to-all-done = f32[8,64,384]{2,1,0:T(8,128)S(1)} async-done(((f32[8,64,384]{2,1,0:T(8,128)}), f32[8,64,384]{2,1,0:T(8,128)S(1)}, u32[]{:S(2)}, u32[]{:S(2)}) %all-to-all-start) | async-done | bytes 786464 | tf_op jit(solution)/shard_map/all_to_all | solution.py:168
  154.4 0.8 slice.192
  156.2 1.2 copy.88
  157.9 1.0 fusion.28
  161.3 0.7 copy.89
  162.5 3.8 %copy.72 = bf16[64,40,384]{0,2,1:T(8,128)(2,1)} copy(bf16[64,40,384]{2,1,0:T(8,128)(2,1)S(1)} %copy-done.2) | data formatting | bytes 3932160 | tf_op jit(solution)/shard_map/slice | solution.py:157
  166.3 3.3 %slice.200 = bf16[64,12800]{0,1:T(8,128)(2,1)} slice(bf16[64,15360]{0,1:T(8,128)(2,1)} %bitcast.160), slice={[0:64], [0:12800]} | slice | bytes 3276800 | tf_op jit(solution)/shard_map/slice | solution.py:157
  169.6 7.1 %reshape.343 = bf16[64,2560,5]{0,2,1:T(8,128)(2,1)} reshape(bf16[64,12800]{0,1:T(8,128)(2,1)} %slice.200) | data formatting | bytes 3276800 | tf_op jit(solution)/shard_map/reshape | solution.py:159
  176.7 4.6 %fusion.70 = (bf16[256,64,5]{1,2,0:T(8,128)(2,1)S(1)}, bf16[256,64,5]{1,2,0:T(8,128)(2,1)}, bf16[256,64,5]{1,2,0:T(8,128)(2,1)}, bf16[256,64,5]{1,2,0:T(8,128)(2...) fusion(bf16[2560,64,5]{1,2,0:T(8,128)(2,1)} %bitcast.158), kind=kLoop, calls=%fused_computation.155 | loop fusion | bytes 3276800 | tf_op jit(solution)/shard_map/slice | solution.py:207
  181.3 1.5 copy.82
  182.8 0.7 slice.181
  183.6 1.5 copy.81
  185.1 0.8 slice.178
  185.8 1.5 copy.80
  187.3 0.7 slice.175
  188.0 1.5 copy.79
  189.5 0.7 slice.172
  193.5 0.6 gather_fusion.1
  194.1 0.9 broadcast_select_fusion
  195.0 1.4 fusion.16
  196.4 1.2 fusion.17
  197.6 1.2 fusion.18
  200.6 1.2 fusion.12
  (131 shorter events, 13.0 us)
Async XLA Ops:
  7.2 134.9 %copy-start = (bf16[4,2,128,256]{3,2,1,0:T(8,128)(2,1)S(1)}, bf16[4,2,128,256]{3,2,1,0:T(8,128)(2,1)}, u32[]{:S(2)}) copy-start(bf16[4,2,128,256]{3,2,1,0:T(8,128)(2,1)} %param.15) | copy-start | bytes 1572868
  7.2 18.2 %copy-start.12 = (s32[8]{0:T(128)S(1)}, s32[8]{0:T(128)}, u32[]{:S(2)}) copy-start(s32[8]{0:T(128)} %param.19) | copy-start | bytes 100
  7.2 20.1 %copy-start.13 = (s32[8]{0:T(128)S(1)}, s32[8]{0:T(128)}, u32[]{:S(2)}) copy-start(s32[8]{0:T(128)} %param.18) | copy-start | bytes 100
  7.2 23.4 %copy-start.11 = (s32[8,4]{0,1:T(4,128)S(1)}, s32[8,4]{0,1:T(4,128)}, u32[]{:S(2)}) copy-start(s32[8,4]{0,1:T(4,128)} %param.16) | copy-start | bytes 388
  7.2 113.9 %all-gather.3.cloned.1.call-start = ((), (), s32[]{:S(2)}) async-start(), calls=%async_computation.1 | async-start | bytes 2949120 | tf_op jit(solution)/shard_map/all_gather | solution.py:163
  11.3 20.1 %collective-permute-start = (bf16[80,384]{1,0:T(8,128)(2,1)S(1)}, bf16[80,384]{1,0:T(8,128)(2,1)S(1)}, u32[]{:S(2)}, u32[]{:S(2)}) collective-permute-start(bf16[80,384]{1,0:T(8,128)(2,1)S(1)} %get-tuple-element.6), channel_id=1, source_target_pairs={{0,32},{32,64},{64,96},{96,128},{128,160},{160,192},{192,224},{224... | collective-permute-start | bytes 184328 | tf_op jit(solution)/shard_map/ppermute | solution.py:97
  15.7 17.7 %collective-permute-start.1 = (bf16[80,384]{1,0:T(8,128)(2,1)S(1)}, bf16[80,384]{1,0:T(8,128)(2,1)S(1)}, u32[]{:S(2)}, u32[]{:S(2)}) collective-permute-start(bf16[80,384]{1,0:T(8,128)(2,1)S(1)} %get-tuple-element.6), channel_id=1, source_target_pairs={{0,480},{32,0},{64,32},{96,64},{128,96},{160,128},{192,160},{224,1... | collective-permute-start | bytes 184328 | tf_op jit(solution)/shard_map/ppermute | solution.py:100
  31.4 6.6 %collective-permute-start.2 = (bf16[80,384]{1,0:T(8,128)(2,1)S(1)}, bf16[80,384]{1,0:T(8,128)(2,1)S(1)}, u32[]{:S(2)}, u32[]{:S(2)}) collective-permute-start(bf16[80,384]{1,0:T(8,128)(2,1)S(1)} %collective-permute-done), channel_id=1, source_target_pairs={{0,32},{32,64},{64,96},{96,128},{128,160},{160,192},{192,224},{224... | collective-permute-start | bytes 184328 | tf_op jit(solution)/shard_map/ppermute | solution.py:97
  33.4 6.6 %collective-permute-start.3 = (bf16[80,384]{1,0:T(8,128)(2,1)S(1)}, bf16[80,384]{1,0:T(8,128)(2,1)S(1)}, u32[]{:S(2)}, u32[]{:S(2)}) collective-permute-start(bf16[80,384]{1,0:T(8,128)(2,1)S(1)} %collective-permute-done.1), channel_id=1, source_target_pairs={{0,480},{32,0},{64,32},{96,64},{128,96},{160,128},{192,160},{224,1... | collective-permute-start | bytes 184328 | tf_op jit(solution)/shard_map/ppermute | solution.py:100
  38.0 6.6 %collective-permute-start.4 = (bf16[80,384]{1,0:T(8,128)(2,1)S(1)}, bf16[80,384]{1,0:T(8,128)(2,1)S(1)}, u32[]{:S(2)}, u32[]{:S(2)}) collective-permute-start(bf16[80,384]{1,0:T(8,128)(2,1)S(1)} %collective-permute-done.2), channel_id=1, source_target_pairs={{0,32},{32,64},{64,96},{96,128},{128,160},{160,192},{192,224},{224... | collective-permute-start | bytes 184328 | tf_op jit(solution)/shard_map/ppermute | solution.py:97
  40.0 6.6 %collective-permute-start.5 = (bf16[80,384]{1,0:T(8,128)(2,1)S(1)}, bf16[80,384]{1,0:T(8,128)(2,1)S(1)}, u32[]{:S(2)}, u32[]{:S(2)}) collective-permute-start(bf16[80,384]{1,0:T(8,128)(2,1)S(1)} %collective-permute-done.3), channel_id=1, source_target_pairs={{0,480},{32,0},{64,32},{96,64},{128,96},{160,128},{192,160},{224,1... | collective-permute-start | bytes 184328 | tf_op jit(solution)/shard_map/ppermute | solution.py:100
  44.6 6.6 %collective-permute-start.6 = (bf16[80,384]{1,0:T(8,128)(2,1)S(1)}, bf16[80,384]{1,0:T(8,128)(2,1)S(1)}, u32[]{:S(2)}, u32[]{:S(2)}) collective-permute-start(bf16[80,384]{1,0:T(8,128)(2,1)S(1)} %collective-permute-done.4), channel_id=1, source_target_pairs={{0,32},{32,64},{64,96},{96,128},{128,160},{160,192},{192,224},{224... | collective-permute-start | bytes 184328 | tf_op jit(solution)/shard_map/ppermute | solution.py:97
  46.5 6.6 %collective-permute-start.7 = (bf16[80,384]{1,0:T(8,128)(2,1)S(1)}, bf16[80,384]{1,0:T(8,128)(2,1)S(1)}, u32[]{:S(2)}, u32[]{:S(2)}) collective-permute-start(bf16[80,384]{1,0:T(8,128)(2,1)S(1)} %collective-permute-done.5), channel_id=1, source_target_pairs={{0,480},{32,0},{64,32},{96,64},{128,96},{160,128},{192,160},{224,1... | collective-permute-start | bytes 184328 | tf_op jit(solution)/shard_map/ppermute | solution.py:100
  51.2 6.6 %collective-permute-start.8 = (bf16[80,384]{1,0:T(8,128)(2,1)S(1)}, bf16[80,384]{1,0:T(8,128)(2,1)S(1)}, u32[]{:S(2)}, u32[]{:S(2)}) collective-permute-start(bf16[80,384]{1,0:T(8,128)(2,1)S(1)} %collective-permute-done.6), channel_id=1, source_target_pairs={{0,32},{32,64},{64,96},{96,128},{128,160},{160,192},{192,224},{224... | collective-permute-start | bytes 184328 | tf_op jit(solution)/shard_map/ppermute | solution.py:97
  53.1 6.6 %collective-permute-start.9 = (bf16[80,384]{1,0:T(8,128)(2,1)S(1)}, bf16[80,384]{1,0:T(8,128)(2,1)S(1)}, u32[]{:S(2)}, u32[]{:S(2)}) collective-permute-start(bf16[80,384]{1,0:T(8,128)(2,1)S(1)} %collective-permute-done.7), channel_id=1, source_target_pairs={{0,480},{32,0},{64,32},{96,64},{128,96},{160,128},{192,160},{224,1... | collective-permute-start | bytes 184328 | tf_op jit(solution)/shard_map/ppermute | solution.py:100
  57.8 6.6 %collective-permute-start.10 = (bf16[80,384]{1,0:T(8,128)(2,1)S(1)}, bf16[80,384]{1,0:T(8,128)(2,1)S(1)}, u32[]{:S(2)}, u32[]{:S(2)}) collective-permute-start(bf16[80,384]{1,0:T(8,128)(2,1)S(1)} %collective-permute-done.8), channel_id=1, source_target_pairs={{0,32},{32,64},{64,96},{96,128},{128,160},{160,192},{192,224},{224... | collective-permute-start | bytes 184328 | tf_op jit(solution)/shard_map/ppermute | solution.py:97
  59.7 6.6 %collective-permute-start.11 = (bf16[80,384]{1,0:T(8,128)(2,1)S(1)}, bf16[80,384]{1,0:T(8,128)(2,1)S(1)}, u32[]{:S(2)}, u32[]{:S(2)}) collective-permute-start(bf16[80,384]{1,0:T(8,128)(2,1)S(1)} %collective-permute-done.9), channel_id=1, source_target_pairs={{0,480},{32,0},{64,32},{96,64},{128,96},{160,128},{192,160},{224,1... | collective-permute-start | bytes 184328 | tf_op jit(solution)/shard_map/ppermute | solution.py:100
  64.3 6.6 %collective-permute-start.12 = (bf16[80,384]{1,0:T(8,128)(2,1)S(1)}, bf16[80,384]{1,0:T(8,128)(2,1)S(1)}, u32[]{:S(2)}, u32[]{:S(2)}) collective-permute-start(bf16[80,384]{1,0:T(8,128)(2,1)S(1)} %collective-permute-done.10), channel_id=1, source_target_pairs={{0,32},{32,64},{64,96},{96,128},{128,160},{160,192},{192,224},{224... | collective-permute-start | bytes 184328 | tf_op jit(solution)/shard_map/ppermute | solution.py:97
  66.3 6.6 %collective-permute-start.13 = (bf16[80,384]{1,0:T(8,128)(2,1)S(1)}, bf16[80,384]{1,0:T(8,128)(2,1)S(1)}, u32[]{:S(2)}, u32[]{:S(2)}) collective-permute-start(bf16[80,384]{1,0:T(8,128)(2,1)S(1)} %collective-permute-done.11), channel_id=1, source_target_pairs={{0,480},{32,0},{64,32},{96,64},{128,96},{160,128},{192,160},{224,1... | collective-permute-start | bytes 184328 | tf_op jit(solution)/shard_map/ppermute | solution.py:100
  70.9 6.2 %collective-permute-start.14 = (bf16[80,384]{1,0:T(8,128)(2,1)S(1)}, bf16[80,384]{1,0:T(8,128)(2,1)S(1)}, u32[]{:S(2)}, u32[]{:S(2)}) collective-permute-start(bf16[80,384]{1,0:T(8,128)(2,1)S(1)} %collective-permute-done.12), channel_id=1, source_target_pairs={{0,32},{32,64},{64,96},{96,128},{128,160},{160,192},{192,224},{224... | collective-permute-start | bytes 184328 | tf_op jit(solution)/shard_map/ppermute | solution.py:97
  77.1 19.9 %collective-permute-start.15 = (bf16[16,80,384]{2,1,0:T(8,128)(2,1)S(1)}, bf16[16,80,384]{2,1,0:T(8,128)(2,1)S(1)}, u32[]{:S(2)}, u32[]{:S(2)}) collective-permute-start(bf16[16,80,384]{2,1,0:T(8,128)(2,1)S(1)} %bitcast_dynamic-update-slice_fusion.4), channel_id=1, source_target_pairs={{0,8},{8,16},{16,24},{24,0},{1,9},{9,17},{17,25},{25,1},{2,10},{10... | collective-permute-start | bytes 2949128 | tf_op jit(solution)/shard_map/ppermute | solution.py:97
  80.4 19.7 %collective-permute-start.16 = (bf16[16,80,384]{2,1,0:T(8,128)(2,1)S(1)}, bf16[16,80,384]{2,1,0:T(8,128)(2,1)S(1)}, u32[]{:S(2)}, u32[]{:S(2)}) collective-permute-start(bf16[16,80,384]{2,1,0:T(8,128)(2,1)S(1)} %bitcast_dynamic-update-slice_fusion.4), channel_id=1, source_target_pairs={{0,24},{8,0},{16,8},{24,16},{1,25},{9,1},{17,9},{25,17},{2,26},{10... | collective-permute-start | bytes 2949128 | tf_op jit(solution)/shard_map/ppermute | solution.py:100
  97.0 20.3 %collective-permute-start.17 = (bf16[16,80,384]{2,1,0:T(8,128)(2,1)S(1)}, bf16[16,80,384]{2,1,0:T(8,128)(2,1)}, u32[]{:S(2)}, u32[]{:S(2)}) collective-permute-start(bf16[16,80,384]{2,1,0:T(8,128)(2,1)S(1)} %collective-permute-done.15), channel_id=1, source_target_pairs={{0,8},{8,16},{16,24},{24,0},{1,9},{9,17},{17,25},{25,1},{2,10},{10... | collective-permute-start | bytes 2949128 | tf_op jit(solution)/shard_map/ppermute | solution.py:97
  124.7 1.6 copy-start.6
  128.6 24.8 %all-to-all-start = ((f32[8,64,384]{2,1,0:T(8,128)}), f32[8,64,384]{2,1,0:T(8,128)S(1)}, u32[]{:S(2)}, u32[]{:S(2)}) async-start(f32[8,64,384]{2,1,0:T(8,128)} %fusion.79), calls=%async_computation | async-start | bytes 1572864 | tf_op jit(solution)/shard_map/all_to_all | solution.py:168
  141.3 53.7 %all-gather.5.cloned.1.call-start = ((), (), s32[]{:S(2)}) async-start(), calls=%async_computation.2 | async-start | bytes 2949120 | tf_op jit(solution)/shard_map/all_gather | solution.py:197
  155.4 2.5 %copy-start.5 = (bf16[4,2,128,256]{3,2,1,0:T(8,128)(2,1)S(1)}, bf16[4,2,128,256]{3,2,1,0:T(8,128)(2,1)}, u32[]{:S(2)}) copy-start(bf16[4,2,128,256]{3,2,1,0:T(8,128)(2,1)} %gather_fusion) | copy-start | bytes 1572868
  160.9 1.7 copy-start.2
  191.2 2.2 %copy-start.4 = (bf16[4,2,128,256]{3,2,1,0:T(8,128)(2,1)S(1)}, bf16[4,2,128,256]{3,2,1,0:T(8,128)(2,1)}, u32[]{:S(2)}) copy-start(bf16[4,2,128,256]{3,2,1,0:T(8,128)(2,1)} %get-tuple-element.3) | copy-start | bytes 1572868
  192.3 2.7 %copy-start.7 = (bf16[256,320]{0,1:T(8,128)(2,1)S(1)}, bf16[256,320]{0,1:T(8,128)(2,1)}, u32[]{:S(2)}) copy-start(bf16[256,320]{0,1:T(8,128)(2,1)} %slice.181) | copy-start | bytes 491524
  192.4 4.0 %copy-start.8 = (bf16[256,320]{0,1:T(8,128)(2,1)S(1)}, bf16[256,320]{0,1:T(8,128)(2,1)}, u32[]{:S(2)}) copy-start(bf16[256,320]{0,1:T(8,128)(2,1)} %slice.178) | copy-start | bytes 491524
  192.9 4.7 %copy-start.9 = (bf16[256,320]{0,1:T(8,128)(2,1)S(1)}, bf16[256,320]{0,1:T(8,128)(2,1)}, u32[]{:S(2)}) copy-start(bf16[256,320]{0,1:T(8,128)(2,1)} %slice.175) | copy-start | bytes 491524
  193.5 5.4 %copy-start.10 = (bf16[256,320]{0,1:T(8,128)(2,1)S(1)}, bf16[256,320]{0,1:T(8,128)(2,1)}, u32[]{:S(2)}) copy-start(bf16[256,320]{0,1:T(8,128)(2,1)} %slice.172) | copy-start | bytes 491524
  195.0 3.9 %copy-start.3 = (bf16[512,2560]{1,0:T(8,128)(2,1)S(1)}, bf16[512,2560]{1,0:T(8,128)(2,1)}, u32[]{:S(2)}) copy-start(bf16[512,2560]{1,0:T(8,128)(2,1)} %all-gather.5.cloned.1.call-done) | copy-start | bytes 7864324
  200.3 1.5 copy-start.1
Sparse Core Ops, SparseCore 0:
  25.3 32.5 all-gather.2
  162.2 29.0 all-gather.4

commit v2 on v1

--- a/solution.py
+++ b/solution.py
@@ -112,11 +112,7 @@
         column = lax.dynamic_update_slice_in_dim(
             column, got[None], (z_index + offset) % z_size, axis=0
         )
-    placed = jnp.zeros((z_size, x_size) + piece.shape, piece.dtype)
-    for offset, got in ring_pieces(column, "tx").items():
-        placed = lax.dynamic_update_slice_in_dim(
-            placed, got[:, None], (x_index + offset) % x_size, axis=1
-        )
+    placed = lax.all_gather(column, "tx", axis=1, tiled=False)
     return placed.reshape((z_size * x_size,) + piece.shape)
 
 
@@ -195,20 +191,22 @@
         reach[None],
     )
     mixed = lax.all_gather(result.reshape(DRAFT, HQ * HD), "head", axis=0, tiled=True)
-    summed = jnp.zeros((mixed.shape[0], wo_cols.shape[1]), jnp.float32)
+    per_head = lax.dot_general(
+        mixed.reshape(mixed.shape[0], HQ, HD),
+        wo_cols.reshape(HQ, HD, wo_cols.shape[1]),
+        (((2,), (1,)), ((1,), (0,))),
+        preferred_element_type=jnp.float32,
+    )
+    summed = None
     for group in range(head_count):
         head_ids = [k for k in range(group, HQ, head_count)]
         if not head_ids:
             continue
-        partial_value = None
-        for k in head_ids:
-            term = jnp.dot(
-                mixed[:, k * HD : (k + 1) * HD],
-                wo_cols[k * HD : (k + 1) * HD],
-                preferred_element_type=jnp.float32,
-            )
-            partial_value = term if partial_value is None else partial_value + term
-        summed = summed + partial_value.astype(jnp.bfloat16).astype(jnp.float32)
+        partial_value = per_head[head_ids[0]]
+        for k in head_ids[1:]:
+            partial_value = partial_value + per_head[k]
+        term = partial_value.astype(jnp.bfloat16).astype(jnp.float32)
+        summed = term if summed is None else summed + term
     attended = summed.astype(jnp.bfloat16)
     new_pages = refresh(own_pages, length, leaf, reach, depth, tree_keys, tree_values)
     matches = (own_table[:, None] == jnp.arange(pages_dev, dtype=jnp.int32)[None, :]).astype(

time: 210 us -> 215 us (1.024)
  waiting for transfers between devices: 43.8 us -> 62.2 us
  starting transfers between devices: 75.9 us -> 59.9 us
  other arithmetic: 6.56 us -> 13.5 us
  local copies, waits for them, and re-layouts: 52.6 us -> 50.4 us
    all_gather x0 -> x1, waiting for transfers between devices: none -> 43.6 us  [grid_gather(): placed = lax.all_gather(column, 'tx', axis=1, tiled=False)]
    ppermute x10 -> x8, waiting for transfers between devices: 34.5 us -> 4.21 us  [ring_pieces(): lax.ppermute(ahead, axis, [(i, (i + 1) % size) for i in range(size)])]
    slice x22 -> x0, local copies, waits for them, and re-layouts: 18.9 us -> none  [the longest x21 16.6 us: shards(): wo_cols[k * HD:(k + 1) * HD]]
    all_to_all x1, starting transfers between devices: 12.7 us -> 5.12 us  [shards(): mine = lax.all_to_all(both, 'head', 0, 1, tiled=True)]
    transpose x0 -> x1, local copies, waits for them, and re-layouts: none -> 7.17 us  [shards(): wo_cols = stacked[:, part_rows:].reshape(tok_count, -1)[:, :wo_flat.shape...]
    all_gather x1, waiting for transfers between devices: 0.01 us -> 6.05 us  [shards(): lax.all_gather(result.reshape(DRAFT, HQ * HD), 'head', axis=0, tiled=True)]
    ppermute x10 -> x8, starting transfers between devices: 22.8 us -> 17.8 us  [ring_pieces(): lax.ppermute(ahead, axis, [(i, (i + 1) % size) for i in range(size)])]
    dot_general x10 -> x1, matrix products: 6.62 us -> 3.11 us  [shards(): lax.dot_general(mixed.reshape(mixed.shape[0], HQ, HD), wo_cols.reshape(HQ...]
  transfers between devices with their start and end apart: 21 -> 19, of which waited for: 4 -> 4; matrix products, arithmetic and copies ran while one was open for 21% -> 22% of each run, Pallas kernels for 0% -> 0%
where the time goes in v2:
time: 215 us; the launch traced here: 213 us
  waiting for transfers between devices  62.2 us (29%)
  starting transfers between devices  59.9 us (28%)
  local copies, waits for them, and re-layouts  50.4 us (23%)
  between operations  16.8 us (8%)
  other arithmetic  13.5 us (6%)
  matrix products  10.3 us (5%)
    all_gather x1, waiting for transfers between devices, grid_gather(): placed = lax.all_gather(column, 'tx', axis=1, tiled=False)  43.6 us
    ppermute x7, starting transfers between devices, ring_pieces(): lax.ppermute(behind, axis, [(i, (i - 1) % size) for i in range(size)])  36.9 us
    ppermute x8, starting transfers between devices, ring_pieces(): lax.ppermute(ahead, axis, [(i, (i + 1) % size) for i in range(size)])  17.8 us
    slice x3, local copies, waits for them, and re-layouts, shards(): stacked[:, part_rows:].reshape(tok_count, -1)[:, :wo_flat.shape[0]]  9.77 us
    all_to_all x1, waiting for transfers between devices, shards(): mine = lax.all_to_all(both, 'head', 0, 1, tiled=True)  7.63 us
    transpose x1, local copies, waits for them, and re-layouts, shards(): wo_cols = stacked[:, part_rows:].reshape(tok_count, -1)[:, :wo_flat.shape...  7.17 us
    reshape x1, local copies, waits for them, and re-layouts, shards(): wo_cols = stacked[:, part_rows:].reshape(tok_count, -1)[:, :wo_flat.shape...  7.09 us
    all_gather x1, waiting for transfers between devices, shards(): lax.all_gather(result.reshape(DRAFT, HQ * HD), 'head', axis=0, tiled=True)  6.05 us
  transfers between devices with their start and end apart: 19, of which 4 were waited for; matrix products, arithmetic and copies ran while one was open for 22% of the time, Pallas kernels for 0%

profile of v2, /device:TPU:1, one launch (start us, length us, event | category | flops | bytes accessed | tf_op | source)
XLA Modules:
  0.0 213.2 jit_solution(10912593153138224858)
XLA Ops:
  7.2 0.7 all-gather.4.cloned.1.call-update
  8.0 1.2 copy.51
  9.1 1.0 reshape.398
  10.2 0.8 constant_dynamic-slice_fusion.1
  11.0 0.9 constant_dynamic-slice_fusion.2
  12.0 4.4 %collective-permute-start = (bf16[80,384]{1,0:T(8,128)(2,1)S(1)}, bf16[80,384]{1,0:T(8,128)(2,1)S(1)}, u32[]{:S(2)}, u32[]{:S(2)}) collective-permute-start(bf16[80,384]{1,0:T(8,128)(2,1)S(1)} %get-tuple-element.6), channel_id=1, source_target_pairs={{0,32},{32,64},{64,96},{96,128},{128,160},{160,192},{192,224},{224... | collective-permute-start | bytes 184328 | tf_op jit(solution)/shard_map/ppermute | solution.py:97
  16.4 9.5 %collective-permute-start.1 = (bf16[80,384]{1,0:T(8,128)(2,1)S(1)}, bf16[80,384]{1,0:T(8,128)(2,1)S(1)}, u32[]{:S(2)}, u32[]{:S(2)}) collective-permute-start(bf16[80,384]{1,0:T(8,128)(2,1)S(1)} %get-tuple-element.6), channel_id=1, source_target_pairs={{0,480},{32,0},{64,32},{96,64},{128,96},{160,128},{192,160},{224,1... | collective-permute-start | bytes 184328 | tf_op jit(solution)/shard_map/ppermute | solution.py:100
  26.1 1.9 collective-permute-start.2
  28.1 4.6 %collective-permute-start.3 = (bf16[80,384]{1,0:T(8,128)(2,1)S(1)}, bf16[80,384]{1,0:T(8,128)(2,1)S(1)}, u32[]{:S(2)}, u32[]{:S(2)}) collective-permute-start(bf16[80,384]{1,0:T(8,128)(2,1)S(1)} %collective-permute-done.1), channel_id=1, source_target_pairs={{0,480},{32,0},{64,32},{96,64},{128,96},{160,128},{192,160},{224,1... | collective-permute-start | bytes 184328 | tf_op jit(solution)/shard_map/ppermute | solution.py:100
  32.7 1.9 collective-permute-start.4
  34.6 4.6 %collective-permute-start.5 = (bf16[80,384]{1,0:T(8,128)(2,1)S(1)}, bf16[80,384]{1,0:T(8,128)(2,1)S(1)}, u32[]{:S(2)}, u32[]{:S(2)}) collective-permute-start(bf16[80,384]{1,0:T(8,128)(2,1)S(1)} %collective-permute-done.3), channel_id=1, source_target_pairs={{0,480},{32,0},{64,32},{96,64},{128,96},{160,128},{192,160},{224,1... | collective-permute-start | bytes 184328 | tf_op jit(solution)/shard_map/ppermute | solution.py:100
  39.3 1.9 collective-permute-start.6
  41.2 4.6 %collective-permute-start.7 = (bf16[80,384]{1,0:T(8,128)(2,1)S(1)}, bf16[80,384]{1,0:T(8,128)(2,1)S(1)}, u32[]{:S(2)}, u32[]{:S(2)}) collective-permute-start(bf16[80,384]{1,0:T(8,128)(2,1)S(1)} %collective-permute-done.5), channel_id=1, source_target_pairs={{0,480},{32,0},{64,32},{96,64},{128,96},{160,128},{192,160},{224,1... | collective-permute-start | bytes 184328 | tf_op jit(solution)/shard_map/ppermute | solution.py:100
  45.9 1.9 collective-permute-start.8
  47.8 4.6 %collective-permute-start.9 = (bf16[80,384]{1,0:T(8,128)(2,1)S(1)}, bf16[80,384]{1,0:T(8,128)(2,1)S(1)}, u32[]{:S(2)}, u32[]{:S(2)}) collective-permute-start(bf16[80,384]{1,0:T(8,128)(2,1)S(1)} %collective-permute-done.7), channel_id=1, source_target_pairs={{0,480},{32,0},{64,32},{96,64},{128,96},{160,128},{192,160},{224,1... | collective-permute-start | bytes 184328 | tf_op jit(solution)/shard_map/ppermute | solution.py:100
  52.4 1.9 collective-permute-start.10
  54.4 4.6 %collective-permute-start.11 = (bf16[80,384]{1,0:T(8,128)(2,1)S(1)}, bf16[80,384]{1,0:T(8,128)(2,1)S(1)}, u32[]{:S(2)}, u32[]{:S(2)}) collective-permute-start(bf16[80,384]{1,0:T(8,128)(2,1)S(1)} %collective-permute-done.9), channel_id=1, source_target_pairs={{0,480},{32,0},{64,32},{96,64},{128,96},{160,128},{192,160},{224,1... | collective-permute-start | bytes 184328 | tf_op jit(solution)/shard_map/ppermute | solution.py:100
  59.0 1.9 collective-permute-start.12
  61.0 4.6 %collective-permute-start.13 = (bf16[80,384]{1,0:T(8,128)(2,1)S(1)}, bf16[80,384]{1,0:T(8,128)(2,1)S(1)}, u32[]{:S(2)}, u32[]{:S(2)}) collective-permute-start(bf16[80,384]{1,0:T(8,128)(2,1)S(1)} %collective-permute-done.11), channel_id=1, source_target_pairs={{0,480},{32,0},{64,32},{96,64},{128,96},{160,128},{192,160},{224,1... | collective-permute-start | bytes 184328 | tf_op jit(solution)/shard_map/ppermute | solution.py:100
  65.6 1.9 collective-permute-start.14
  67.6 4.2 %collective-permute-done.14 = bf16[80,384]{1,0:T(8,128)(2,1)S(1)} collective-permute-done((bf16[80,384]{1,0:T(8,128)(2,1)S(1)}, bf16[80,384]{1,0:T(8,128)(2,1)S(1)}, u32[]{:S(2)}, u32[]{:S(2)}) %collective-permute-start.14) | collective-permute-done | bytes 61472 | tf_op jit(solution)/shard_map/ppermute | solution.py:97
  71.8 1.0 copy-done.1
  72.8 0.6 dynamic_slice.29
  74.7 0.6 dynamic_slice.25
  75.9 0.7 fusion.39
  78.0 0.7 iota_compare_fusion.6
  78.7 0.7 iota_subtract_fusion
  79.5 0.5 compare_select_fusion
  80.2 1.1 add_add_fusion
  81.3 3.0 %copy.50 = bf16[512,2560]{1,0:T(8,128)(2,1)S(1)} copy(bf16[512,2560]{0,1:T(8,128)(2,1)} %all-gather.4.cloned.1.call-done) | data formatting | bytes 5242880 | tf_op jit(solution)/shard_map/all_gather | solution.py:159
  84.3 0.6 fusion
  84.9 2.0 fusion.1
  86.9 43.6 %all-gather.6.cloned.1.call-done = bf16[16,4,80,384]{3,2,1,0:T(8,128)(2,1)} async-done(((bf16[16,1,80,384]{3,2,1,0:T(8,128)(2,1)}), bf16[16,4,80,384]{3,2,1,0:T(8,128)(2,1)}) %all-gather.6.cloned.1.call-update) | async-done | bytes 3932176 | tf_op jit(solution)/shard_map/all_gather | solution.py:115
  130.5 2.7 %fusion.45 = (bf16[64,40,384]{2,1,0:T(8,128)(2,1)S(1)}, bf16[64,40,384]{2,1,0:T(8,128)(2,1)S(1)}) fusion(bf16[64,80,384]{2,1,0:T(8,128)(2,1)} %bitcast.131), kind=kLoop, calls=%fused_computation.121 | loop fusion | bytes 7864320 | tf_op jit(solution)/shard_map/slice | solution.py:153
  133.4 2.4 %fusion.54 = f32[8,64,384]{2,1,0:T(8,128)} fusion(bf16[8,64,2560]{2,1,0:T(8,128)(2,1)S(1)} %bitcast.132, bf16[2560,384,1]{1,0,2:T(8,128)(2,1)S(1)} %bitcast.133), kind=kOutput, calls=%fused_computation.128 | convolution fusion | flops 1006632960 | bytes 5373952 | tf_op jit(solution)/shard_map/dot_general | solution.py:163
  135.8 5.1 %all-to-all-start = ((f32[8,64,384]{2,1,0:T(8,128)}), f32[8,64,384]{2,1,0:T(8,128)S(1)}, u32[]{:S(2)}, u32[]{:S(2)}) async-start(f32[8,64,384]{2,1,0:T(8,128)} %fusion.54), calls=%async_computation | async-start | bytes 1572864 | tf_op jit(solution)/shard_map/all_to_all | solution.py:164
  141.0 0.6 multiply_exponential_fusion
  141.6 0.7 copy.56
  142.2 1.4 gather_fusion
  143.6 0.6 compare_and_fusion.3
  144.2 0.6 compare_bitcast_fusion
  144.8 0.7 fusion.20
  145.5 7.6 %all-to-all-done = f32[8,64,384]{2,1,0:T(8,128)S(1)} async-done(((f32[8,64,384]{2,1,0:T(8,128)}), f32[8,64,384]{2,1,0:T(8,128)S(1)}, u32[]{:S(2)}, u32[]{:S(2)}) %all-to-all-start) | async-done | bytes 786464 | tf_op jit(solution)/shard_map/all_to_all | solution.py:164
  153.4 0.8 reshape.403
  154.2 0.9 convert.35
  155.1 0.6 copy-done.6
  155.7 1.7 convolution_convert_fusion
  157.5 1.3 copy.52
  158.8 1.6 reshape.402
  160.7 0.6 copy-done.5
  161.9 1.0 fusion.14
  163.7 0.5 fusion.48
  165.5 0.7 copy.72
  166.3 3.8 %copy.61 = bf16[64,40,384]{0,2,1:T(8,128)(2,1)} copy(bf16[64,40,384]{2,1,0:T(8,128)(2,1)S(1)} %get-tuple-element.7) | data formatting | bytes 3932160 | tf_op jit(solution)/shard_map/slice | solution.py:153
  170.1 3.3 %slice.113 = bf16[64,12800]{0,1:T(8,128)(2,1)} slice(bf16[64,15360]{0,1:T(8,128)(2,1)} %bitcast.127), slice={[0:64], [0:12800]} | slice | bytes 3276800 | tf_op jit(solution)/shard_map/slice | solution.py:153
  173.4 7.1 %reshape.409 = bf16[64,2560,5]{0,2,1:T(8,128)(2,1)} reshape(bf16[64,12800]{0,1:T(8,128)(2,1)} %slice.113) | data formatting | bytes 3276800 | tf_op jit(solution)/shard_map/reshape | solution.py:155
  180.4 7.2 %copy.62 = bf16[2560,64,5]{0,2,1:T(8,128)(2,1)S(1)} copy(bf16[2560,64,5]{1,2,0:T(8,128)(2,1)} %bitcast.126) | data formatting | bytes 3276800 | tf_op jit(solution)/shard_map/transpose | solution.py:156
  187.6 3.1 %reshape_reshape.3 = bf16[10,256,320]{1,0,2:T(8,128)(2,1)} reshape(bf16[2560,64,5]{0,2,1:T(8,128)(2,1)S(1)} %copy.62) | data formatting | bytes 3276800 | tf_op jit(solution)/shard_map/reshape;reshape | solution.py:196
  190.7 1.6 gather_fusion.1
  192.4 0.9 broadcast_select_fusion
  193.3 6.0 %all-gather.8.cloned.1.call-done = bf16[512,2560]{1,0:T(8,128)(2,1)} async-done(((bf16[64,2560]{1,0:T(8,128)(2,1)}), bf16[512,2560]{1,0:T(8,128)(2,1)}) %all-gather.8.cloned.1.call-update) | async-done | bytes 2621456 | tf_op jit(solution)/shard_map/all_gather | solution.py:193
  199.3 3.0 %copy.60 = bf16[512,2560]{0,1:T(8,128)(2,1)S(1)} copy(bf16[512,2560]{1,0:T(8,128)(2,1)} %all-gather.8.cloned.1.call-done) | data formatting | bytes 5242880 | tf_op jit(solution)/shard_map/all_gather | solution.py:193
  202.3 3.1 %fusion.50 = (bf16[10,512,320]{1,2,0:T(8,128)(2,1)S(1)}, f32[10,512,320]{1,2,0:T(8,128)S(1)}) fusion(bf16[512,10,256]{0,2,1:T(8,128)(2,1)S(1)} %bitcast.128, bf16[10,256,320]{1,0,2:T(8,128)(2,1)} %reshape_reshape.3), kind=kOutput, calls=%fused_computation.126 | convolution fusion | flops 840499200 | bytes 14090240 | tf_op jit(solution)/shard_map/dot_general | solution.py:194
  205.4 1.2 fusion.15
  (118 shorter events, 5.6 us)
Async XLA Ops:
  7.2 135.1 %copy-start = (bf16[4,2,128,256]{3,2,1,0:T(8,128)(2,1)S(1)}, bf16[4,2,128,256]{3,2,1,0:T(8,128)(2,1)}, u32[]{:S(2)}) copy-start(bf16[4,2,128,256]{3,2,1,0:T(8,128)(2,1)} %param.15) | copy-start | bytes 1572868
  7.2 74.1 %all-gather.4.cloned.1.call-start = ((), (), s32[]{:S(2)}) async-start(), calls=%async_computation.1 | async-start | bytes 2949120 | tf_op jit(solution)/shard_map/all_gather | solution.py:159
  7.9 122.6 %all-gather.6.cloned.1.call-start = ((), (), s32[]{:S(2)}) async-start(), calls=%async_computation.2 | async-start | bytes 4915200 | tf_op jit(solution)/shard_map/all_gather | solution.py:115
  9.1 63.6 %copy-start.23 = (s32[8]{0:T(128)S(1)}, s32[8]{0:T(128)}, u32[]{:S(2)}) copy-start(s32[8]{0:T(128)} %param.19) | copy-start | bytes 100
  9.1 65.6 %copy-start.24 = (s32[8]{0:T(128)S(1)}, s32[8]{0:T(128)}, u32[]{:S(2)}) copy-start(s32[8]{0:T(128)} %param.18) | copy-start | bytes 100
  10.1 67.7 %copy-start.18 = (s32[8,4]{0,1:T(4,128)S(1)}, s32[8,4]{0,1:T(4,128)}, u32[]{:S(2)}) copy-start(s32[8,4]{0,1:T(4,128)} %param.16) | copy-start | bytes 388
  12.0 14.1 %collective-permute-start = (bf16[80,384]{1,0:T(8,128)(2,1)S(1)}, bf16[80,384]{1,0:T(8,128)(2,1)S(1)}, u32[]{:S(2)}, u32[]{:S(2)}) collective-permute-start(bf16[80,384]{1,0:T(8,128)(2,1)S(1)} %get-tuple-element.6), channel_id=1, source_target_pairs={{0,32},{32,64},{64,96},{96,128},{128,160},{160,192},{192,224},{224... | collective-permute-start | bytes 184328 | tf_op jit(solution)/shard_map/ppermute | solution.py:97
  16.4 11.7 %collective-permute-start.1 = (bf16[80,384]{1,0:T(8,128)(2,1)S(1)}, bf16[80,384]{1,0:T(8,128)(2,1)S(1)}, u32[]{:S(2)}, u32[]{:S(2)}) collective-permute-start(bf16[80,384]{1,0:T(8,128)(2,1)S(1)} %get-tuple-element.6), channel_id=1, source_target_pairs={{0,480},{32,0},{64,32},{96,64},{128,96},{160,128},{192,160},{224,1... | collective-permute-start | bytes 184328 | tf_op jit(solution)/shard_map/ppermute | solution.py:100
  26.1 6.6 %collective-permute-start.2 = (bf16[80,384]{1,0:T(8,128)(2,1)S(1)}, bf16[80,384]{1,0:T(8,128)(2,1)S(1)}, u32[]{:S(2)}, u32[]{:S(2)}) collective-permute-start(bf16[80,384]{1,0:T(8,128)(2,1)S(1)} %collective-permute-done), channel_id=1, source_target_pairs={{0,32},{32,64},{64,96},{96,128},{128,160},{160,192},{192,224},{224... | collective-permute-start | bytes 184328 | tf_op jit(solution)/shard_map/ppermute | solution.py:97
  28.1 6.6 %collective-permute-start.3 = (bf16[80,384]{1,0:T(8,128)(2,1)S(1)}, bf16[80,384]{1,0:T(8,128)(2,1)S(1)}, u32[]{:S(2)}, u32[]{:S(2)}) collective-permute-start(bf16[80,384]{1,0:T(8,128)(2,1)S(1)} %collective-permute-done.1), channel_id=1, source_target_pairs={{0,480},{32,0},{64,32},{96,64},{128,96},{160,128},{192,160},{224,1... | collective-permute-start | bytes 184328 | tf_op jit(solution)/shard_map/ppermute | solution.py:100
  32.7 6.6 %collective-permute-start.4 = (bf16[80,384]{1,0:T(8,128)(2,1)S(1)}, bf16[80,384]{1,0:T(8,128)(2,1)S(1)}, u32[]{:S(2)}, u32[]{:S(2)}) collective-permute-start(bf16[80,384]{1,0:T(8,128)(2,1)S(1)} %collective-permute-done.2), channel_id=1, source_target_pairs={{0,32},{32,64},{64,96},{96,128},{128,160},{160,192},{192,224},{224... | collective-permute-start | bytes 184328 | tf_op jit(solution)/shard_map/ppermute | solution.py:97
  34.6 6.6 %collective-permute-start.5 = (bf16[80,384]{1,0:T(8,128)(2,1)S(1)}, bf16[80,384]{1,0:T(8,128)(2,1)S(1)}, u32[]{:S(2)}, u32[]{:S(2)}) collective-permute-start(bf16[80,384]{1,0:T(8,128)(2,1)S(1)} %collective-permute-done.3), channel_id=1, source_target_pairs={{0,480},{32,0},{64,32},{96,64},{128,96},{160,128},{192,160},{224,1... | collective-permute-start | bytes 184328 | tf_op jit(solution)/shard_map/ppermute | solution.py:100
  39.3 6.6 %collective-permute-start.6 = (bf16[80,384]{1,0:T(8,128)(2,1)S(1)}, bf16[80,384]{1,0:T(8,128)(2,1)S(1)}, u32[]{:S(2)}, u32[]{:S(2)}) collective-permute-start(bf16[80,384]{1,0:T(8,128)(2,1)S(1)} %collective-permute-done.4), channel_id=1, source_target_pairs={{0,32},{32,64},{64,96},{96,128},{128,160},{160,192},{192,224},{224... | collective-permute-start | bytes 184328 | tf_op jit(solution)/shard_map/ppermute | solution.py:97
  41.2 6.6 %collective-permute-start.7 = (bf16[80,384]{1,0:T(8,128)(2,1)S(1)}, bf16[80,384]{1,0:T(8,128)(2,1)S(1)}, u32[]{:S(2)}, u32[]{:S(2)}) collective-permute-start(bf16[80,384]{1,0:T(8,128)(2,1)S(1)} %collective-permute-done.5), channel_id=1, source_target_pairs={{0,480},{32,0},{64,32},{96,64},{128,96},{160,128},{192,160},{224,1... | collective-permute-start | bytes 184328 | tf_op jit(solution)/shard_map/ppermute | solution.py:100
  45.9 6.6 %collective-permute-start.8 = (bf16[80,384]{1,0:T(8,128)(2,1)S(1)}, bf16[80,384]{1,0:T(8,128)(2,1)S(1)}, u32[]{:S(2)}, u32[]{:S(2)}) collective-permute-start(bf16[80,384]{1,0:T(8,128)(2,1)S(1)} %collective-permute-done.6), channel_id=1, source_target_pairs={{0,32},{32,64},{64,96},{96,128},{128,160},{160,192},{192,224},{224... | collective-permute-start | bytes 184328 | tf_op jit(solution)/shard_map/ppermute | solution.py:97
  47.8 6.6 %collective-permute-start.9 = (bf16[80,384]{1,0:T(8,128)(2,1)S(1)}, bf16[80,384]{1,0:T(8,128)(2,1)S(1)}, u32[]{:S(2)}, u32[]{:S(2)}) collective-permute-start(bf16[80,384]{1,0:T(8,128)(2,1)S(1)} %collective-permute-done.7), channel_id=1, source_target_pairs={{0,480},{32,0},{64,32},{96,64},{128,96},{160,128},{192,160},{224,1... | collective-permute-start | bytes 184328 | tf_op jit(solution)/shard_map/ppermute | solution.py:100
  52.4 6.6 %collective-permute-start.10 = (bf16[80,384]{1,0:T(8,128)(2,1)S(1)}, bf16[80,384]{1,0:T(8,128)(2,1)S(1)}, u32[]{:S(2)}, u32[]{:S(2)}) collective-permute-start(bf16[80,384]{1,0:T(8,128)(2,1)S(1)} %collective-permute-done.8), channel_id=1, source_target_pairs={{0,32},{32,64},{64,96},{96,128},{128,160},{160,192},{192,224},{224... | collective-permute-start | bytes 184328 | tf_op jit(solution)/shard_map/ppermute | solution.py:97
  54.4 6.6 %collective-permute-start.11 = (bf16[80,384]{1,0:T(8,128)(2,1)S(1)}, bf16[80,384]{1,0:T(8,128)(2,1)S(1)}, u32[]{:S(2)}, u32[]{:S(2)}) collective-permute-start(bf16[80,384]{1,0:T(8,128)(2,1)S(1)} %collective-permute-done.9), channel_id=1, source_target_pairs={{0,480},{32,0},{64,32},{96,64},{128,96},{160,128},{192,160},{224,1... | collective-permute-start | bytes 184328 | tf_op jit(solution)/shard_map/ppermute | solution.py:100
  59.0 6.6 %collective-permute-start.12 = (bf16[80,384]{1,0:T(8,128)(2,1)S(1)}, bf16[80,384]{1,0:T(8,128)(2,1)S(1)}, u32[]{:S(2)}, u32[]{:S(2)}) collective-permute-start(bf16[80,384]{1,0:T(8,128)(2,1)S(1)} %collective-permute-done.10), channel_id=1, source_target_pairs={{0,32},{32,64},{64,96},{96,128},{128,160},{160,192},{192,224},{224... | collective-permute-start | bytes 184328 | tf_op jit(solution)/shard_map/ppermute | solution.py:97
  61.0 6.6 %collective-permute-start.13 = (bf16[80,384]{1,0:T(8,128)(2,1)S(1)}, bf16[80,384]{1,0:T(8,128)(2,1)S(1)}, u32[]{:S(2)}, u32[]{:S(2)}) collective-permute-start(bf16[80,384]{1,0:T(8,128)(2,1)S(1)} %collective-permute-done.11), channel_id=1, source_target_pairs={{0,480},{32,0},{64,32},{96,64},{128,96},{160,128},{192,160},{224,1... | collective-permute-start | bytes 184328 | tf_op jit(solution)/shard_map/ppermute | solution.py:100
  65.6 6.2 %collective-permute-start.14 = (bf16[80,384]{1,0:T(8,128)(2,1)S(1)}, bf16[80,384]{1,0:T(8,128)(2,1)S(1)}, u32[]{:S(2)}, u32[]{:S(2)}) collective-permute-start(bf16[80,384]{1,0:T(8,128)(2,1)S(1)} %collective-permute-done.12), channel_id=1, source_target_pairs={{0,32},{32,64},{64,96},{96,128},{128,160},{160,192},{192,224},{224... | collective-permute-start | bytes 184328 | tf_op jit(solution)/shard_map/ppermute | solution.py:97
  71.8 1.0 copy-start.1
  78.7 2.6 %copy-start.12 = (pred[64]{0:T(512)(128)(4,1)}, pred[64]{0:T(512)(128)(4,1)S(1)}, u32[]{:S(2)}) copy-start(pred[64]{0:T(512)(128)(4,1)S(1)} %compare_bitcast_fusion.1) | copy-start | bytes 196
  79.4 0.6 copy-start.10
  80.0 1.3 copy-start.14
  130.5 2.9 %copy-start.2 = (bf16[512,2560]{1,0:T(8,128)(2,1)S(1)}, bf16[512,2560]{1,0:T(8,128)(2,1)}, u32[]{:S(2)}) copy-start(bf16[512,2560]{1,0:T(8,128)(2,1)} %fusion.1) | copy-start | bytes 7864324
  135.8 17.3 %all-to-all-start = ((f32[8,64,384]{2,1,0:T(8,128)}), f32[8,64,384]{2,1,0:T(8,128)S(1)}, u32[]{:S(2)}, u32[]{:S(2)}) async-start(f32[8,64,384]{2,1,0:T(8,128)} %fusion.54), calls=%async_computation | async-start | bytes 1572864 | tf_op jit(solution)/shard_map/all_to_all | solution.py:164
  141.0 58.4 %all-gather.8.cloned.1.call-start = ((), (), s32[]{:S(2)}) async-start(), calls=%async_computation.3 | async-start | bytes 2949120 | tf_op jit(solution)/shard_map/all_gather | solution.py:193
  155.1 0.6 copy-start.6
  160.4 0.9 copy-start.5
  160.4 0.9 copy-start.17
  160.4 0.9 copy-start.22
  160.4 1.1 copy-start.11
  160.4 1.1 copy-start.13
  160.4 1.1 copy-start.15
  160.4 1.4 copy-start.3
  160.5 1.4 copy-start.4
  160.5 1.4 copy-start.20
  160.5 1.4 copy-start.21
  161.9 1.3 copy-start.9
  162.9 0.8 copy-start.8
  163.2 1.5 copy-start.7
  165.0 1.2 copy-start.19
  187.6 4.7 %copy-start.16 = (pred[4]{0:T(512)(128)(4,1)S(1)}, pred[4]{0:T(512)(128)(4,1)}, u32[]{:S(2)}) copy-start(pred[4]{0:T(512)(128)(4,1)} %get-tuple-element.33) | copy-start | bytes 16
Sparse Core Ops, SparseCore 0:
  10.1 39.3 all-gather.3
  72.9 57.5 all-gather.5
  166.4 32.9 all-gather.7

commit v3 on v2

--- a/solution.py
+++ b/solution.py
@@ -90,16 +90,23 @@
 
 def ring_pieces(piece, axis):
     size = lax.axis_size(axis)
-    by_offset = {0: piece}
+    got = [(0, 0, piece)]
     ahead = piece
     behind = piece
+    forward = [(i, (i + 1) % size) for i in range(size)]
+    backward = [(i, (i - 1) % size) for i in range(size)]
     for step in range(1, size // 2 + 1):
-        ahead = lax.ppermute(ahead, axis, [(i, (i + 1) % size) for i in range(size)])
-        by_offset[size - step] = ahead
+        if 2 * step == size and size > 2:
+            half = piece.shape[0] // 2
+            got.append((step, 0, lax.ppermute(ahead[:half], axis, forward)))
+            got.append((step, half, lax.ppermute(behind[half:], axis, backward)))
+            break
+        ahead = lax.ppermute(ahead, axis, forward)
+        got.append((size - step, 0, ahead))
         if step <= (size - 1) // 2:
-            behind = lax.ppermute(behind, axis, [(i, (i - 1) % size) for i in range(size)])
-            by_offset[step] = behind
-    return by_offset
+            behind = lax.ppermute(behind, axis, backward)
+            got.append((step, 0, behind))
+    return got
 
 
 def grid_gather(piece):
@@ -107,12 +114,17 @@
     x_size = lax.axis_size("tx")
     z_index = lax.axis_index("tz")
     x_index = lax.axis_index("tx")
+    zero = jnp.int32(0)
     column = jnp.zeros((z_size,) + piece.shape, piece.dtype)
-    for offset, got in ring_pieces(piece, "tz").items():
-        column = lax.dynamic_update_slice_in_dim(
-            column, got[None], (z_index + offset) % z_size, axis=0
+    for offset, first, part in ring_pieces(piece, "tz"):
+        column = lax.dynamic_update_slice(
+            column, part[None], ((z_index + offset) % z_size, jnp.int32(first), zero)
         )
-    placed = lax.all_gather(column, "tx", axis=1, tiled=False)
+    placed = jnp.zeros((z_size, x_size) + piece.shape, piece.dtype)
+    for offset, first, part in ring_pieces(column, "tx"):
+        placed = lax.dynamic_update_slice(
+            placed, part[:, None], (jnp.int32(first), (x_index + offset) % x_size, zero, zero)
+        )
     return placed.reshape((z_size * x_size,) + piece.shape)
 
 

time: 215 us -> 202 us (0.940)
  waiting for transfers between devices: 62.2 us -> 34.4 us
  starting transfers between devices: 59.9 us -> 86.2 us
  other arithmetic: 13.5 us -> 7.75 us
  local copies, waits for them, and re-layouts: 50.4 us -> 46.4 us
    all_gather x1 -> x0, waiting for transfers between devices: 43.6 us -> none  [grid_gather(): placed = lax.all_gather(column, 'tx', axis=1, tiled=False)]
    ppermute x15 -> x20, starting transfers between devices: 54.7 us -> 72.8 us  [the longest x8 41.3 us: ring_pieces(): behind = lax.ppermute(behind, axis, backward)]
    ppermute x15 -> x20, waiting for transfers between devices: 4.23 us -> 21.3 us  [the longest x8 11 us: ring_pieces(): behind = lax.ppermute(behind, axis, backward)]
    all_to_all x1, starting transfers between devices: 5.12 us -> 13.3 us  [shards(): mine = lax.all_to_all(both, 'head', 0, 1, tiled=True)]
    all_gather x1, waiting for transfers between devices: 6.05 us -> 1.74 us  [shards(): lax.all_gather(result.reshape(DRAFT, HQ * HD), 'head', axis=0, tiled=True)]
    all_to_all x1, waiting for transfers between devices: 7.63 us -> 11.3 us  [shards(): mine = lax.all_to_all(both, 'head', 0, 1, tiled=True)]
    unnamed x53 -> x17, local copies, waits for them, and re-layouts: 4.46 us -> 3.57 us
  transfers between devices with their start and end apart: 19 -> 23, of which waited for: 4 -> 5; matrix products, arithmetic and copies ran while one was open for 22% -> 18% of each run, Pallas kernels for 0% -> 0%
where the time goes in v3:
time: 202 us; the launch traced here: 201 us
  starting transfers between devices  86.2 us (43%)
  local copies, waits for them, and re-layouts  46.4 us (23%)
  waiting for transfers between devices  34.4 us (17%)
  between operations  17.2 us (9%)
  matrix products  8.93 us (4%)
  other arithmetic  7.75 us (4%)
    ppermute x8, starting transfers between devices, ring_pieces(): behind = lax.ppermute(behind, axis, backward)  41.3 us
    ppermute x8, starting transfers between devices, ring_pieces(): ahead = lax.ppermute(ahead, axis, forward)  17.8 us
    all_to_all x1, starting transfers between devices, shards(): mine = lax.all_to_all(both, 'head', 0, 1, tiled=True)  13.3 us
    all_to_all x1, waiting for transfers between devices, shards(): mine = lax.all_to_all(both, 'head', 0, 1, tiled=True)  11.3 us
    ppermute x8, waiting for transfers between devices, ring_pieces(): behind = lax.ppermute(behind, axis, backward)  11 us
    ppermute x2, starting transfers between devices, ring_pieces(): got.append((step, half, lax.ppermute(behind[half:], axis, backward)))  9.89 us
    ppermute x2, waiting for transfers between devices, ring_pieces(): got.append((step, 0, lax.ppermute(ahead[:half], axis, forward)))  9.46 us
    slice x3, local copies, waits for them, and re-layouts, shards(): stacked[:, part_rows:].reshape(tok_count, -1)[:, :wo_flat.shape[0]]  9.41 us
  transfers between devices with their start and end apart: 23, of which 5 were waited for; matrix products, arithmetic and copies ran while one was open for 18% of the time, Pallas kernels for 0%

profile of v3, /device:TPU:1, one launch (start us, length us, event | category | flops | bytes accessed | tf_op | source)
XLA Modules:
  0.0 201.0 jit_solution(405656939958231230)
XLA Ops:
  7.3 1.2 copy.51
  8.5 1.0 reshape.350
  9.5 0.8 constant_dynamic-slice_fusion.1
  10.3 0.9 constant_dynamic-slice_fusion.2
  11.3 4.4 %collective-permute-start = (bf16[80,384]{1,0:T(8,128)(2,1)S(1)}, bf16[80,384]{1,0:T(8,128)(2,1)S(1)}, u32[]{:S(2)}, u32[]{:S(2)}) collective-permute-start(bf16[80,384]{1,0:T(8,128)(2,1)S(1)} %get-tuple-element.6), channel_id=1, source_target_pairs={{0,32},{32,64},{64,96},{96,128},{128,160},{160,192},{192,224},{224... | collective-permute-start | bytes 184328 | tf_op jit(solution)/shard_map/ppermute | solution.py:104
  15.7 9.5 %collective-permute-start.1 = (bf16[80,384]{1,0:T(8,128)(2,1)S(1)}, bf16[80,384]{1,0:T(8,128)(2,1)S(1)}, u32[]{:S(2)}, u32[]{:S(2)}) collective-permute-start(bf16[80,384]{1,0:T(8,128)(2,1)S(1)} %get-tuple-element.6), channel_id=1, source_target_pairs={{0,480},{32,0},{64,32},{96,64},{128,96},{160,128},{192,160},{224,1... | collective-permute-start | bytes 184328 | tf_op jit(solution)/shard_map/ppermute | solution.py:107
  25.4 0.6 dynamic_slice.29
  27.3 0.6 dynamic_slice.25
  27.9 0.7 fusion.39
  28.9 0.6 iota_subtract_fusion
  31.4 0.7 iota_compare_fusion.6
  32.1 1.9 collective-permute-start.2
  34.0 4.6 %collective-permute-start.3 = (bf16[80,384]{1,0:T(8,128)(2,1)S(1)}, bf16[80,384]{1,0:T(8,128)(2,1)S(1)}, u32[]{:S(2)}, u32[]{:S(2)}) collective-permute-start(bf16[80,384]{1,0:T(8,128)(2,1)S(1)} %collective-permute-done.1), channel_id=1, source_target_pairs={{0,480},{32,0},{64,32},{96,64},{128,96},{160,128},{192,160},{224,1... | collective-permute-start | bytes 184328 | tf_op jit(solution)/shard_map/ppermute | solution.py:107
  38.6 1.9 collective-permute-start.4
  40.6 4.6 %collective-permute-start.5 = (bf16[80,384]{1,0:T(8,128)(2,1)S(1)}, bf16[80,384]{1,0:T(8,128)(2,1)S(1)}, u32[]{:S(2)}, u32[]{:S(2)}) collective-permute-start(bf16[80,384]{1,0:T(8,128)(2,1)S(1)} %collective-permute-done.3), channel_id=1, source_target_pairs={{0,480},{32,0},{64,32},{96,64},{128,96},{160,128},{192,160},{224,1... | collective-permute-start | bytes 184328 | tf_op jit(solution)/shard_map/ppermute | solution.py:107
  45.2 1.9 collective-permute-start.6
  47.2 4.6 %collective-permute-start.7 = (bf16[80,384]{1,0:T(8,128)(2,1)S(1)}, bf16[80,384]{1,0:T(8,128)(2,1)S(1)}, u32[]{:S(2)}, u32[]{:S(2)}) collective-permute-start(bf16[80,384]{1,0:T(8,128)(2,1)S(1)} %collective-permute-done.5), channel_id=1, source_target_pairs={{0,480},{32,0},{64,32},{96,64},{128,96},{160,128},{192,160},{224,1... | collective-permute-start | bytes 184328 | tf_op jit(solution)/shard_map/ppermute | solution.py:107
  51.8 1.9 collective-permute-start.8
  53.7 4.6 %collective-permute-start.9 = (bf16[80,384]{1,0:T(8,128)(2,1)S(1)}, bf16[80,384]{1,0:T(8,128)(2,1)S(1)}, u32[]{:S(2)}, u32[]{:S(2)}) collective-permute-start(bf16[80,384]{1,0:T(8,128)(2,1)S(1)} %collective-permute-done.7), channel_id=1, source_target_pairs={{0,480},{32,0},{64,32},{96,64},{128,96},{160,128},{192,160},{224,1... | collective-permute-start | bytes 184328 | tf_op jit(solution)/shard_map/ppermute | solution.py:107
  58.4 1.9 collective-permute-start.10
  60.3 4.6 %collective-permute-start.11 = (bf16[80,384]{1,0:T(8,128)(2,1)S(1)}, bf16[80,384]{1,0:T(8,128)(2,1)S(1)}, u32[]{:S(2)}, u32[]{:S(2)}) collective-permute-start(bf16[80,384]{1,0:T(8,128)(2,1)S(1)} %collective-permute-done.9), channel_id=1, source_target_pairs={{0,480},{32,0},{64,32},{96,64},{128,96},{160,128},{192,160},{224,1... | collective-permute-start | bytes 184328 | tf_op jit(solution)/shard_map/ppermute | solution.py:107
  65.0 1.9 collective-permute-start.12
  66.9 4.6 %collective-permute-start.13 = (bf16[80,384]{1,0:T(8,128)(2,1)S(1)}, bf16[80,384]{1,0:T(8,128)(2,1)S(1)}, u32[]{:S(2)}, u32[]{:S(2)}) collective-permute-start(bf16[80,384]{1,0:T(8,128)(2,1)S(1)} %collective-permute-done.11), channel_id=1, source_target_pairs={{0,480},{32,0},{64,32},{96,64},{128,96},{160,128},{192,160},{224,1... | collective-permute-start | bytes 184328 | tf_op jit(solution)/shard_map/ppermute | solution.py:107
  71.6 1.9 collective-permute-start.14
  73.5 4.6 %collective-permute-start.15 = (bf16[40,384]{1,0:T(8,128)(2,1)S(1)}, bf16[40,384]{1,0:T(8,128)(2,1)S(1)}, u32[]{:S(2)}, u32[]{:S(2)}) collective-permute-start(bf16[40,384]{1,0:T(8,128)(2,1)S(1)} %slice.129), channel_id=1, source_target_pairs={{0,480},{32,0},{64,32},{96,64},{128,96},{160,128},{192,160},{224,1... | collective-permute-start | bytes 92168 | tf_op jit(solution)/shard_map/ppermute | solution.py:102
  78.2 0.9 collective-permute-done.15
  79.1 4.4 %collective-permute-start.17 = (bf16[16,80,384]{2,1,0:T(8,128)(2,1)S(1)}, bf16[16,80,384]{2,1,0:T(8,128)(2,1)S(1)}, u32[]{:S(2)}, u32[]{:S(2)}) collective-permute-start(bf16[16,80,384]{2,1,0:T(8,128)(2,1)S(1)} %bitcast_dynamic-update-slice_fusion.20), channel_id=1, source_target_pairs={{0,24},{8,0},{16,8},{24,16},{1,25},{9,1},{17,9},{25,17},{2,26},{10... | collective-permute-start | bytes 2949128 | tf_op jit(solution)/shard_map/ppermute | solution.py:107
  83.5 1.9 collective-permute-start.16
  85.7 0.7 add_add_fusion
  86.4 0.5 broadcast_in_dim.137
  87.1 10.9 %collective-permute-done.17 = bf16[16,80,384]{2,1,0:T(8,128)(2,1)S(1)} collective-permute-done((bf16[16,80,384]{2,1,0:T(8,128)(2,1)S(1)}, bf16[16,80,384]{2,1,0:T(8,128)(2,1)S(1)}, u32[]{:S(2)}, u32[]{:S(2)}) %collective-permute-start.17) | collective-permute-done | bytes 983072 | tf_op jit(solution)/shard_map/ppermute | solution.py:107
  98.1 5.3 %collective-permute-start.19 = (bf16[8,80,384]{2,1,0:T(8,128)(2,1)S(1)}, bf16[8,80,384]{2,1,0:T(8,128)(2,1)S(1)}, u32[]{:S(2)}, u32[]{:S(2)}) collective-permute-start(bf16[8,80,384]{2,1,0:T(8,128)(2,1)S(1)} %slice.131), channel_id=1, source_target_pairs={{0,24},{8,0},{16,8},{24,16},{1,25},{9,1},{17,9},{25,17},{2,26},{10... | collective-permute-start | bytes 1474568 | tf_op jit(solution)/shard_map/ppermute | solution.py:102
  103.5 1.9 collective-permute-start.18
  105.9 9.5 %collective-permute-done.18 = bf16[8,80,384]{2,1,0:T(8,128)(2,1)S(1)} collective-permute-done((bf16[8,80,384]{2,1,0:T(8,128)(2,1)S(1)}, bf16[8,80,384]{2,1,0:T(8,128)(2,1)S(1)}, u32[]{:S(2)}, u32[]{:S(2)}) %collective-permute-start.18) | collective-permute-done | bytes 491552 | tf_op jit(solution)/shard_map/ppermute | solution.py:101
  115.5 2.3 %fusion.45 = (bf16[64,40,384]{2,1,0:T(8,128)(2,1)}, bf16[64,40,384]{2,1,0:T(8,128)(2,1)}) fusion(bf16[64,80,384]{2,1,0:T(8,128)(2,1)S(1)} %bitcast.139), kind=kLoop, calls=%fused_computation.127 | loop fusion | bytes 7864320 | tf_op jit(solution)/shard_map/slice | solution.py:165
  117.8 3.0 %copy.50 = bf16[512,2560]{1,0:T(8,128)(2,1)S(1)} copy(bf16[512,2560]{0,1:T(8,128)(2,1)} %all-gather.3.cloned.1.call-done) | data formatting | bytes 5242880 | tf_op jit(solution)/shard_map/all_gather | solution.py:171
  120.8 0.6 fusion
  121.4 0.5 fusion.1
  121.9 1.0 copy-done.3
  123.0 2.4 %fusion.54 = f32[8,64,384]{2,1,0:T(8,128)} fusion(bf16[8,64,2560]{2,1,0:T(8,128)(2,1)S(1)} %bitcast.144, bf16[2560,384,1]{1,0,2:T(8,128)(2,1)S(1)} %bitcast.145), kind=kOutput, calls=%fused_computation.134 | convolution fusion | flops 1006632960 | bytes 5373952 | tf_op jit(solution)/shard_map/dot_general | solution.py:175
  125.4 13.3 %all-to-all-start = ((f32[8,64,384]{2,1,0:T(8,128)}), f32[8,64,384]{2,1,0:T(8,128)S(1)}, u32[]{:S(2)}, u32[]{:S(2)}) async-start(f32[8,64,384]{2,1,0:T(8,128)} %fusion.54), calls=%async_computation | async-start | bytes 1572864 | tf_op jit(solution)/shard_map/all_to_all | solution.py:176
  138.8 0.6 gather_fusion
  139.5 11.3 %all-to-all-done = f32[8,64,384]{2,1,0:T(8,128)S(1)} async-done(((f32[8,64,384]{2,1,0:T(8,128)}), f32[8,64,384]{2,1,0:T(8,128)S(1)}, u32[]{:S(2)}, u32[]{:S(2)}) %all-to-all-start) | async-done | bytes 786464 | tf_op jit(solution)/shard_map/all_to_all | solution.py:176
  151.6 0.5 copy.52
  152.1 0.4 reshape.354
  153.0 0.3 convolution_convert_fusion.1
  153.3 1.0 fusion.14
  154.7 0.4 fusion.49
  155.1 0.5 fusion.48
  155.6 0.4 fusion.8
  156.4 0.4 fusion.51
  156.9 0.7 copy.72
  157.6 0.4 copy-done.2
  158.1 3.8 %copy.61 = bf16[64,40,384]{0,2,1:T(8,128)(2,1)} copy(bf16[64,40,384]{2,1,0:T(8,128)(2,1)S(1)} %copy-done.2) | data formatting | bytes 3932160 | tf_op jit(solution)/shard_map/slice | solution.py:165
  161.9 3.3 %slice.133 = bf16[64,12800]{0,1:T(8,128)(2,1)} slice(bf16[64,15360]{0,1:T(8,128)(2,1)} %bitcast.140), slice={[0:64], [0:12800]} | slice | bytes 3276800 | tf_op jit(solution)/shard_map/slice | solution.py:165
  165.2 7.2 %reshape.361 = bf16[64,2560,5]{0,2,1:T(8,128)(2,1)} reshape(bf16[64,12800]{0,1:T(8,128)(2,1)} %slice.133) | data formatting | bytes 3276800 | tf_op jit(solution)/shard_map/reshape | solution.py:167
  172.3 7.0 %copy.62 = bf16[2560,64,5]{0,2,1:T(8,128)(2,1)S(1)} copy(bf16[2560,64,5]{1,2,0:T(8,128)(2,1)} %bitcast.138) | data formatting | bytes 3276800 | tf_op jit(solution)/shard_map/transpose | solution.py:168
  179.4 3.1 %reshape_reshape.3 = bf16[10,256,320]{1,0,2:T(8,128)(2,1)} reshape(bf16[2560,64,5]{0,2,1:T(8,128)(2,1)S(1)} %copy.62) | data formatting | bytes 3276800 | tf_op jit(solution)/shard_map/reshape;reshape | solution.py:208
  182.5 1.6 gather_fusion.1
  184.1 0.9 broadcast_select_fusion
  185.0 1.7 all-gather.5.cloned.1.call-done
  186.7 3.0 %copy.60 = bf16[512,2560]{0,1:T(8,128)(2,1)S(1)} copy(bf16[512,2560]{1,0:T(8,128)(2,1)} %all-gather.5.cloned.1.call-done) | data formatting | bytes 5242880 | tf_op jit(solution)/shard_map/all_gather | solution.py:205
  189.8 3.2 %fusion.50 = (bf16[10,512,320]{1,2,0:T(8,128)(2,1)S(1)}, f32[10,512,320]{1,2,0:T(8,128)S(1)}) fusion(bf16[512,10,256]{0,2,1:T(8,128)(2,1)S(1)} %bitcast.141, bf16[10,256,320]{1,0,2:T(8,128)(2,1)} %reshape_reshape.3), kind=kOutput, calls=%fused_computation.132 | convolution fusion | flops 840499200 | bytes 14090240 | tf_op jit(solution)/shard_map/dot_general | solution.py:206
  192.9 1.2 fusion.15
  (100 shorter events, 5.3 us)
Async XLA Ops:
  7.2 131.6 %copy-start = (bf16[4,2,128,256]{3,2,1,0:T(8,128)(2,1)S(1)}, bf16[4,2,128,256]{3,2,1,0:T(8,128)(2,1)}, u32[]{:S(2)}) copy-start(bf16[4,2,128,256]{3,2,1,0:T(8,128)(2,1)} %param.15) | copy-start | bytes 1572868
  7.2 18.2 %copy-start.5 = (s32[8]{0:T(128)S(1)}, s32[8]{0:T(128)}, u32[]{:S(2)}) copy-start(s32[8]{0:T(128)} %param.19) | copy-start | bytes 100
  7.2 20.1 %copy-start.6 = (s32[8]{0:T(128)S(1)}, s32[8]{0:T(128)}, u32[]{:S(2)}) copy-start(s32[8]{0:T(128)} %param.18) | copy-start | bytes 100
  7.2 21.4 %copy-start.4 = (s32[8,4]{0,1:T(4,128)S(1)}, s32[8,4]{0,1:T(4,128)}, u32[]{:S(2)}) copy-start(s32[8,4]{0,1:T(4,128)} %param.16) | copy-start | bytes 388
  7.2 110.6 %all-gather.3.cloned.1.call-start = ((), (), s32[]{:S(2)}) async-start(), calls=%async_computation.1 | async-start | bytes 2949120 | tf_op jit(solution)/shard_map/all_gather | solution.py:171
  11.3 20.7 %collective-permute-start = (bf16[80,384]{1,0:T(8,128)(2,1)S(1)}, bf16[80,384]{1,0:T(8,128)(2,1)S(1)}, u32[]{:S(2)}, u32[]{:S(2)}) collective-permute-start(bf16[80,384]{1,0:T(8,128)(2,1)S(1)} %get-tuple-element.6), channel_id=1, source_target_pairs={{0,32},{32,64},{64,96},{96,128},{128,160},{160,192},{192,224},{224... | collective-permute-start | bytes 184328 | tf_op jit(solution)/shard_map/ppermute | solution.py:104
  15.7 18.3 %collective-permute-start.1 = (bf16[80,384]{1,0:T(8,128)(2,1)S(1)}, bf16[80,384]{1,0:T(8,128)(2,1)S(1)}, u32[]{:S(2)}, u32[]{:S(2)}) collective-permute-start(bf16[80,384]{1,0:T(8,128)(2,1)S(1)} %get-tuple-element.6), channel_id=1, source_target_pairs={{0,480},{32,0},{64,32},{96,64},{128,96},{160,128},{192,160},{224,1... | collective-permute-start | bytes 184328 | tf_op jit(solution)/shard_map/ppermute | solution.py:107
  32.1 6.6 %collective-permute-start.2 = (bf16[80,384]{1,0:T(8,128)(2,1)S(1)}, bf16[80,384]{1,0:T(8,128)(2,1)S(1)}, u32[]{:S(2)}, u32[]{:S(2)}) collective-permute-start(bf16[80,384]{1,0:T(8,128)(2,1)S(1)} %collective-permute-done), channel_id=1, source_target_pairs={{0,32},{32,64},{64,96},{96,128},{128,160},{160,192},{192,224},{224... | collective-permute-start | bytes 184328 | tf_op jit(solution)/shard_map/ppermute | solution.py:104
  34.0 6.6 %collective-permute-start.3 = (bf16[80,384]{1,0:T(8,128)(2,1)S(1)}, bf16[80,384]{1,0:T(8,128)(2,1)S(1)}, u32[]{:S(2)}, u32[]{:S(2)}) collective-permute-start(bf16[80,384]{1,0:T(8,128)(2,1)S(1)} %collective-permute-done.1), channel_id=1, source_target_pairs={{0,480},{32,0},{64,32},{96,64},{128,96},{160,128},{192,160},{224,1... | collective-permute-start | bytes 184328 | tf_op jit(solution)/shard_map/ppermute | solution.py:107
  38.6 6.6 %collective-permute-start.4 = (bf16[80,384]{1,0:T(8,128)(2,1)S(1)}, bf16[80,384]{1,0:T(8,128)(2,1)S(1)}, u32[]{:S(2)}, u32[]{:S(2)}) collective-permute-start(bf16[80,384]{1,0:T(8,128)(2,1)S(1)} %collective-permute-done.2), channel_id=1, source_target_pairs={{0,32},{32,64},{64,96},{96,128},{128,160},{160,192},{192,224},{224... | collective-permute-start | bytes 184328 | tf_op jit(solution)/shard_map/ppermute | solution.py:104
  40.6 6.6 %collective-permute-start.5 = (bf16[80,384]{1,0:T(8,128)(2,1)S(1)}, bf16[80,384]{1,0:T(8,128)(2,1)S(1)}, u32[]{:S(2)}, u32[]{:S(2)}) collective-permute-start(bf16[80,384]{1,0:T(8,128)(2,1)S(1)} %collective-permute-done.3), channel_id=1, source_target_pairs={{0,480},{32,0},{64,32},{96,64},{128,96},{160,128},{192,160},{224,1... | collective-permute-start | bytes 184328 | tf_op jit(solution)/shard_map/ppermute | solution.py:107
  45.2 6.6 %collective-permute-start.6 = (bf16[80,384]{1,0:T(8,128)(2,1)S(1)}, bf16[80,384]{1,0:T(8,128)(2,1)S(1)}, u32[]{:S(2)}, u32[]{:S(2)}) collective-permute-start(bf16[80,384]{1,0:T(8,128)(2,1)S(1)} %collective-permute-done.4), channel_id=1, source_target_pairs={{0,32},{32,64},{64,96},{96,128},{128,160},{160,192},{192,224},{224... | collective-permute-start | bytes 184328 | tf_op jit(solution)/shard_map/ppermute | solution.py:104
  47.2 6.6 %collective-permute-start.7 = (bf16[80,384]{1,0:T(8,128)(2,1)S(1)}, bf16[80,384]{1,0:T(8,128)(2,1)S(1)}, u32[]{:S(2)}, u32[]{:S(2)}) collective-permute-start(bf16[80,384]{1,0:T(8,128)(2,1)S(1)} %collective-permute-done.5), channel_id=1, source_target_pairs={{0,480},{32,0},{64,32},{96,64},{128,96},{160,128},{192,160},{224,1... | collective-permute-start | bytes 184328 | tf_op jit(solution)/shard_map/ppermute | solution.py:107
  51.8 6.6 %collective-permute-start.8 = (bf16[80,384]{1,0:T(8,128)(2,1)S(1)}, bf16[80,384]{1,0:T(8,128)(2,1)S(1)}, u32[]{:S(2)}, u32[]{:S(2)}) collective-permute-start(bf16[80,384]{1,0:T(8,128)(2,1)S(1)} %collective-permute-done.6), channel_id=1, source_target_pairs={{0,32},{32,64},{64,96},{96,128},{128,160},{160,192},{192,224},{224... | collective-permute-start | bytes 184328 | tf_op jit(solution)/shard_map/ppermute | solution.py:104
  53.7 6.6 %collective-permute-start.9 = (bf16[80,384]{1,0:T(8,128)(2,1)S(1)}, bf16[80,384]{1,0:T(8,128)(2,1)S(1)}, u32[]{:S(2)}, u32[]{:S(2)}) collective-permute-start(bf16[80,384]{1,0:T(8,128)(2,1)S(1)} %collective-permute-done.7), channel_id=1, source_target_pairs={{0,480},{32,0},{64,32},{96,64},{128,96},{160,128},{192,160},{224,1... | collective-permute-start | bytes 184328 | tf_op jit(solution)/shard_map/ppermute | solution.py:107
  58.4 6.6 %collective-permute-start.10 = (bf16[80,384]{1,0:T(8,128)(2,1)S(1)}, bf16[80,384]{1,0:T(8,128)(2,1)S(1)}, u32[]{:S(2)}, u32[]{:S(2)}) collective-permute-start(bf16[80,384]{1,0:T(8,128)(2,1)S(1)} %collective-permute-done.8), channel_id=1, source_target_pairs={{0,32},{32,64},{64,96},{96,128},{128,160},{160,192},{192,224},{224... | collective-permute-start | bytes 184328 | tf_op jit(solution)/shard_map/ppermute | solution.py:104
  60.3 6.6 %collective-permute-start.11 = (bf16[80,384]{1,0:T(8,128)(2,1)S(1)}, bf16[80,384]{1,0:T(8,128)(2,1)S(1)}, u32[]{:S(2)}, u32[]{:S(2)}) collective-permute-start(bf16[80,384]{1,0:T(8,128)(2,1)S(1)} %collective-permute-done.9), channel_id=1, source_target_pairs={{0,480},{32,0},{64,32},{96,64},{128,96},{160,128},{192,160},{224,1... | collective-permute-start | bytes 184328 | tf_op jit(solution)/shard_map/ppermute | solution.py:107
  65.0 6.6 %collective-permute-start.12 = (bf16[80,384]{1,0:T(8,128)(2,1)S(1)}, bf16[80,384]{1,0:T(8,128)(2,1)S(1)}, u32[]{:S(2)}, u32[]{:S(2)}) collective-permute-start(bf16[80,384]{1,0:T(8,128)(2,1)S(1)} %collective-permute-done.10), channel_id=1, source_target_pairs={{0,32},{32,64},{64,96},{96,128},{128,160},{160,192},{192,224},{224... | collective-permute-start | bytes 184328 | tf_op jit(solution)/shard_map/ppermute | solution.py:104
  66.9 6.6 %collective-permute-start.13 = (bf16[80,384]{1,0:T(8,128)(2,1)S(1)}, bf16[80,384]{1,0:T(8,128)(2,1)S(1)}, u32[]{:S(2)}, u32[]{:S(2)}) collective-permute-start(bf16[80,384]{1,0:T(8,128)(2,1)S(1)} %collective-permute-done.11), channel_id=1, source_target_pairs={{0,480},{32,0},{64,32},{96,64},{128,96},{160,128},{192,160},{224,1... | collective-permute-start | bytes 184328 | tf_op jit(solution)/shard_map/ppermute | solution.py:107
  71.6 6.6 %collective-permute-start.14 = (bf16[40,384]{1,0:T(8,128)(2,1)S(1)}, bf16[40,384]{1,0:T(8,128)(2,1)S(1)}, u32[]{:S(2)}, u32[]{:S(2)}) collective-permute-start(bf16[40,384]{1,0:T(8,128)(2,1)S(1)} %slice.128), channel_id=1, source_target_pairs={{0,32},{32,64},{64,96},{96,128},{128,160},{160,192},{192,224},{224... | collective-permute-start | bytes 92168 | tf_op jit(solution)/shard_map/ppermute | solution.py:101
  73.5 5.6 %collective-permute-start.15 = (bf16[40,384]{1,0:T(8,128)(2,1)S(1)}, bf16[40,384]{1,0:T(8,128)(2,1)S(1)}, u32[]{:S(2)}, u32[]{:S(2)}) collective-permute-start(bf16[40,384]{1,0:T(8,128)(2,1)S(1)} %slice.129), channel_id=1, source_target_pairs={{0,480},{32,0},{64,32},{96,64},{128,96},{160,128},{192,160},{224,1... | collective-permute-start | bytes 92168 | tf_op jit(solution)/shard_map/ppermute | solution.py:102
  79.1 19.0 %collective-permute-start.17 = (bf16[16,80,384]{2,1,0:T(8,128)(2,1)S(1)}, bf16[16,80,384]{2,1,0:T(8,128)(2,1)S(1)}, u32[]{:S(2)}, u32[]{:S(2)}) collective-permute-start(bf16[16,80,384]{2,1,0:T(8,128)(2,1)S(1)} %bitcast_dynamic-update-slice_fusion.20), channel_id=1, source_target_pairs={{0,24},{8,0},{16,8},{24,16},{1,25},{9,1},{17,9},{25,17},{2,26},{10... | collective-permute-start | bytes 2949128 | tf_op jit(solution)/shard_map/ppermute | solution.py:107
  83.5 20.0 %collective-permute-start.16 = (bf16[16,80,384]{2,1,0:T(8,128)(2,1)S(1)}, bf16[16,80,384]{2,1,0:T(8,128)(2,1)S(1)}, u32[]{:S(2)}, u32[]{:S(2)}) collective-permute-start(bf16[16,80,384]{2,1,0:T(8,128)(2,1)S(1)} %bitcast_dynamic-update-slice_fusion.20), channel_id=1, source_target_pairs={{0,8},{8,16},{16,24},{24,0},{1,9},{9,17},{17,25},{25,1},{2,10},{10... | collective-permute-start | bytes 2949128 | tf_op jit(solution)/shard_map/ppermute | solution.py:104
  98.1 17.3 %collective-permute-start.19 = (bf16[8,80,384]{2,1,0:T(8,128)(2,1)S(1)}, bf16[8,80,384]{2,1,0:T(8,128)(2,1)S(1)}, u32[]{:S(2)}, u32[]{:S(2)}) collective-permute-start(bf16[8,80,384]{2,1,0:T(8,128)(2,1)S(1)} %slice.131), channel_id=1, source_target_pairs={{0,24},{8,0},{16,8},{24,16},{1,25},{9,1},{17,9},{25,17},{2,26},{10... | collective-permute-start | bytes 1474568 | tf_op jit(solution)/shard_map/ppermute | solution.py:102
  103.5 11.8 %collective-permute-start.18 = (bf16[8,80,384]{2,1,0:T(8,128)(2,1)S(1)}, bf16[8,80,384]{2,1,0:T(8,128)(2,1)S(1)}, u32[]{:S(2)}, u32[]{:S(2)}) collective-permute-start(bf16[8,80,384]{2,1,0:T(8,128)(2,1)S(1)} %slice.130), channel_id=1, source_target_pairs={{0,8},{8,16},{16,24},{24,0},{1,9},{9,17},{17,25},{25,1},{2,10},{10... | collective-permute-start | bytes 1474568 | tf_op jit(solution)/shard_map/ppermute | solution.py:101
  121.4 1.6 copy-start.3
  125.4 25.5 %all-to-all-start = ((f32[8,64,384]{2,1,0:T(8,128)}), f32[8,64,384]{2,1,0:T(8,128)S(1)}, u32[]{:S(2)}, u32[]{:S(2)}) async-start(f32[8,64,384]{2,1,0:T(8,128)} %fusion.54), calls=%async_computation | async-start | bytes 1572864 | tf_op jit(solution)/shard_map/all_to_all | solution.py:176
  138.7 48.1 %all-gather.5.cloned.1.call-start = ((), (), s32[]{:S(2)}) async-start(), calls=%async_computation.2 | async-start | bytes 2949120 | tf_op jit(solution)/shard_map/all_gather | solution.py:205
  156.4 1.7 copy-start.2
  189.7 4.4 %copy-start.1 = (bf16[4,2,128,256]{3,2,1,0:T(8,128)(2,1)S(1)}, bf16[4,2,128,256]{3,2,1,0:T(8,128)(2,1)}, u32[]{:S(2)}) copy-start(bf16[4,2,128,256]{3,2,1,0:T(8,128)(2,1)} %param.15) | copy-start | bytes 1572868
Sparse Core Ops, SparseCore 0:
  25.3 32.5 all-gather.2
  157.7 28.9 all-gather.4

commit v4 on v3

--- a/solution.py
+++ b/solution.py
@@ -60,10 +60,10 @@
     cache_weights = (cache_weights / denominator).astype(jnp.bfloat16)
     tree_weights = (tree_weights / denominator).astype(jnp.bfloat16)
     result = jnp.einsum(
-        "rhnc,rcd->rnhd", cache_weights, cache_values, preferred_element_type=jnp.float32
+        "rhnc,rcd->rhnd", cache_weights, cache_values, preferred_element_type=jnp.float32
     )
     result = result + jnp.einsum(
-        "rhnm,rmd->rnhd", tree_weights, tree_values, preferred_element_type=jnp.float32
+        "rhnm,rmd->rhnd", tree_weights, tree_values, preferred_element_type=jnp.float32
     )
     return result.astype(jnp.bfloat16)
 
@@ -202,11 +202,11 @@
         position[None],
         reach[None],
     )
-    mixed = lax.all_gather(result.reshape(DRAFT, HQ * HD), "head", axis=0, tiled=True)
+    mixed = lax.all_gather(result[0], "head", axis=1, tiled=True)
     per_head = lax.dot_general(
-        mixed.reshape(mixed.shape[0], HQ, HD),
+        mixed,
         wo_cols.reshape(HQ, HD, wo_cols.shape[1]),
-        (((2,), (1,)), ((1,), (0,))),
+        (((2,), (1,)), ((0,), (0,))),
         preferred_element_type=jnp.float32,
     )
     summed = None

time: 202 us -> 200 us (0.990)
  local copies, waits for them, and re-layouts: 46.4 us -> 42.6 us
    all_gather x1 -> x0, local copies, waits for them, and re-layouts: 2.99 us -> none  [shards(): lax.all_gather(result.reshape(DRAFT, HQ * HD), 'head', axis=0, tiled=True)]
  transfers between devices with their start and end apart: 23 -> 23, of which waited for: 5 -> 5; matrix products, arithmetic and copies ran while one was open for 18% -> 19% of each run, Pallas kernels for 0% -> 0%
where the time goes in v4:
time: 200 us; the launch traced here: 199 us
  starting transfers between devices  86.2 us (43%)
  local copies, waits for them, and re-layouts  42.6 us (21%)
  waiting for transfers between devices  34.5 us (17%)
  between operations  17.2 us (9%)
  matrix products  10.5 us (5%)
  other arithmetic  7.76 us (4%)
    ppermute x8, starting transfers between devices, ring_pieces(): behind = lax.ppermute(behind, axis, backward)  41.3 us
    ppermute x8, starting transfers between devices, ring_pieces(): ahead = lax.ppermute(ahead, axis, forward)  17.8 us
    all_to_all x1, starting transfers between devices, shards(): mine = lax.all_to_all(both, 'head', 0, 1, tiled=True)  13.3 us
    ppermute x8, waiting for transfers between devices, ring_pieces(): behind = lax.ppermute(behind, axis, backward)  11.6 us
    all_to_all x1, waiting for transfers between devices, shards(): mine = lax.all_to_all(both, 'head', 0, 1, tiled=True)  10.7 us
    ppermute x2, starting transfers between devices, ring_pieces(): got.append((step, half, lax.ppermute(behind[half:], axis, backward)))  9.89 us
    ppermute x2, waiting for transfers between devices, ring_pieces(): got.append((step, 0, lax.ppermute(ahead[:half], axis, forward)))  9.46 us
    slice x3, local copies, waits for them, and re-layouts, shards(): stacked[:, part_rows:].reshape(tok_count, -1)[:, :wo_flat.shape[0]]  9.38 us
  transfers between devices with their start and end apart: 23, of which 5 were waited for; matrix products, arithmetic and copies ran while one was open for 19% of the time, Pallas kernels for 0%

profile of v4, /device:TPU:1, one launch (start us, length us, event | category | flops | bytes accessed | tf_op | source)
XLA Modules:
  0.0 198.7 jit_solution(2662571134446232722)
XLA Ops:
  7.3 1.2 copy.43
  8.5 1.0 reshape.344
  9.5 0.8 constant_dynamic-slice_fusion.1
  10.3 0.9 constant_dynamic-slice_fusion.2
  11.3 4.4 %collective-permute-start = (bf16[80,384]{1,0:T(8,128)(2,1)S(1)}, bf16[80,384]{1,0:T(8,128)(2,1)S(1)}, u32[]{:S(2)}, u32[]{:S(2)}) collective-permute-start(bf16[80,384]{1,0:T(8,128)(2,1)S(1)} %get-tuple-element.6), channel_id=1, source_target_pairs={{0,32},{32,64},{64,96},{96,128},{128,160},{160,192},{192,224},{224... | collective-permute-start | bytes 184328 | tf_op jit(solution)/shard_map/ppermute | solution.py:104
  15.7 9.5 %collective-permute-start.1 = (bf16[80,384]{1,0:T(8,128)(2,1)S(1)}, bf16[80,384]{1,0:T(8,128)(2,1)S(1)}, u32[]{:S(2)}, u32[]{:S(2)}) collective-permute-start(bf16[80,384]{1,0:T(8,128)(2,1)S(1)} %get-tuple-element.6), channel_id=1, source_target_pairs={{0,480},{32,0},{64,32},{96,64},{128,96},{160,128},{192,160},{224,1... | collective-permute-start | bytes 184328 | tf_op jit(solution)/shard_map/ppermute | solution.py:107
  25.4 0.6 dynamic_slice.29
  27.3 0.6 dynamic_slice.24
  27.9 0.7 fusion.38
  28.9 0.6 iota_subtract_fusion
  31.4 0.7 iota_compare_fusion.6
  32.1 1.9 collective-permute-start.2
  34.0 4.6 %collective-permute-start.3 = (bf16[80,384]{1,0:T(8,128)(2,1)S(1)}, bf16[80,384]{1,0:T(8,128)(2,1)S(1)}, u32[]{:S(2)}, u32[]{:S(2)}) collective-permute-start(bf16[80,384]{1,0:T(8,128)(2,1)S(1)} %collective-permute-done.1), channel_id=1, source_target_pairs={{0,480},{32,0},{64,32},{96,64},{128,96},{160,128},{192,160},{224,1... | collective-permute-start | bytes 184328 | tf_op jit(solution)/shard_map/ppermute | solution.py:107
  38.6 1.9 collective-permute-start.4
  40.6 4.6 %collective-permute-start.5 = (bf16[80,384]{1,0:T(8,128)(2,1)S(1)}, bf16[80,384]{1,0:T(8,128)(2,1)S(1)}, u32[]{:S(2)}, u32[]{:S(2)}) collective-permute-start(bf16[80,384]{1,0:T(8,128)(2,1)S(1)} %collective-permute-done.3), channel_id=1, source_target_pairs={{0,480},{32,0},{64,32},{96,64},{128,96},{160,128},{192,160},{224,1... | collective-permute-start | bytes 184328 | tf_op jit(solution)/shard_map/ppermute | solution.py:107
  45.2 1.9 collective-permute-start.6
  47.2 4.6 %collective-permute-start.7 = (bf16[80,384]{1,0:T(8,128)(2,1)S(1)}, bf16[80,384]{1,0:T(8,128)(2,1)S(1)}, u32[]{:S(2)}, u32[]{:S(2)}) collective-permute-start(bf16[80,384]{1,0:T(8,128)(2,1)S(1)} %collective-permute-done.5), channel_id=1, source_target_pairs={{0,480},{32,0},{64,32},{96,64},{128,96},{160,128},{192,160},{224,1... | collective-permute-start | bytes 184328 | tf_op jit(solution)/shard_map/ppermute | solution.py:107
  51.8 1.9 collective-permute-start.8
  53.7 4.6 %collective-permute-start.9 = (bf16[80,384]{1,0:T(8,128)(2,1)S(1)}, bf16[80,384]{1,0:T(8,128)(2,1)S(1)}, u32[]{:S(2)}, u32[]{:S(2)}) collective-permute-start(bf16[80,384]{1,0:T(8,128)(2,1)S(1)} %collective-permute-done.7), channel_id=1, source_target_pairs={{0,480},{32,0},{64,32},{96,64},{128,96},{160,128},{192,160},{224,1... | collective-permute-start | bytes 184328 | tf_op jit(solution)/shard_map/ppermute | solution.py:107
  58.4 1.9 collective-permute-start.10
  60.3 4.6 %collective-permute-start.11 = (bf16[80,384]{1,0:T(8,128)(2,1)S(1)}, bf16[80,384]{1,0:T(8,128)(2,1)S(1)}, u32[]{:S(2)}, u32[]{:S(2)}) collective-permute-start(bf16[80,384]{1,0:T(8,128)(2,1)S(1)} %collective-permute-done.9), channel_id=1, source_target_pairs={{0,480},{32,0},{64,32},{96,64},{128,96},{160,128},{192,160},{224,1... | collective-permute-start | bytes 184328 | tf_op jit(solution)/shard_map/ppermute | solution.py:107
  65.0 1.9 collective-permute-start.12
  66.9 4.6 %collective-permute-start.13 = (bf16[80,384]{1,0:T(8,128)(2,1)S(1)}, bf16[80,384]{1,0:T(8,128)(2,1)S(1)}, u32[]{:S(2)}, u32[]{:S(2)}) collective-permute-start(bf16[80,384]{1,0:T(8,128)(2,1)S(1)} %collective-permute-done.11), channel_id=1, source_target_pairs={{0,480},{32,0},{64,32},{96,64},{128,96},{160,128},{192,160},{224,1... | collective-permute-start | bytes 184328 | tf_op jit(solution)/shard_map/ppermute | solution.py:107
  71.6 1.9 collective-permute-start.14
  73.5 4.6 %collective-permute-start.15 = (bf16[40,384]{1,0:T(8,128)(2,1)S(1)}, bf16[40,384]{1,0:T(8,128)(2,1)S(1)}, u32[]{:S(2)}, u32[]{:S(2)}) collective-permute-start(bf16[40,384]{1,0:T(8,128)(2,1)S(1)} %slice.130), channel_id=1, source_target_pairs={{0,480},{32,0},{64,32},{96,64},{128,96},{160,128},{192,160},{224,1... | collective-permute-start | bytes 92168 | tf_op jit(solution)/shard_map/ppermute | solution.py:102
  78.2 0.9 collective-permute-done.15
  79.1 4.4 %collective-permute-start.17 = (bf16[16,80,384]{2,1,0:T(8,128)(2,1)S(1)}, bf16[16,80,384]{2,1,0:T(8,128)(2,1)S(1)}, u32[]{:S(2)}, u32[]{:S(2)}) collective-permute-start(bf16[16,80,384]{2,1,0:T(8,128)(2,1)S(1)} %bitcast_dynamic-update-slice_fusion.20), channel_id=1, source_target_pairs={{0,24},{8,0},{16,8},{24,16},{1,25},{9,1},{17,9},{25,17},{2,26},{10... | collective-permute-start | bytes 2949128 | tf_op jit(solution)/shard_map/ppermute | solution.py:107
  83.5 1.9 collective-permute-start.16
  85.8 0.5 broadcast_in_dim.137
  86.5 11.6 %collective-permute-done.17 = bf16[16,80,384]{2,1,0:T(8,128)(2,1)S(1)} collective-permute-done((bf16[16,80,384]{2,1,0:T(8,128)(2,1)S(1)}, bf16[16,80,384]{2,1,0:T(8,128)(2,1)S(1)}, u32[]{:S(2)}, u32[]{:S(2)}) %collective-permute-start.17) | collective-permute-done | bytes 983072 | tf_op jit(solution)/shard_map/ppermute | solution.py:107
  98.1 5.3 %collective-permute-start.19 = (bf16[8,80,384]{2,1,0:T(8,128)(2,1)S(1)}, bf16[8,80,384]{2,1,0:T(8,128)(2,1)S(1)}, u32[]{:S(2)}, u32[]{:S(2)}) collective-permute-start(bf16[8,80,384]{2,1,0:T(8,128)(2,1)S(1)} %slice.132), channel_id=1, source_target_pairs={{0,24},{8,0},{16,8},{24,16},{1,25},{9,1},{17,9},{25,17},{2,26},{10... | collective-permute-start | bytes 1474568 | tf_op jit(solution)/shard_map/ppermute | solution.py:102
  103.5 1.9 collective-permute-start.18
  105.9 9.5 %collective-permute-done.18 = bf16[8,80,384]{2,1,0:T(8,128)(2,1)S(1)} collective-permute-done((bf16[8,80,384]{2,1,0:T(8,128)(2,1)S(1)}, bf16[8,80,384]{2,1,0:T(8,128)(2,1)S(1)}, u32[]{:S(2)}, u32[]{:S(2)}) %collective-permute-start.18) | collective-permute-done | bytes 491552 | tf_op jit(solution)/shard_map/ppermute | solution.py:101
  115.5 2.3 %fusion.44 = (bf16[64,40,384]{2,1,0:T(8,128)(2,1)}, bf16[64,40,384]{2,1,0:T(8,128)(2,1)}) fusion(bf16[64,80,384]{2,1,0:T(8,128)(2,1)S(1)} %bitcast.125), kind=kLoop, calls=%fused_computation.126 | loop fusion | bytes 7864320 | tf_op jit(solution)/shard_map/slice | solution.py:165
  117.8 3.0 %copy.42 = bf16[512,2560]{1,0:T(8,128)(2,1)S(1)} copy(bf16[512,2560]{0,1:T(8,128)(2,1)} %all-gather.3.cloned.1.call-done) | data formatting | bytes 5242880 | tf_op jit(solution)/shard_map/all_gather | solution.py:171
  120.8 0.6 fusion
  121.4 0.5 fusion.1
  121.9 1.0 copy-done.3
  123.0 2.4 %fusion.50 = f32[8,64,384]{2,1,0:T(8,128)} fusion(bf16[8,64,2560]{2,1,0:T(8,128)(2,1)S(1)} %bitcast.129, bf16[2560,384,1]{1,0,2:T(8,128)(2,1)S(1)} %bitcast.130), kind=kOutput, calls=%fused_computation.132 | convolution fusion | flops 1006632960 | bytes 5373952 | tf_op jit(solution)/shard_map/dot_general | solution.py:175
  125.4 13.3 %all-to-all-start = ((f32[8,64,384]{2,1,0:T(8,128)}), f32[8,64,384]{2,1,0:T(8,128)S(1)}, u32[]{:S(2)}, u32[]{:S(2)}) async-start(f32[8,64,384]{2,1,0:T(8,128)} %fusion.50), calls=%async_computation | async-start | bytes 1572864 | tf_op jit(solution)/shard_map/all_to_all | solution.py:176
  138.8 0.6 gather_fusion
  139.4 0.7 add_add_fusion
  140.2 10.7 %all-to-all-done = f32[8,64,384]{2,1,0:T(8,128)S(1)} async-done(((f32[8,64,384]{2,1,0:T(8,128)}), f32[8,64,384]{2,1,0:T(8,128)S(1)}, u32[]{:S(2)}, u32[]{:S(2)}) %all-to-all-start) | async-done | bytes 786464 | tf_op jit(solution)/shard_map/all_to_all | solution.py:176
  151.3 0.3 convolution_convert_fusion
  151.6 0.5 copy.44
  152.1 0.4 reshape.348
  153.0 0.3 convolution_convert_fusion.1
  153.3 1.0 fusion.13
  154.6 0.4 fusion.48
  155.1 0.5 fusion.47
  155.6 0.4 fusion.7
  156.1 0.3 fusion.16
  156.4 1.2 fusion.5
  157.6 0.4 copy-done.2
  158.0 3.8 %copy.51 = bf16[64,40,384]{0,2,1:T(8,128)(2,1)} copy(bf16[64,40,384]{2,1,0:T(8,128)(2,1)S(1)} %copy-done.2) | data formatting | bytes 3932160 | tf_op jit(solution)/shard_map/slice | solution.py:165
  161.8 3.3 %slice.145 = bf16[64,12800]{0,1:T(8,128)(2,1)} slice(bf16[64,15360]{0,1:T(8,128)(2,1)} %bitcast.126), slice={[0:64], [0:12800]} | slice | bytes 3276800 | tf_op jit(solution)/shard_map/slice | solution.py:165
  165.1 7.1 %reshape.354 = bf16[64,2560,5]{0,2,1:T(8,128)(2,1)} reshape(bf16[64,12800]{0,1:T(8,128)(2,1)} %slice.145) | data formatting | bytes 3276800 | tf_op jit(solution)/shard_map/reshape | solution.py:167
  172.2 7.0 %copy.52 = bf16[2560,64,5]{0,2,1:T(8,128)(2,1)S(1)} copy(bf16[2560,64,5]{1,2,0:T(8,128)(2,1)} %bitcast.124) | data formatting | bytes 3276800 | tf_op jit(solution)/shard_map/transpose | solution.py:168
  179.3 3.1 %reshape_reshape.3 = bf16[10,256,320]{1,0,2:T(8,128)(2,1)} reshape(bf16[2560,64,5]{0,2,1:T(8,128)(2,1)S(1)} %copy.52) | data formatting | bytes 3276800 | tf_op jit(solution)/shard_map/reshape;reshape | solution.py:208
  182.3 1.6 gather_fusion.1
  184.0 0.9 broadcast_select_fusion
  184.9 1.8 all-gather.5.cloned.1.call-done
  186.7 4.0 %fusion.49 = (bf16[10,512,320]{1,2,0:T(8,128)(2,1)S(1)}, f32[10,512,320]{1,2,0:T(8,128)S(1)}) fusion(bf16[10,512,256]{2,1,0:T(8,128)(2,1)} %all-gather.5.cloned.1.call-done, bf16[10,256,320]{1,0,2:T(8,128)(2,1)} %reshape_reshape.3), kind=kOutput, calls=%fused_computation.131 | convolution fusion | flops 840499200 | bytes 14090240 | tf_op jit(solution)/shard_map/dot_general | solution.py:206
  190.7 1.2 fusion.14
  (99 shorter events, 4.6 us)
Async XLA Ops:
  7.2 131.6 %copy-start = (bf16[4,2,128,256]{3,2,1,0:T(8,128)(2,1)S(1)}, bf16[4,2,128,256]{3,2,1,0:T(8,128)(2,1)}, u32[]{:S(2)}) copy-start(bf16[4,2,128,256]{3,2,1,0:T(8,128)(2,1)} %param.15) | copy-start | bytes 1572868
  7.2 18.2 %copy-start.5 = (s32[8]{0:T(128)S(1)}, s32[8]{0:T(128)}, u32[]{:S(2)}) copy-start(s32[8]{0:T(128)} %param.19) | copy-start | bytes 100
  7.2 20.1 %copy-start.6 = (s32[8]{0:T(128)S(1)}, s32[8]{0:T(128)}, u32[]{:S(2)}) copy-start(s32[8]{0:T(128)} %param.18) | copy-start | bytes 100
  7.2 21.4 %copy-start.4 = (s32[8,4]{0,1:T(4,128)S(1)}, s32[8,4]{0,1:T(4,128)}, u32[]{:S(2)}) copy-start(s32[8,4]{0,1:T(4,128)} %param.16) | copy-start | bytes 388
  7.2 110.6 %all-gather.3.cloned.1.call-start = ((), (), s32[]{:S(2)}) async-start(), calls=%async_computation.1 | async-start | bytes 2949120 | tf_op jit(solution)/shard_map/all_gather | solution.py:171
  11.3 20.7 %collective-permute-start = (bf16[80,384]{1,0:T(8,128)(2,1)S(1)}, bf16[80,384]{1,0:T(8,128)(2,1)S(1)}, u32[]{:S(2)}, u32[]{:S(2)}) collective-permute-start(bf16[80,384]{1,0:T(8,128)(2,1)S(1)} %get-tuple-element.6), channel_id=1, source_target_pairs={{0,32},{32,64},{64,96},{96,128},{128,160},{160,192},{192,224},{224... | collective-permute-start | bytes 184328 | tf_op jit(solution)/shard_map/ppermute | solution.py:104
  15.7 18.3 %collective-permute-start.1 = (bf16[80,384]{1,0:T(8,128)(2,1)S(1)}, bf16[80,384]{1,0:T(8,128)(2,1)S(1)}, u32[]{:S(2)}, u32[]{:S(2)}) collective-permute-start(bf16[80,384]{1,0:T(8,128)(2,1)S(1)} %get-tuple-element.6), channel_id=1, source_target_pairs={{0,480},{32,0},{64,32},{96,64},{128,96},{160,128},{192,160},{224,1... | collective-permute-start | bytes 184328 | tf_op jit(solution)/shard_map/ppermute | solution.py:107
  32.1 6.6 %collective-permute-start.2 = (bf16[80,384]{1,0:T(8,128)(2,1)S(1)}, bf16[80,384]{1,0:T(8,128)(2,1)S(1)}, u32[]{:S(2)}, u32[]{:S(2)}) collective-permute-start(bf16[80,384]{1,0:T(8,128)(2,1)S(1)} %collective-permute-done), channel_id=1, source_target_pairs={{0,32},{32,64},{64,96},{96,128},{128,160},{160,192},{192,224},{224... | collective-permute-start | bytes 184328 | tf_op jit(solution)/shard_map/ppermute | solution.py:104
  34.0 6.6 %collective-permute-start.3 = (bf16[80,384]{1,0:T(8,128)(2,1)S(1)}, bf16[80,384]{1,0:T(8,128)(2,1)S(1)}, u32[]{:S(2)}, u32[]{:S(2)}) collective-permute-start(bf16[80,384]{1,0:T(8,128)(2,1)S(1)} %collective-permute-done.1), channel_id=1, source_target_pairs={{0,480},{32,0},{64,32},{96,64},{128,96},{160,128},{192,160},{224,1... | collective-permute-start | bytes 184328 | tf_op jit(solution)/shard_map/ppermute | solution.py:107
  38.6 6.6 %collective-permute-start.4 = (bf16[80,384]{1,0:T(8,128)(2,1)S(1)}, bf16[80,384]{1,0:T(8,128)(2,1)S(1)}, u32[]{:S(2)}, u32[]{:S(2)}) collective-permute-start(bf16[80,384]{1,0:T(8,128)(2,1)S(1)} %collective-permute-done.2), channel_id=1, source_target_pairs={{0,32},{32,64},{64,96},{96,128},{128,160},{160,192},{192,224},{224... | collective-permute-start | bytes 184328 | tf_op jit(solution)/shard_map/ppermute | solution.py:104
  40.6 6.6 %collective-permute-start.5 = (bf16[80,384]{1,0:T(8,128)(2,1)S(1)}, bf16[80,384]{1,0:T(8,128)(2,1)S(1)}, u32[]{:S(2)}, u32[]{:S(2)}) collective-permute-start(bf16[80,384]{1,0:T(8,128)(2,1)S(1)} %collective-permute-done.3), channel_id=1, source_target_pairs={{0,480},{32,0},{64,32},{96,64},{128,96},{160,128},{192,160},{224,1... | collective-permute-start | bytes 184328 | tf_op jit(solution)/shard_map/ppermute | solution.py:107
  45.2 6.6 %collective-permute-start.6 = (bf16[80,384]{1,0:T(8,128)(2,1)S(1)}, bf16[80,384]{1,0:T(8,128)(2,1)S(1)}, u32[]{:S(2)}, u32[]{:S(2)}) collective-permute-start(bf16[80,384]{1,0:T(8,128)(2,1)S(1)} %collective-permute-done.4), channel_id=1, source_target_pairs={{0,32},{32,64},{64,96},{96,128},{128,160},{160,192},{192,224},{224... | collective-permute-start | bytes 184328 | tf_op jit(solution)/shard_map/ppermute | solution.py:104
  47.2 6.6 %collective-permute-start.7 = (bf16[80,384]{1,0:T(8,128)(2,1)S(1)}, bf16[80,384]{1,0:T(8,128)(2,1)S(1)}, u32[]{:S(2)}, u32[]{:S(2)}) collective-permute-start(bf16[80,384]{1,0:T(8,128)(2,1)S(1)} %collective-permute-done.5), channel_id=1, source_target_pairs={{0,480},{32,0},{64,32},{96,64},{128,96},{160,128},{192,160},{224,1... | collective-permute-start | bytes 184328 | tf_op jit(solution)/shard_map/ppermute | solution.py:107
  51.8 6.6 %collective-permute-start.8 = (bf16[80,384]{1,0:T(8,128)(2,1)S(1)}, bf16[80,384]{1,0:T(8,128)(2,1)S(1)}, u32[]{:S(2)}, u32[]{:S(2)}) collective-permute-start(bf16[80,384]{1,0:T(8,128)(2,1)S(1)} %collective-permute-done.6), channel_id=1, source_target_pairs={{0,32},{32,64},{64,96},{96,128},{128,160},{160,192},{192,224},{224... | collective-permute-start | bytes 184328 | tf_op jit(solution)/shard_map/ppermute | solution.py:104
  53.7 6.6 %collective-permute-start.9 = (bf16[80,384]{1,0:T(8,128)(2,1)S(1)}, bf16[80,384]{1,0:T(8,128)(2,1)S(1)}, u32[]{:S(2)}, u32[]{:S(2)}) collective-permute-start(bf16[80,384]{1,0:T(8,128)(2,1)S(1)} %collective-permute-done.7), channel_id=1, source_target_pairs={{0,480},{32,0},{64,32},{96,64},{128,96},{160,128},{192,160},{224,1... | collective-permute-start | bytes 184328 | tf_op jit(solution)/shard_map/ppermute | solution.py:107
  58.4 6.6 %collective-permute-start.10 = (bf16[80,384]{1,0:T(8,128)(2,1)S(1)}, bf16[80,384]{1,0:T(8,128)(2,1)S(1)}, u32[]{:S(2)}, u32[]{:S(2)}) collective-permute-start(bf16[80,384]{1,0:T(8,128)(2,1)S(1)} %collective-permute-done.8), channel_id=1, source_target_pairs={{0,32},{32,64},{64,96},{96,128},{128,160},{160,192},{192,224},{224... | collective-permute-start | bytes 184328 | tf_op jit(solution)/shard_map/ppermute | solution.py:104
  60.3 6.6 %collective-permute-start.11 = (bf16[80,384]{1,0:T(8,128)(2,1)S(1)}, bf16[80,384]{1,0:T(8,128)(2,1)S(1)}, u32[]{:S(2)}, u32[]{:S(2)}) collective-permute-start(bf16[80,384]{1,0:T(8,128)(2,1)S(1)} %collective-permute-done.9), channel_id=1, source_target_pairs={{0,480},{32,0},{64,32},{96,64},{128,96},{160,128},{192,160},{224,1... | collective-permute-start | bytes 184328 | tf_op jit(solution)/shard_map/ppermute | solution.py:107
  65.0 6.6 %collective-permute-start.12 = (bf16[80,384]{1,0:T(8,128)(2,1)S(1)}, bf16[80,384]{1,0:T(8,128)(2,1)S(1)}, u32[]{:S(2)}, u32[]{:S(2)}) collective-permute-start(bf16[80,384]{1,0:T(8,128)(2,1)S(1)} %collective-permute-done.10), channel_id=1, source_target_pairs={{0,32},{32,64},{64,96},{96,128},{128,160},{160,192},{192,224},{224... | collective-permute-start | bytes 184328 | tf_op jit(solution)/shard_map/ppermute | solution.py:104
  66.9 6.6 %collective-permute-start.13 = (bf16[80,384]{1,0:T(8,128)(2,1)S(1)}, bf16[80,384]{1,0:T(8,128)(2,1)S(1)}, u32[]{:S(2)}, u32[]{:S(2)}) collective-permute-start(bf16[80,384]{1,0:T(8,128)(2,1)S(1)} %collective-permute-done.11), channel_id=1, source_target_pairs={{0,480},{32,0},{64,32},{96,64},{128,96},{160,128},{192,160},{224,1... | collective-permute-start | bytes 184328 | tf_op jit(solution)/shard_map/ppermute | solution.py:107
  71.6 6.6 %collective-permute-start.14 = (bf16[40,384]{1,0:T(8,128)(2,1)S(1)}, bf16[40,384]{1,0:T(8,128)(2,1)S(1)}, u32[]{:S(2)}, u32[]{:S(2)}) collective-permute-start(bf16[40,384]{1,0:T(8,128)(2,1)S(1)} %slice.129), channel_id=1, source_target_pairs={{0,32},{32,64},{64,96},{96,128},{128,160},{160,192},{192,224},{224... | collective-permute-start | bytes 92168 | tf_op jit(solution)/shard_map/ppermute | solution.py:101
  73.5 5.6 %collective-permute-start.15 = (bf16[40,384]{1,0:T(8,128)(2,1)S(1)}, bf16[40,384]{1,0:T(8,128)(2,1)S(1)}, u32[]{:S(2)}, u32[]{:S(2)}) collective-permute-start(bf16[40,384]{1,0:T(8,128)(2,1)S(1)} %slice.130), channel_id=1, source_target_pairs={{0,480},{32,0},{64,32},{96,64},{128,96},{160,128},{192,160},{224,1... | collective-permute-start | bytes 92168 | tf_op jit(solution)/shard_map/ppermute | solution.py:102
  79.1 19.0 %collective-permute-start.17 = (bf16[16,80,384]{2,1,0:T(8,128)(2,1)S(1)}, bf16[16,80,384]{2,1,0:T(8,128)(2,1)S(1)}, u32[]{:S(2)}, u32[]{:S(2)}) collective-permute-start(bf16[16,80,384]{2,1,0:T(8,128)(2,1)S(1)} %bitcast_dynamic-update-slice_fusion.20), channel_id=1, source_target_pairs={{0,24},{8,0},{16,8},{24,16},{1,25},{9,1},{17,9},{25,17},{2,26},{10... | collective-permute-start | bytes 2949128 | tf_op jit(solution)/shard_map/ppermute | solution.py:107
  83.5 20.0 %collective-permute-start.16 = (bf16[16,80,384]{2,1,0:T(8,128)(2,1)S(1)}, bf16[16,80,384]{2,1,0:T(8,128)(2,1)S(1)}, u32[]{:S(2)}, u32[]{:S(2)}) collective-permute-start(bf16[16,80,384]{2,1,0:T(8,128)(2,1)S(1)} %bitcast_dynamic-update-slice_fusion.20), channel_id=1, source_target_pairs={{0,8},{8,16},{16,24},{24,0},{1,9},{9,17},{17,25},{25,1},{2,10},{10... | collective-permute-start | bytes 2949128 | tf_op jit(solution)/shard_map/ppermute | solution.py:104
  98.1 17.3 %collective-permute-start.19 = (bf16[8,80,384]{2,1,0:T(8,128)(2,1)S(1)}, bf16[8,80,384]{2,1,0:T(8,128)(2,1)S(1)}, u32[]{:S(2)}, u32[]{:S(2)}) collective-permute-start(bf16[8,80,384]{2,1,0:T(8,128)(2,1)S(1)} %slice.132), channel_id=1, source_target_pairs={{0,24},{8,0},{16,8},{24,16},{1,25},{9,1},{17,9},{25,17},{2,26},{10... | collective-permute-start | bytes 1474568 | tf_op jit(solution)/shard_map/ppermute | solution.py:102
  103.5 11.8 %collective-permute-start.18 = (bf16[8,80,384]{2,1,0:T(8,128)(2,1)S(1)}, bf16[8,80,384]{2,1,0:T(8,128)(2,1)S(1)}, u32[]{:S(2)}, u32[]{:S(2)}) collective-permute-start(bf16[8,80,384]{2,1,0:T(8,128)(2,1)S(1)} %slice.131), channel_id=1, source_target_pairs={{0,8},{8,16},{16,24},{24,0},{1,9},{9,17},{17,25},{25,1},{2,10},{10... | collective-permute-start | bytes 1474568 | tf_op jit(solution)/shard_map/ppermute | solution.py:101
  121.4 1.6 copy-start.3
  125.4 25.5 %all-to-all-start = ((f32[8,64,384]{2,1,0:T(8,128)}), f32[8,64,384]{2,1,0:T(8,128)S(1)}, u32[]{:S(2)}, u32[]{:S(2)}) async-start(f32[8,64,384]{2,1,0:T(8,128)} %fusion.50), calls=%async_computation | async-start | bytes 1572864 | tf_op jit(solution)/shard_map/all_to_all | solution.py:176
  138.7 48.0 %all-gather.5.cloned.1.call-start = ((), (), s32[]{:S(2)}) async-start(), calls=%async_computation.2 | async-start | bytes 2949120 | tf_op jit(solution)/shard_map/all_gather | solution.py:205
  156.4 1.7 copy-start.2
  186.7 5.2 %copy-start.1 = (bf16[4,2,128,256]{3,2,1,0:T(8,128)(2,1)S(1)}, bf16[4,2,128,256]{3,2,1,0:T(8,128)(2,1)}, u32[]{:S(2)}) copy-start(bf16[4,2,128,256]{3,2,1,0:T(8,128)(2,1)} %param.15) | copy-start | bytes 1572868
Sparse Core Ops, SparseCore 0:
  25.3 32.5 all-gather.2
  157.7 28.9 all-gather.4

commit v5 on v4

--- a/solution.py
+++ b/solution.py
@@ -173,8 +173,8 @@
     mean_square = jnp.mean(wide * wide, axis=1, keepdims=True)
     normed = (wide * lax.rsqrt(mean_square + 1e-06)).astype(jnp.bfloat16)
     both = jnp.dot(normed, proj_w, preferred_element_type=jnp.float32)
-    mine = lax.all_to_all(both, "head", 0, 1, tiled=True)
-    mine = mine.reshape(DRAFT, head_count, q_cols + kv_cols)
+    mine = lax.all_to_all(both.astype(jnp.bfloat16), "head", 0, 1, tiled=True)
+    mine = mine.reshape(DRAFT, head_count, q_cols + kv_cols).astype(jnp.float32)
     q_pre = mine[:, :, :q_cols].reshape(DRAFT, HQ, HD)
     kv_pre = mine[:, :, q_cols:].reshape(DRAFT, 2 * HD)
     parent_row = lax.dynamic_index_in_dim(parents, head_index, 0, keepdims=False)

time: 200 us -> 202 us (1.010)
  waiting for transfers between devices: 34.5 us -> 26.3 us
  other arithmetic: 7.76 us -> 14.5 us
  matrix products: 10.5 us -> 13.3 us
    all_to_all x1, waiting for transfers between devices: 10.7 us -> 3.8 us  [shards(): mine = lax.all_to_all(both.astype(jnp.bfloat16), 'head', 0, 1, tiled=True)]
    slice x3 -> x2, local copies, waits for them, and re-layouts: 9.38 us -> 5.02 us  [shards(): stacked[:, part_rows:].reshape(tok_count, -1)[:, :wo_flat.shape[0]]]
    reshape x1 -> x2, local copies, waits for them, and re-layouts: 7.12 us -> 10.9 us  [shards(): wo_cols = stacked[:, part_rows:].reshape(tok_count, -1)[:, :wo_flat.shape...]
    all_gather x1 -> x0, local copies, waits for them, and re-layouts: 2.98 us -> none  [shards(): gathered = lax.all_gather(tokens, 'head', axis=1, tiled=True)]
  transfers between devices with their start and end apart: 23 -> 23, of which waited for: 5 -> 5; matrix products, arithmetic and copies ran while one was open for 19% -> 21% of each run, Pallas kernels for 0% -> 0%
where the time goes in v5:
time: 202 us; the launch traced here: 200 us
  starting transfers between devices  86.2 us (43%)
  local copies, waits for them, and re-layouts  42.9 us (21%)
  waiting for transfers between devices  26.3 us (13%)
  between operations  17.4 us (9%)
  other arithmetic  14.5 us (7%)
  matrix products  13.3 us (7%)
    ppermute x8, starting transfers between devices, ring_pieces(): behind = lax.ppermute(behind, axis, backward)  41.3 us
    ppermute x8, starting transfers between devices, ring_pieces(): ahead = lax.ppermute(ahead, axis, forward)  17.8 us
    all_to_all x1, starting transfers between devices, shards(): mine = lax.all_to_all(both.astype(jnp.bfloat16), 'head', 0, 1, tiled=True)  13.3 us
    reshape x2, local copies, waits for them, and re-layouts, shards(): wo_cols = stacked[:, part_rows:].reshape(tok_count, -1)[:, :wo_flat.shape...  10.9 us
    ppermute x2, starting transfers between devices, ring_pieces(): got.append((step, half, lax.ppermute(behind[half:], axis, backward)))  9.89 us
    ppermute x8, waiting for transfers between devices, ring_pieces(): behind = lax.ppermute(behind, axis, backward)  9.62 us
    ppermute x2, waiting for transfers between devices, ring_pieces(): got.append((step, 0, lax.ppermute(ahead[:half], axis, forward)))  9.45 us
    transpose x1, local copies, waits for them, and re-layouts, shards(): wo_cols = stacked[:, part_rows:].reshape(tok_count, -1)[:, :wo_flat.shape...  7 us
  transfers between devices with their start and end apart: 23, of which 5 were waited for; matrix products, arithmetic and copies ran while one was open for 21% of the time, Pallas kernels for 0%

profile of v5, /device:TPU:1, one launch (start us, length us, event | category | flops | bytes accessed | tf_op | source)
XLA Modules:
  0.0 200.5 jit_solution(7967247948551152880)
XLA Ops:
  7.3 1.2 copy.47
  8.5 1.0 reshape.343
  9.5 0.8 constant_dynamic-slice_fusion.1
  10.3 0.9 constant_dynamic-slice_fusion.2
  11.3 4.4 %collective-permute-start = (bf16[80,384]{1,0:T(8,128)(2,1)S(1)}, bf16[80,384]{1,0:T(8,128)(2,1)S(1)}, u32[]{:S(2)}, u32[]{:S(2)}) collective-permute-start(bf16[80,384]{1,0:T(8,128)(2,1)S(1)} %get-tuple-element.6), channel_id=1, source_target_pairs={{0,32},{32,64},{64,96},{96,128},{128,160},{160,192},{192,224},{224... | collective-permute-start | bytes 184328 | tf_op jit(solution)/shard_map/ppermute | solution.py:104
  15.7 9.5 %collective-permute-start.1 = (bf16[80,384]{1,0:T(8,128)(2,1)S(1)}, bf16[80,384]{1,0:T(8,128)(2,1)S(1)}, u32[]{:S(2)}, u32[]{:S(2)}) collective-permute-start(bf16[80,384]{1,0:T(8,128)(2,1)S(1)} %get-tuple-element.6), channel_id=1, source_target_pairs={{0,480},{32,0},{64,32},{96,64},{128,96},{160,128},{192,160},{224,1... | collective-permute-start | bytes 184328 | tf_op jit(solution)/shard_map/ppermute | solution.py:107
  25.4 0.6 dynamic_slice.29
  27.3 0.6 dynamic_slice.24
  27.9 0.7 fusion.44
  28.9 0.6 compare_select_fusion
  29.5 0.6 iota_subtract_fusion
  32.3 1.9 collective-permute-start.2
  34.2 4.6 %collective-permute-start.3 = (bf16[80,384]{1,0:T(8,128)(2,1)S(1)}, bf16[80,384]{1,0:T(8,128)(2,1)S(1)}, u32[]{:S(2)}, u32[]{:S(2)}) collective-permute-start(bf16[80,384]{1,0:T(8,128)(2,1)S(1)} %collective-permute-done.1), channel_id=1, source_target_pairs={{0,480},{32,0},{64,32},{96,64},{128,96},{160,128},{192,160},{224,1... | collective-permute-start | bytes 184328 | tf_op jit(solution)/shard_map/ppermute | solution.py:107
  38.9 1.9 collective-permute-start.4
  40.8 4.6 %collective-permute-start.5 = (bf16[80,384]{1,0:T(8,128)(2,1)S(1)}, bf16[80,384]{1,0:T(8,128)(2,1)S(1)}, u32[]{:S(2)}, u32[]{:S(2)}) collective-permute-start(bf16[80,384]{1,0:T(8,128)(2,1)S(1)} %collective-permute-done.3), channel_id=1, source_target_pairs={{0,480},{32,0},{64,32},{96,64},{128,96},{160,128},{192,160},{224,1... | collective-permute-start | bytes 184328 | tf_op jit(solution)/shard_map/ppermute | solution.py:107
  45.4 1.9 collective-permute-start.6
  47.4 4.6 %collective-permute-start.7 = (bf16[80,384]{1,0:T(8,128)(2,1)S(1)}, bf16[80,384]{1,0:T(8,128)(2,1)S(1)}, u32[]{:S(2)}, u32[]{:S(2)}) collective-permute-start(bf16[80,384]{1,0:T(8,128)(2,1)S(1)} %collective-permute-done.5), channel_id=1, source_target_pairs={{0,480},{32,0},{64,32},{96,64},{128,96},{160,128},{192,160},{224,1... | collective-permute-start | bytes 184328 | tf_op jit(solution)/shard_map/ppermute | solution.py:107
  52.0 1.9 collective-permute-start.8
  54.0 4.6 %collective-permute-start.9 = (bf16[80,384]{1,0:T(8,128)(2,1)S(1)}, bf16[80,384]{1,0:T(8,128)(2,1)S(1)}, u32[]{:S(2)}, u32[]{:S(2)}) collective-permute-start(bf16[80,384]{1,0:T(8,128)(2,1)S(1)} %collective-permute-done.7), channel_id=1, source_target_pairs={{0,480},{32,0},{64,32},{96,64},{128,96},{160,128},{192,160},{224,1... | collective-permute-start | bytes 184328 | tf_op jit(solution)/shard_map/ppermute | solution.py:107
  58.6 1.9 collective-permute-start.10
  60.5 4.6 %collective-permute-start.11 = (bf16[80,384]{1,0:T(8,128)(2,1)S(1)}, bf16[80,384]{1,0:T(8,128)(2,1)S(1)}, u32[]{:S(2)}, u32[]{:S(2)}) collective-permute-start(bf16[80,384]{1,0:T(8,128)(2,1)S(1)} %collective-permute-done.9), channel_id=1, source_target_pairs={{0,480},{32,0},{64,32},{96,64},{128,96},{160,128},{192,160},{224,1... | collective-permute-start | bytes 184328 | tf_op jit(solution)/shard_map/ppermute | solution.py:107
  65.2 1.9 collective-permute-start.12
  67.1 4.6 %collective-permute-start.13 = (bf16[80,384]{1,0:T(8,128)(2,1)S(1)}, bf16[80,384]{1,0:T(8,128)(2,1)S(1)}, u32[]{:S(2)}, u32[]{:S(2)}) collective-permute-start(bf16[80,384]{1,0:T(8,128)(2,1)S(1)} %collective-permute-done.11), channel_id=1, source_target_pairs={{0,480},{32,0},{64,32},{96,64},{128,96},{160,128},{192,160},{224,1... | collective-permute-start | bytes 184328 | tf_op jit(solution)/shard_map/ppermute | solution.py:107
  71.8 1.9 collective-permute-start.14
  73.7 4.6 %collective-permute-start.15 = (bf16[40,384]{1,0:T(8,128)(2,1)S(1)}, bf16[40,384]{1,0:T(8,128)(2,1)S(1)}, u32[]{:S(2)}, u32[]{:S(2)}) collective-permute-start(bf16[40,384]{1,0:T(8,128)(2,1)S(1)} %slice.130), channel_id=1, source_target_pairs={{0,480},{32,0},{64,32},{96,64},{128,96},{160,128},{192,160},{224,1... | collective-permute-start | bytes 92168 | tf_op jit(solution)/shard_map/ppermute | solution.py:102
  78.4 0.9 collective-permute-done.15
  79.3 4.4 %collective-permute-start.17 = (bf16[16,80,384]{2,1,0:T(8,128)(2,1)S(1)}, bf16[16,80,384]{2,1,0:T(8,128)(2,1)S(1)}, u32[]{:S(2)}, u32[]{:S(2)}) collective-permute-start(bf16[16,80,384]{2,1,0:T(8,128)(2,1)S(1)} %bitcast_dynamic-update-slice_fusion.20), channel_id=1, source_target_pairs={{0,24},{8,0},{16,8},{24,16},{1,25},{9,1},{17,9},{25,17},{2,26},{10... | collective-permute-start | bytes 2949128 | tf_op jit(solution)/shard_map/ppermute | solution.py:107
  83.7 1.9 collective-permute-start.16
  86.2 1.2 add_add_fusion
  87.5 0.5 compare_bitcast_fusion
  88.7 9.6 %collective-permute-done.17 = bf16[16,80,384]{2,1,0:T(8,128)(2,1)S(1)} collective-permute-done((bf16[16,80,384]{2,1,0:T(8,128)(2,1)S(1)}, bf16[16,80,384]{2,1,0:T(8,128)(2,1)S(1)}, u32[]{:S(2)}, u32[]{:S(2)}) %collective-permute-start.17) | collective-permute-done | bytes 983072 | tf_op jit(solution)/shard_map/ppermute | solution.py:107
  98.4 5.3 %collective-permute-start.19 = (bf16[8,80,384]{2,1,0:T(8,128)(2,1)S(1)}, bf16[8,80,384]{2,1,0:T(8,128)(2,1)S(1)}, u32[]{:S(2)}, u32[]{:S(2)}) collective-permute-start(bf16[8,80,384]{2,1,0:T(8,128)(2,1)S(1)} %slice.132), channel_id=1, source_target_pairs={{0,24},{8,0},{16,8},{24,16},{1,25},{9,1},{17,9},{25,17},{2,26},{10... | collective-permute-start | bytes 1474568 | tf_op jit(solution)/shard_map/ppermute | solution.py:102
  103.8 1.9 collective-permute-start.18
  106.1 9.5 %collective-permute-done.18 = bf16[8,80,384]{2,1,0:T(8,128)(2,1)S(1)} collective-permute-done((bf16[8,80,384]{2,1,0:T(8,128)(2,1)S(1)}, bf16[8,80,384]{2,1,0:T(8,128)(2,1)S(1)}, u32[]{:S(2)}, u32[]{:S(2)}) %collective-permute-start.18) | collective-permute-done | bytes 491552 | tf_op jit(solution)/shard_map/ppermute | solution.py:101
  115.8 1.7 fusion.50
  117.5 2.5 %fusion = f32[512]{0:T(512)S(1)} fusion(bf16[512,2560]{0,1:T(8,128)(2,1)} %all-gather.3.cloned.1.call-done), kind=kLoop, calls=%fused_computation.4 | loop fusion | flops 3931648 | bytes 2623488 | tf_op jit(solution)/shard_map/reduce_sum | solution.py:173
  120.0 3.9 %fusion.8 = bf16[512,384]{1,0:T(8,128)(2,1)} fusion(bf16[2560,384]{1,0:T(8,128)(2,1)} %bitcast.134, bf16[512,2560]{0,1:T(8,128)(2,1)S(1)} %copy-done.1, f32[512]{0:T(512)S(1)} %add_rsqrt_fusion), kind=kOutput, calls=%fused_computation.15 | convolution fusion | flops 1010761728 | bytes 4982784 | tf_op jit(solution)/shard_map/dot_general | solution.py:175
  123.9 13.3 %all-to-all-start = ((bf16[8,64,384]{2,1,0:T(8,128)(2,1)}), bf16[8,64,384]{2,1,0:T(8,128)(2,1)}, u32[]{:S(2)}, u32[]{:S(2)}) async-start(bf16[8,64,384]{2,1,0:T(8,128)(2,1)} %bitcast.32), calls=%async_computation | async-start | bytes 786432 | tf_op jit(solution)/shard_map/all_to_all | solution.py:176
  137.2 0.6 iota_compare_fusion.6
  137.8 0.7 copy.56
  138.5 1.4 gather_fusion
  139.9 0.6 multiply_exponential_fusion
  140.5 0.7 fusion.25
  141.2 3.8 %all-to-all-done = bf16[8,64,384]{2,1,0:T(8,128)(2,1)} async-done(((bf16[8,64,384]{2,1,0:T(8,128)(2,1)}), bf16[8,64,384]{2,1,0:T(8,128)(2,1)}, u32[]{:S(2)}, u32[]{:S(2)}) %all-to-all-start) | async-done | bytes 393248 | tf_op jit(solution)/shard_map/all_to_all | solution.py:176
  145.0 1.1 convert_bitcast_fusion
  146.3 0.8 reshape.348
  147.1 0.9 convert.36
  148.1 0.6 copy-done.5
  148.7 1.7 convolution_convert_fusion
  150.4 1.3 copy.52
  151.7 1.6 reshape.347
  153.6 0.6 copy-done.4
  154.8 1.0 fusion.19
  157.9 1.2 fusion.11
  159.2 3.8 %copy.65 = bf16[64,40,384]{0,2,1:T(8,128)(2,1)} copy(bf16[64,40,384]{2,1,0:T(8,128)(2,1)S(1)} %get-tuple-element.7) | data formatting | bytes 3932160 | tf_op jit(solution)/shard_map/reshape | solution.py:166
  163.0 3.3 %slice.145 = bf16[64,12800]{0,1:T(8,128)(2,1)} slice(bf16[64,15360]{0,1:T(8,128)(2,1)} %bitcast.132), slice={[0:64], [0:12800]} | slice | bytes 3276800 | tf_op jit(solution)/shard_map/slice | solution.py:165
  166.3 7.1 %reshape.353 = bf16[64,2560,5]{0,2,1:T(8,128)(2,1)} reshape(bf16[64,12800]{0,1:T(8,128)(2,1)} %slice.145) | data formatting | bytes 3276800 | tf_op jit(solution)/shard_map/reshape | solution.py:167
  173.4 7.0 %copy.60 = bf16[2560,64,5]{0,2,1:T(8,128)(2,1)S(1)} copy(bf16[2560,64,5]{1,2,0:T(8,128)(2,1)} %bitcast.130) | data formatting | bytes 3276800 | tf_op jit(solution)/shard_map/transpose | solution.py:168
  180.4 3.1 %reshape_reshape.3 = bf16[10,256,320]{1,0,2:T(8,128)(2,1)} reshape(bf16[2560,64,5]{0,2,1:T(8,128)(2,1)S(1)} %copy.60) | data formatting | bytes 3276800 | tf_op jit(solution)/shard_map/reshape;reshape | solution.py:208
  183.5 1.6 gather_fusion.1
  185.2 0.9 broadcast_select_fusion
  186.1 2.4 %all-gather.5.cloned.1.call-done = bf16[10,512,256]{2,1,0:T(8,128)(2,1)} async-done(((bf16[10,64,256]{2,1,0:T(8,128)(2,1)}), bf16[10,512,256]{2,1,0:T(8,128)(2,1)}) %all-gather.5.cloned.1.call-update) | async-done | bytes 2621456 | tf_op jit(solution)/shard_map/all_gather | solution.py:205
  188.5 3.9 %fusion.55 = (bf16[10,512,320]{1,2,0:T(8,128)(2,1)S(1)}, f32[10,512,320]{1,2,0:T(8,128)S(1)}) fusion(bf16[10,512,256]{2,1,0:T(8,128)(2,1)} %all-gather.5.cloned.1.call-done, bf16[10,256,320]{1,0,2:T(8,128)(2,1)} %reshape_reshape.3), kind=kOutput, calls=%fused_computation.135 | convolution fusion | flops 840499200 | bytes 14090240 | tf_op jit(solution)/shard_map/dot_general | solution.py:206
  192.4 1.2 fusion.20
  (134 shorter events, 7.3 us)
Async XLA Ops:
  7.2 131.4 %copy-start = (bf16[4,2,128,256]{3,2,1,0:T(8,128)(2,1)S(1)}, bf16[4,2,128,256]{3,2,1,0:T(8,128)(2,1)}, u32[]{:S(2)}) copy-start(bf16[4,2,128,256]{3,2,1,0:T(8,128)(2,1)} %param.15) | copy-start | bytes 1572868
  7.2 18.2 %copy-start.23 = (s32[8]{0:T(128)S(1)}, s32[8]{0:T(128)}, u32[]{:S(2)}) copy-start(s32[8]{0:T(128)} %param.19) | copy-start | bytes 100
  7.2 20.1 %copy-start.24 = (s32[8]{0:T(128)S(1)}, s32[8]{0:T(128)}, u32[]{:S(2)}) copy-start(s32[8]{0:T(128)} %param.18) | copy-start | bytes 100
  7.2 21.4 %copy-start.16 = (s32[8,4]{0,1:T(4,128)S(1)}, s32[8,4]{0,1:T(4,128)}, u32[]{:S(2)}) copy-start(s32[8,4]{0,1:T(4,128)} %param.16) | copy-start | bytes 388
  7.2 110.3 %all-gather.3.cloned.1.call-start = ((), (), s32[]{:S(2)}) async-start(), calls=%async_computation.1 | async-start | bytes 2949120 | tf_op jit(solution)/shard_map/all_gather | solution.py:171
  11.3 20.9 %collective-permute-start = (bf16[80,384]{1,0:T(8,128)(2,1)S(1)}, bf16[80,384]{1,0:T(8,128)(2,1)S(1)}, u32[]{:S(2)}, u32[]{:S(2)}) collective-permute-start(bf16[80,384]{1,0:T(8,128)(2,1)S(1)} %get-tuple-element.6), channel_id=1, source_target_pairs={{0,32},{32,64},{64,96},{96,128},{128,160},{160,192},{192,224},{224... | collective-permute-start | bytes 184328 | tf_op jit(solution)/shard_map/ppermute | solution.py:104
  15.7 18.5 %collective-permute-start.1 = (bf16[80,384]{1,0:T(8,128)(2,1)S(1)}, bf16[80,384]{1,0:T(8,128)(2,1)S(1)}, u32[]{:S(2)}, u32[]{:S(2)}) collective-permute-start(bf16[80,384]{1,0:T(8,128)(2,1)S(1)} %get-tuple-element.6), channel_id=1, source_target_pairs={{0,480},{32,0},{64,32},{96,64},{128,96},{160,128},{192,160},{224,1... | collective-permute-start | bytes 184328 | tf_op jit(solution)/shard_map/ppermute | solution.py:107
  28.9 2.0 %copy-start.20 = (s32[4]{0:T(128)}, s32[4]{0:T(128)S(1)}, u32[]{:S(2)}) copy-start(s32[4]{0:T(128)S(1)} %select_reduce_fusion) | copy-start | bytes 52
  30.1 49.2 %copy-start.9 = (s32[512]{0:T(512)}, s32[512]{0:T(512)S(1)}, u32[]{:S(2)}) copy-start(s32[512]{0:T(512)S(1)} %iota_subtract_fusion) | copy-start | bytes 6148
  31.9 47.4 %copy-start.11 = (pred[64]{0:T(512)(128)(4,1)}, pred[64]{0:T(512)(128)(4,1)S(1)}, u32[]{:S(2)}) copy-start(pred[64]{0:T(512)(128)(4,1)S(1)} %compare_bitcast_fusion.1) | copy-start | bytes 196
  32.1 39.7 %copy-start.13 = (s32[64]{0:T(128)}, s32[64]{0:T(128)S(1)}, u32[]{:S(2)}) copy-start(s32[64]{0:T(128)S(1)} %add_convert_fusion.2) | copy-start | bytes 772
  32.3 6.6 %collective-permute-start.2 = (bf16[80,384]{1,0:T(8,128)(2,1)S(1)}, bf16[80,384]{1,0:T(8,128)(2,1)S(1)}, u32[]{:S(2)}, u32[]{:S(2)}) collective-permute-start(bf16[80,384]{1,0:T(8,128)(2,1)S(1)} %collective-permute-done), channel_id=1, source_target_pairs={{0,32},{32,64},{64,96},{96,128},{128,160},{160,192},{192,224},{224... | collective-permute-start | bytes 184328 | tf_op jit(solution)/shard_map/ppermute | solution.py:104
  34.2 6.6 %collective-permute-start.3 = (bf16[80,384]{1,0:T(8,128)(2,1)S(1)}, bf16[80,384]{1,0:T(8,128)(2,1)S(1)}, u32[]{:S(2)}, u32[]{:S(2)}) collective-permute-start(bf16[80,384]{1,0:T(8,128)(2,1)S(1)} %collective-permute-done.1), channel_id=1, source_target_pairs={{0,480},{32,0},{64,32},{96,64},{128,96},{160,128},{192,160},{224,1... | collective-permute-start | bytes 184328 | tf_op jit(solution)/shard_map/ppermute | solution.py:107
  38.9 6.6 %collective-permute-start.4 = (bf16[80,384]{1,0:T(8,128)(2,1)S(1)}, bf16[80,384]{1,0:T(8,128)(2,1)S(1)}, u32[]{:S(2)}, u32[]{:S(2)}) collective-permute-start(bf16[80,384]{1,0:T(8,128)(2,1)S(1)} %collective-permute-done.2), channel_id=1, source_target_pairs={{0,32},{32,64},{64,96},{96,128},{128,160},{160,192},{192,224},{224... | collective-permute-start | bytes 184328 | tf_op jit(solution)/shard_map/ppermute | solution.py:104
  40.8 6.6 %collective-permute-start.5 = (bf16[80,384]{1,0:T(8,128)(2,1)S(1)}, bf16[80,384]{1,0:T(8,128)(2,1)S(1)}, u32[]{:S(2)}, u32[]{:S(2)}) collective-permute-start(bf16[80,384]{1,0:T(8,128)(2,1)S(1)} %collective-permute-done.3), channel_id=1, source_target_pairs={{0,480},{32,0},{64,32},{96,64},{128,96},{160,128},{192,160},{224,1... | collective-permute-start | bytes 184328 | tf_op jit(solution)/shard_map/ppermute | solution.py:107
  45.4 6.6 %collective-permute-start.6 = (bf16[80,384]{1,0:T(8,128)(2,1)S(1)}, bf16[80,384]{1,0:T(8,128)(2,1)S(1)}, u32[]{:S(2)}, u32[]{:S(2)}) collective-permute-start(bf16[80,384]{1,0:T(8,128)(2,1)S(1)} %collective-permute-done.4), channel_id=1, source_target_pairs={{0,32},{32,64},{64,96},{96,128},{128,160},{160,192},{192,224},{224... | collective-permute-start | bytes 184328 | tf_op jit(solution)/shard_map/ppermute | solution.py:104
  47.4 6.6 %collective-permute-start.7 = (bf16[80,384]{1,0:T(8,128)(2,1)S(1)}, bf16[80,384]{1,0:T(8,128)(2,1)S(1)}, u32[]{:S(2)}, u32[]{:S(2)}) collective-permute-start(bf16[80,384]{1,0:T(8,128)(2,1)S(1)} %collective-permute-done.5), channel_id=1, source_target_pairs={{0,480},{32,0},{64,32},{96,64},{128,96},{160,128},{192,160},{224,1... | collective-permute-start | bytes 184328 | tf_op jit(solution)/shard_map/ppermute | solution.py:107
  52.0 6.6 %collective-permute-start.8 = (bf16[80,384]{1,0:T(8,128)(2,1)S(1)}, bf16[80,384]{1,0:T(8,128)(2,1)S(1)}, u32[]{:S(2)}, u32[]{:S(2)}) collective-permute-start(bf16[80,384]{1,0:T(8,128)(2,1)S(1)} %collective-permute-done.6), channel_id=1, source_target_pairs={{0,32},{32,64},{64,96},{96,128},{128,160},{160,192},{192,224},{224... | collective-permute-start | bytes 184328 | tf_op jit(solution)/shard_map/ppermute | solution.py:104
  54.0 6.6 %collective-permute-start.9 = (bf16[80,384]{1,0:T(8,128)(2,1)S(1)}, bf16[80,384]{1,0:T(8,128)(2,1)S(1)}, u32[]{:S(2)}, u32[]{:S(2)}) collective-permute-start(bf16[80,384]{1,0:T(8,128)(2,1)S(1)} %collective-permute-done.7), channel_id=1, source_target_pairs={{0,480},{32,0},{64,32},{96,64},{128,96},{160,128},{192,160},{224,1... | collective-permute-start | bytes 184328 | tf_op jit(solution)/shard_map/ppermute | solution.py:107
  58.6 6.6 %collective-permute-start.10 = (bf16[80,384]{1,0:T(8,128)(2,1)S(1)}, bf16[80,384]{1,0:T(8,128)(2,1)S(1)}, u32[]{:S(2)}, u32[]{:S(2)}) collective-permute-start(bf16[80,384]{1,0:T(8,128)(2,1)S(1)} %collective-permute-done.8), channel_id=1, source_target_pairs={{0,32},{32,64},{64,96},{96,128},{128,160},{160,192},{192,224},{224... | collective-permute-start | bytes 184328 | tf_op jit(solution)/shard_map/ppermute | solution.py:104
  60.5 6.6 %collective-permute-start.11 = (bf16[80,384]{1,0:T(8,128)(2,1)S(1)}, bf16[80,384]{1,0:T(8,128)(2,1)S(1)}, u32[]{:S(2)}, u32[]{:S(2)}) collective-permute-start(bf16[80,384]{1,0:T(8,128)(2,1)S(1)} %collective-permute-done.9), channel_id=1, source_target_pairs={{0,480},{32,0},{64,32},{96,64},{128,96},{160,128},{192,160},{224,1... | collective-permute-start | bytes 184328 | tf_op jit(solution)/shard_map/ppermute | solution.py:107
  65.2 6.6 %collective-permute-start.12 = (bf16[80,384]{1,0:T(8,128)(2,1)S(1)}, bf16[80,384]{1,0:T(8,128)(2,1)S(1)}, u32[]{:S(2)}, u32[]{:S(2)}) collective-permute-start(bf16[80,384]{1,0:T(8,128)(2,1)S(1)} %collective-permute-done.10), channel_id=1, source_target_pairs={{0,32},{32,64},{64,96},{96,128},{128,160},{160,192},{192,224},{224... | collective-permute-start | bytes 184328 | tf_op jit(solution)/shard_map/ppermute | solution.py:104
  67.1 6.6 %collective-permute-start.13 = (bf16[80,384]{1,0:T(8,128)(2,1)S(1)}, bf16[80,384]{1,0:T(8,128)(2,1)S(1)}, u32[]{:S(2)}, u32[]{:S(2)}) collective-permute-start(bf16[80,384]{1,0:T(8,128)(2,1)S(1)} %collective-permute-done.11), channel_id=1, source_target_pairs={{0,480},{32,0},{64,32},{96,64},{128,96},{160,128},{192,160},{224,1... | collective-permute-start | bytes 184328 | tf_op jit(solution)/shard_map/ppermute | solution.py:107
  71.8 6.6 %collective-permute-start.14 = (bf16[40,384]{1,0:T(8,128)(2,1)S(1)}, bf16[40,384]{1,0:T(8,128)(2,1)S(1)}, u32[]{:S(2)}, u32[]{:S(2)}) collective-permute-start(bf16[40,384]{1,0:T(8,128)(2,1)S(1)} %slice.129), channel_id=1, source_target_pairs={{0,32},{32,64},{64,96},{96,128},{128,160},{160,192},{192,224},{224... | collective-permute-start | bytes 92168 | tf_op jit(solution)/shard_map/ppermute | solution.py:101
  73.7 5.6 %collective-permute-start.15 = (bf16[40,384]{1,0:T(8,128)(2,1)S(1)}, bf16[40,384]{1,0:T(8,128)(2,1)S(1)}, u32[]{:S(2)}, u32[]{:S(2)}) collective-permute-start(bf16[40,384]{1,0:T(8,128)(2,1)S(1)} %slice.130), channel_id=1, source_target_pairs={{0,480},{32,0},{64,32},{96,64},{128,96},{160,128},{192,160},{224,1... | collective-permute-start | bytes 92168 | tf_op jit(solution)/shard_map/ppermute | solution.py:102
  79.3 19.0 %collective-permute-start.17 = (bf16[16,80,384]{2,1,0:T(8,128)(2,1)S(1)}, bf16[16,80,384]{2,1,0:T(8,128)(2,1)S(1)}, u32[]{:S(2)}, u32[]{:S(2)}) collective-permute-start(bf16[16,80,384]{2,1,0:T(8,128)(2,1)S(1)} %bitcast_dynamic-update-slice_fusion.20), channel_id=1, source_target_pairs={{0,24},{8,0},{16,8},{24,16},{1,25},{9,1},{17,9},{25,17},{2,26},{10... | collective-permute-start | bytes 2949128 | tf_op jit(solution)/shard_map/ppermute | solution.py:107
  83.7 20.0 %collective-permute-start.16 = (bf16[16,80,384]{2,1,0:T(8,128)(2,1)S(1)}, bf16[16,80,384]{2,1,0:T(8,128)(2,1)S(1)}, u32[]{:S(2)}, u32[]{:S(2)}) collective-permute-start(bf16[16,80,384]{2,1,0:T(8,128)(2,1)S(1)} %bitcast_dynamic-update-slice_fusion.20), channel_id=1, source_target_pairs={{0,8},{8,16},{16,24},{24,0},{1,9},{9,17},{17,25},{25,1},{2,10},{10... | collective-permute-start | bytes 2949128 | tf_op jit(solution)/shard_map/ppermute | solution.py:104
  98.4 17.3 %collective-permute-start.19 = (bf16[8,80,384]{2,1,0:T(8,128)(2,1)S(1)}, bf16[8,80,384]{2,1,0:T(8,128)(2,1)S(1)}, u32[]{:S(2)}, u32[]{:S(2)}) collective-permute-start(bf16[8,80,384]{2,1,0:T(8,128)(2,1)S(1)} %slice.132), channel_id=1, source_target_pairs={{0,24},{8,0},{16,8},{24,16},{1,25},{9,1},{17,9},{25,17},{2,26},{10... | collective-permute-start | bytes 1474568 | tf_op jit(solution)/shard_map/ppermute | solution.py:102
  103.8 11.8 %collective-permute-start.18 = (bf16[8,80,384]{2,1,0:T(8,128)(2,1)S(1)}, bf16[8,80,384]{2,1,0:T(8,128)(2,1)S(1)}, u32[]{:S(2)}, u32[]{:S(2)}) collective-permute-start(bf16[8,80,384]{2,1,0:T(8,128)(2,1)S(1)} %slice.131), channel_id=1, source_target_pairs={{0,8},{8,16},{16,24},{24,0},{1,9},{9,17},{17,25},{25,1},{2,10},{10... | collective-permute-start | bytes 1474568 | tf_op jit(solution)/shard_map/ppermute | solution.py:101
  117.5 2.5 %copy-start.1 = (bf16[512,2560]{0,1:T(8,128)(2,1)S(1)}, bf16[512,2560]{0,1:T(8,128)(2,1)}, u32[]{:S(2)}) copy-start(bf16[512,2560]{0,1:T(8,128)(2,1)} %all-gather.3.cloned.1.call-done) | copy-start | bytes 7864324
  123.9 21.1 %all-to-all-start = ((bf16[8,64,384]{2,1,0:T(8,128)(2,1)}), bf16[8,64,384]{2,1,0:T(8,128)(2,1)}, u32[]{:S(2)}, u32[]{:S(2)}) async-start(bf16[8,64,384]{2,1,0:T(8,128)(2,1)} %bitcast.32), calls=%async_computation | async-start | bytes 786432 | tf_op jit(solution)/shard_map/all_to_all | solution.py:176
  137.2 51.3 %all-gather.5.cloned.1.call-start = ((), (), s32[]{:S(2)}) async-start(), calls=%async_computation.2 | async-start | bytes 2949120 | tf_op jit(solution)/shard_map/all_gather | solution.py:205
  148.0 0.6 copy-start.5
  153.3 0.9 copy-start.4
  153.3 0.9 copy-start.15
  153.3 0.9 copy-start.19
  153.3 1.1 copy-start.10
  153.3 1.1 copy-start.12
  153.3 1.1 copy-start.14
  153.3 1.4 copy-start.2
  153.4 1.4 copy-start.3
  153.4 1.4 copy-start.18
  153.4 1.4 copy-start.22
  154.8 1.3 copy-start.8
  155.8 0.8 copy-start.7
  156.1 1.5 copy-start.6
  157.9 1.2 copy-start.17
  157.9 1.2 copy-start.21
Sparse Core Ops, SparseCore 0:
  25.3 32.5 all-gather.2
  159.3 29.1 all-gather.4

commit v6 on v4

--- a/solution.py
+++ b/solution.py
@@ -109,7 +109,7 @@
     return got
 
 
-def grid_gather(piece):
+def grid_gather(piece, early):
     z_size = lax.axis_size("tz")
     x_size = lax.axis_size("tx")
     z_index = lax.axis_index("tz")
@@ -120,12 +120,13 @@
         column = lax.dynamic_update_slice(
             column, part[None], ((z_index + offset) % z_size, jnp.int32(first), zero)
         )
+    column, early = lax.optimization_barrier((column, early))
     placed = jnp.zeros((z_size, x_size) + piece.shape, piece.dtype)
     for offset, first, part in ring_pieces(column, "tx"):
         placed = lax.dynamic_update_slice(
             placed, part[:, None], (jnp.int32(first), (x_index + offset) % x_size, zero, zero)
         )
-    return placed.reshape((z_size * x_size,) + piece.shape)
+    return placed.reshape((z_size * x_size,) + piece.shape), early
 
 
 def shards(
@@ -158,7 +159,11 @@
     wo_rows = -(-(part_rows + wo_rows) // 8) * 8 - part_rows
     wo_block = jnp.pad(wo_flat, (0, wo_rows * width - wo_flat.shape[0])).reshape(wo_rows, width)
     piece = jnp.concatenate([proj_piece, wo_block], axis=0)
-    stacked = grid_gather(piece)
+    gathered = lax.all_gather(tokens, "head", axis=1, tiled=True)
+    wide = gathered.astype(jnp.float32)
+    mean_square = jnp.mean(wide * wide, axis=1, keepdims=True)
+    normed = (wide * lax.rsqrt(mean_square + 1e-06)).astype(jnp.bfloat16)
+    stacked, normed = grid_gather(piece, normed)
     tok_count = stacked.shape[0]
     proj_w = stacked[:, :part_rows].reshape(tok_count * part_rows, width)
     wo_cols = (
@@ -168,10 +173,6 @@
         .transpose(1, 0, 2)
         .reshape(HQ * HD, tok_count * out_cols)
     )
-    gathered = lax.all_gather(tokens, "head", axis=1, tiled=True)
-    wide = gathered.astype(jnp.float32)
-    mean_square = jnp.mean(wide * wide, axis=1, keepdims=True)
-    normed = (wide * lax.rsqrt(mean_square + 1e-06)).astype(jnp.bfloat16)
     both = jnp.dot(normed, proj_w, preferred_element_type=jnp.float32)
     mine = lax.all_to_all(both, "head", 0, 1, tiled=True)
     mine = mine.reshape(DRAFT, head_count, q_cols + kv_cols)

time: 200 us -> 212 us (1.060)
  local copies, waits for them, and re-layouts: 42.6 us -> 56.6 us
  waiting for transfers between devices: 34.5 us -> 28.6 us
  other arithmetic: 7.76 us -> 13.1 us
    dynamic_update_slice x16, local copies, waits for them, and re-layouts: 0.31 us -> 10.1 us  [grid_gather(): lax.dynamic_update_slice(column, part[None], ((z_index + offset) % z_size...]
    all_to_all x1, waiting for transfers between devices: 10.7 us -> 7.1 us  [shards(): mine = lax.all_to_all(both, 'head', 0, 1, tiled=True)]
  transfers between devices with their start and end apart: 23 -> 23, of which waited for: 5 -> 4; matrix products, arithmetic and copies ran while one was open for 19% -> 24% of each run, Pallas kernels for 0% -> 0%
where the time goes in v6:
time: 212 us; the launch traced here: 211 us
  starting transfers between devices  84.4 us (40%)
  local copies, waits for them, and re-layouts  56.6 us (27%)
  waiting for transfers between devices  28.6 us (13%)
  between operations  17 us (8%)
  other arithmetic  13.1 us (6%)
  matrix products  11.2 us (5%)
    ppermute x8, starting transfers between devices, ring_pieces(): behind = lax.ppermute(behind, axis, backward)  41.3 us
    ppermute x8, starting transfers between devices, ring_pieces(): ahead = lax.ppermute(ahead, axis, forward)  17.7 us
    ppermute x8, waiting for transfers between devices, ring_pieces(): behind = lax.ppermute(behind, axis, backward)  11.8 us
    all_to_all x1, starting transfers between devices, shards(): mine = lax.all_to_all(both, 'head', 0, 1, tiled=True)  11.6 us
    dynamic_update_slice x16, local copies, waits for them, and re-layouts, grid_gather(): lax.dynamic_update_slice(column, part[None], ((z_index + offset) % z_size...  10.1 us
    ppermute x2, starting transfers between devices, ring_pieces(): got.append((step, half, lax.ppermute(behind[half:], axis, backward)))  9.79 us
    ppermute x2, waiting for transfers between devices, ring_pieces(): got.append((step, 0, lax.ppermute(ahead[:half], axis, forward)))  8.45 us
    slice x3, local copies, waits for them, and re-layouts, shards(): stacked[:, part_rows:].reshape(tok_count, -1)[:, :wo_flat.shape[0]]  7.46 us
  transfers between devices with their start and end apart: 23, of which 4 were waited for; matrix products, arithmetic and copies ran while one was open for 24% of the time, Pallas kernels for 0%

profile of v6, /device:TPU:1, one launch (start us, length us, event | category | flops | bytes accessed | tf_op | source)
XLA Modules:
  0.0 210.9 jit_solution(16828217077579279007)
XLA Ops:
  7.3 1.2 copy.42
  8.5 1.0 reshape.344
  9.5 0.8 constant_dynamic-slice_fusion.1
  10.3 0.9 constant_dynamic-slice_fusion.2
  11.1 1.0 broadcast_in_dim.137
  12.2 0.7 bitcast_dynamic-update-slice_fusion.19
  12.9 4.4 %collective-permute-start = (bf16[80,384]{1,0:T(8,128)(2,1)S(1)}, bf16[80,384]{1,0:T(8,128)(2,1)S(1)}, u32[]{:S(2)}, u32[]{:S(2)}) collective-permute-start(bf16[80,384]{1,0:T(8,128)(2,1)S(1)} %get-tuple-element.10), channel_id=1, source_target_pairs={{0,32},{32,64},{64,96},{96,128},{128,160},{160,192},{192,224},{224... | collective-permute-start | bytes 184328 | tf_op jit(solution)/shard_map/ppermute | solution.py:104
  17.2 9.5 %collective-permute-start.1 = (bf16[80,384]{1,0:T(8,128)(2,1)S(1)}, bf16[80,384]{1,0:T(8,128)(2,1)S(1)}, u32[]{:S(2)}, u32[]{:S(2)}) collective-permute-start(bf16[80,384]{1,0:T(8,128)(2,1)S(1)} %get-tuple-element.10), channel_id=1, source_target_pairs={{0,480},{32,0},{64,32},{96,64},{128,96},{160,128},{192,160},{224,1... | collective-permute-start | bytes 184328 | tf_op jit(solution)/shard_map/ppermute | solution.py:107
  26.8 0.7 fusion.38
  32.0 0.7 iota_subtract_fusion
  33.2 0.7 iota_compare_fusion.6
  33.9 1.9 collective-permute-start.2
  35.8 4.6 %collective-permute-start.3 = (bf16[80,384]{1,0:T(8,128)(2,1)S(1)}, bf16[80,384]{1,0:T(8,128)(2,1)S(1)}, u32[]{:S(2)}, u32[]{:S(2)}) collective-permute-start(bf16[80,384]{1,0:T(8,128)(2,1)S(1)} %collective-permute-done.1), channel_id=1, source_target_pairs={{0,480},{32,0},{64,32},{96,64},{128,96},{160,128},{192,160},{224,1... | collective-permute-start | bytes 184328 | tf_op jit(solution)/shard_map/ppermute | solution.py:107
  40.4 0.6 bitcast_dynamic-update-slice_fusion.18
  41.7 1.9 collective-permute-start.4
  43.6 4.6 %collective-permute-start.5 = (bf16[80,384]{1,0:T(8,128)(2,1)S(1)}, bf16[80,384]{1,0:T(8,128)(2,1)S(1)}, u32[]{:S(2)}, u32[]{:S(2)}) collective-permute-start(bf16[80,384]{1,0:T(8,128)(2,1)S(1)} %collective-permute-done.3), channel_id=1, source_target_pairs={{0,480},{32,0},{64,32},{96,64},{128,96},{160,128},{192,160},{224,1... | collective-permute-start | bytes 184328 | tf_op jit(solution)/shard_map/ppermute | solution.py:107
  48.8 0.6 bitcast_dynamic-update-slice_fusion.15
  49.5 1.9 collective-permute-start.6
  51.4 4.6 %collective-permute-start.7 = (bf16[80,384]{1,0:T(8,128)(2,1)S(1)}, bf16[80,384]{1,0:T(8,128)(2,1)S(1)}, u32[]{:S(2)}, u32[]{:S(2)}) collective-permute-start(bf16[80,384]{1,0:T(8,128)(2,1)S(1)} %collective-permute-done.5), channel_id=1, source_target_pairs={{0,480},{32,0},{64,32},{96,64},{128,96},{160,128},{192,160},{224,1... | collective-permute-start | bytes 184328 | tf_op jit(solution)/shard_map/ppermute | solution.py:107
  56.0 0.6 bitcast_dynamic-update-slice_fusion.14
  57.2 1.9 collective-permute-start.8
  59.2 4.6 %collective-permute-start.9 = (bf16[80,384]{1,0:T(8,128)(2,1)S(1)}, bf16[80,384]{1,0:T(8,128)(2,1)S(1)}, u32[]{:S(2)}, u32[]{:S(2)}) collective-permute-start(bf16[80,384]{1,0:T(8,128)(2,1)S(1)} %collective-permute-done.7), channel_id=1, source_target_pairs={{0,480},{32,0},{64,32},{96,64},{128,96},{160,128},{192,160},{224,1... | collective-permute-start | bytes 184328 | tf_op jit(solution)/shard_map/ppermute | solution.py:107
  63.8 0.6 bitcast_dynamic-update-slice_fusion.12
  64.4 0.6 bitcast_dynamic-update-slice_fusion.11
  65.0 1.9 collective-permute-start.10
  67.0 4.6 %collective-permute-start.11 = (bf16[80,384]{1,0:T(8,128)(2,1)S(1)}, bf16[80,384]{1,0:T(8,128)(2,1)S(1)}, u32[]{:S(2)}, u32[]{:S(2)}) collective-permute-start(bf16[80,384]{1,0:T(8,128)(2,1)S(1)} %collective-permute-done.9), channel_id=1, source_target_pairs={{0,480},{32,0},{64,32},{96,64},{128,96},{160,128},{192,160},{224,1... | collective-permute-start | bytes 184328 | tf_op jit(solution)/shard_map/ppermute | solution.py:107
  72.8 1.9 collective-permute-start.12
  74.7 4.6 %collective-permute-start.13 = (bf16[80,384]{1,0:T(8,128)(2,1)S(1)}, bf16[80,384]{1,0:T(8,128)(2,1)S(1)}, u32[]{:S(2)}, u32[]{:S(2)}) collective-permute-start(bf16[80,384]{1,0:T(8,128)(2,1)S(1)} %collective-permute-done.11), channel_id=1, source_target_pairs={{0,480},{32,0},{64,32},{96,64},{128,96},{160,128},{192,160},{224,1... | collective-permute-start | bytes 184328 | tf_op jit(solution)/shard_map/ppermute | solution.py:107
  79.3 0.6 bitcast_dynamic-update-slice_fusion.8
  80.6 1.9 collective-permute-start.14
  82.5 4.6 %collective-permute-start.15 = (bf16[40,384]{1,0:T(8,128)(2,1)S(1)}, bf16[40,384]{1,0:T(8,128)(2,1)S(1)}, u32[]{:S(2)}, u32[]{:S(2)}) collective-permute-start(bf16[40,384]{1,0:T(8,128)(2,1)S(1)} %slice.130), channel_id=1, source_target_pairs={{0,480},{32,0},{64,32},{96,64},{128,96},{160,128},{192,160},{224,1... | collective-permute-start | bytes 92168 | tf_op jit(solution)/shard_map/ppermute | solution.py:102
  87.1 0.6 bitcast_dynamic-update-slice_fusion.6
  89.6 3.0 %copy.43 = bf16[512,2560]{1,0:T(8,128)(2,1)S(1)} copy(bf16[512,2560]{0,1:T(8,128)(2,1)} %all-gather.3.cloned.1.call-done) | data formatting | bytes 5242880 | tf_op jit(solution)/shard_map/all_gather | solution.py:162
  93.2 2.0 fusion.1
  95.2 4.4 %collective-permute-start.17 = (bf16[16,80,384]{2,1,0:T(8,128)(2,1)}, bf16[16,80,384]{2,1,0:T(8,128)(2,1)S(1)}, u32[]{:S(2)}, u32[]{:S(2)}) collective-permute-start(bf16[16,80,384]{2,1,0:T(8,128)(2,1)} %bitcast_dynamic-update-slice_fusion.20), channel_id=1, source_target_pairs={{0,24},{8,0},{16,8},{24,16},{1,25},{9,1},{17,9},{25,17},{2,26},{10... | collective-permute-start | bytes 2949128 | tf_op jit(solution)/shard_map/ppermute | solution.py:107
  99.5 1.9 collective-permute-start.16
  102.9 1.4 bitcast_dynamic-update-slice_fusion.2
  104.3 11.8 %collective-permute-done.17 = bf16[16,80,384]{2,1,0:T(8,128)(2,1)S(1)} collective-permute-done((bf16[16,80,384]{2,1,0:T(8,128)(2,1)}, bf16[16,80,384]{2,1,0:T(8,128)(2,1)S(1)}, u32[]{:S(2)}, u32[]{:S(2)}) %collective-permute-start.17) | collective-permute-done | bytes 983072 | tf_op jit(solution)/shard_map/ppermute | solution.py:107
  116.1 5.2 %collective-permute-start.19 = (bf16[8,80,384]{2,1,0:T(8,128)(2,1)S(1)}, bf16[8,80,384]{2,1,0:T(8,128)(2,1)S(1)}, u32[]{:S(2)}, u32[]{:S(2)}) collective-permute-start(bf16[8,80,384]{2,1,0:T(8,128)(2,1)S(1)} %slice.132), channel_id=1, source_target_pairs={{0,24},{8,0},{16,8},{24,16},{1,25},{9,1},{17,9},{25,17},{2,26},{10... | collective-permute-start | bytes 1474568 | tf_op jit(solution)/shard_map/ppermute | solution.py:102
  121.4 1.9 collective-permute-start.18
  123.8 8.4 %collective-permute-done.18 = bf16[8,80,384]{2,1,0:T(8,128)(2,1)S(1)} collective-permute-done((bf16[8,80,384]{2,1,0:T(8,128)(2,1)S(1)}, bf16[8,80,384]{2,1,0:T(8,128)(2,1)S(1)}, u32[]{:S(2)}, u32[]{:S(2)}) %collective-permute-start.18) | collective-permute-done | bytes 491552 | tf_op jit(solution)/shard_map/ppermute | solution.py:101
  132.8 1.3 copy-done.2
  134.1 2.4 %fusion.50 = f32[8,64,384]{2,1,0:T(8,128)} fusion(bf16[8,64,2560]{2,1,0:T(8,128)(2,1)S(1)} %bitcast.129, bf16[2560,384,1]{1,0,2:T(8,128)(2,1)S(1)} %bitcast.130), kind=kOutput, calls=%fused_computation.132 | convolution fusion | flops 1006632960 | bytes 5373952 | tf_op jit(solution)/shard_map/dot_general | solution.py:176
  136.5 11.6 %all-to-all-start = ((f32[8,64,384]{2,1,0:T(8,128)}), f32[8,64,384]{2,1,0:T(8,128)S(1)}, u32[]{:S(2)}, u32[]{:S(2)}) async-start(f32[8,64,384]{2,1,0:T(8,128)} %fusion.50), calls=%async_computation | async-start | bytes 1572864 | tf_op jit(solution)/shard_map/all_to_all | solution.py:177
  148.8 0.7 copy.48
  149.4 1.4 gather_fusion
  150.8 1.1 add_add_fusion
  152.5 0.7 fusion.19
  153.2 7.1 %all-to-all-done = f32[8,64,384]{2,1,0:T(8,128)S(1)} async-done(((f32[8,64,384]{2,1,0:T(8,128)}), f32[8,64,384]{2,1,0:T(8,128)S(1)}, u32[]{:S(2)}, u32[]{:S(2)}) %all-to-all-start) | async-done | bytes 786464 | tf_op jit(solution)/shard_map/all_to_all | solution.py:177
  160.8 1.1 convolution_convert_fusion
  161.9 1.4 copy.44
  163.2 1.6 reshape.348
  166.3 1.0 fusion.13
  169.4 1.2 fusion.5
  170.7 3.8 %copy.51 = bf16[64,40,384]{0,2,1:T(8,128)(2,1)} copy(bf16[64,40,384]{2,1,0:T(8,128)(2,1)S(1)} %get-tuple-element.11) | data formatting | bytes 3932160 | tf_op jit(solution)/shard_map/slice | solution.py:170
  174.5 3.3 %slice.145 = bf16[64,12800]{0,1:T(8,128)(2,1)} slice(bf16[64,15360]{0,1:T(8,128)(2,1)} %bitcast.126), slice={[0:64], [0:12800]} | slice | bytes 3276800 | tf_op jit(solution)/shard_map/slice | solution.py:170
  177.8 7.2 %reshape.354 = bf16[64,2560,5]{0,2,1:T(8,128)(2,1)} reshape(bf16[64,12800]{0,1:T(8,128)(2,1)} %slice.145) | data formatting | bytes 3276800 | tf_op jit(solution)/shard_map/reshape | solution.py:172
  185.0 7.1 %copy.52 = bf16[2560,64,5]{0,2,1:T(8,128)(2,1)S(1)} copy(bf16[2560,64,5]{1,2,0:T(8,128)(2,1)} %bitcast.124) | data formatting | bytes 3276800 | tf_op jit(solution)/shard_map/transpose | solution.py:173
  192.0 3.1 %reshape_reshape.3 = bf16[10,256,320]{1,0,2:T(8,128)(2,1)} reshape(bf16[2560,64,5]{0,2,1:T(8,128)(2,1)S(1)} %copy.52) | data formatting | bytes 3276800 | tf_op jit(solution)/shard_map/reshape;reshape | solution.py:209
  195.1 1.6 gather_fusion.1
  196.8 0.9 broadcast_select_fusion
  197.7 1.2 all-gather.5.cloned.1.call-done
  198.9 4.0 %fusion.49 = (bf16[10,512,320]{1,2,0:T(8,128)(2,1)S(1)}, f32[10,512,320]{1,2,0:T(8,128)S(1)}) fusion(bf16[10,512,256]{2,1,0:T(8,128)(2,1)} %all-gather.5.cloned.1.call-done, bf16[10,256,320]{1,0,2:T(8,128)(2,1)} %reshape_reshape.3), kind=kOutput, calls=%fused_computation.131 | convolution fusion | flops 840499200 | bytes 14090240 | tf_op jit(solution)/shard_map/dot_general | solution.py:207
  202.9 1.2 fusion.14
  (139 shorter events, 16.8 us)
Async XLA Ops:
  7.2 142.3 %copy-start = (bf16[4,2,128,256]{3,2,1,0:T(8,128)(2,1)S(1)}, bf16[4,2,128,256]{3,2,1,0:T(8,128)(2,1)}, u32[]{:S(2)}) copy-start(bf16[4,2,128,256]{3,2,1,0:T(8,128)(2,1)} %param.15) | copy-start | bytes 1572868
  7.2 20.3 %copy-start.18 = (s32[8,4]{0,1:T(4,128)S(1)}, s32[8,4]{0,1:T(4,128)}, u32[]{:S(2)}) copy-start(s32[8,4]{0,1:T(4,128)} %param.16) | copy-start | bytes 388
  7.2 21.7 %copy-start.25 = (s32[8]{0:T(128)S(1)}, s32[8]{0:T(128)}, u32[]{:S(2)}) copy-start(s32[8]{0:T(128)} %param.19) | copy-start | bytes 100
  7.2 23.6 %copy-start.26 = (s32[8]{0:T(128)S(1)}, s32[8]{0:T(128)}, u32[]{:S(2)}) copy-start(s32[8]{0:T(128)} %param.18) | copy-start | bytes 100
  7.2 82.4 %all-gather.3.cloned.1.call-start = ((), (), s32[]{:S(2)}) async-start(), calls=%async_computation.1 | async-start | bytes 2949120 | tf_op jit(solution)/shard_map/all_gather | solution.py:162
  12.9 21.0 %collective-permute-start = (bf16[80,384]{1,0:T(8,128)(2,1)S(1)}, bf16[80,384]{1,0:T(8,128)(2,1)S(1)}, u32[]{:S(2)}, u32[]{:S(2)}) collective-permute-start(bf16[80,384]{1,0:T(8,128)(2,1)S(1)} %get-tuple-element.10), channel_id=1, source_target_pairs={{0,32},{32,64},{64,96},{96,128},{128,160},{160,192},{192,224},{224... | collective-permute-start | bytes 184328 | tf_op jit(solution)/shard_map/ppermute | solution.py:104
  17.2 18.6 %collective-permute-start.1 = (bf16[80,384]{1,0:T(8,128)(2,1)S(1)}, bf16[80,384]{1,0:T(8,128)(2,1)S(1)}, u32[]{:S(2)}, u32[]{:S(2)}) collective-permute-start(bf16[80,384]{1,0:T(8,128)(2,1)S(1)} %get-tuple-element.10), channel_id=1, source_target_pairs={{0,480},{32,0},{64,32},{96,64},{128,96},{160,128},{192,160},{224,1... | collective-permute-start | bytes 184328 | tf_op jit(solution)/shard_map/ppermute | solution.py:107
  27.8 64.8 %copy-start.22 = (s32[4]{0:T(128)}, s32[4]{0:T(128)S(1)}, u32[]{:S(2)}) copy-start(s32[4]{0:T(128)S(1)} %select_reduce_fusion) | copy-start | bytes 52
  32.7 128.1 %copy-start.11 = (s32[512]{0:T(512)}, s32[512]{0:T(512)S(1)}, u32[]{:S(2)}) copy-start(s32[512]{0:T(512)S(1)} %iota_subtract_fusion) | copy-start | bytes 6148
  33.9 7.8 %collective-permute-start.2 = (bf16[80,384]{1,0:T(8,128)(2,1)S(1)}, bf16[80,384]{1,0:T(8,128)(2,1)S(1)}, u32[]{:S(2)}, u32[]{:S(2)}) collective-permute-start(bf16[80,384]{1,0:T(8,128)(2,1)S(1)} %collective-permute-done), channel_id=1, source_target_pairs={{0,32},{32,64},{64,96},{96,128},{128,160},{160,192},{192,224},{224... | collective-permute-start | bytes 184328 | tf_op jit(solution)/shard_map/ppermute | solution.py:104
  35.8 7.8 %collective-permute-start.3 = (bf16[80,384]{1,0:T(8,128)(2,1)S(1)}, bf16[80,384]{1,0:T(8,128)(2,1)S(1)}, u32[]{:S(2)}, u32[]{:S(2)}) collective-permute-start(bf16[80,384]{1,0:T(8,128)(2,1)S(1)} %collective-permute-done.1), channel_id=1, source_target_pairs={{0,480},{32,0},{64,32},{96,64},{128,96},{160,128},{192,160},{224,1... | collective-permute-start | bytes 184328 | tf_op jit(solution)/shard_map/ppermute | solution.py:107
  41.7 7.8 %collective-permute-start.4 = (bf16[80,384]{1,0:T(8,128)(2,1)S(1)}, bf16[80,384]{1,0:T(8,128)(2,1)S(1)}, u32[]{:S(2)}, u32[]{:S(2)}) collective-permute-start(bf16[80,384]{1,0:T(8,128)(2,1)S(1)} %collective-permute-done.2), channel_id=1, source_target_pairs={{0,32},{32,64},{64,96},{96,128},{128,160},{160,192},{192,224},{224... | collective-permute-start | bytes 184328 | tf_op jit(solution)/shard_map/ppermute | solution.py:104
  43.6 7.8 %collective-permute-start.5 = (bf16[80,384]{1,0:T(8,128)(2,1)S(1)}, bf16[80,384]{1,0:T(8,128)(2,1)S(1)}, u32[]{:S(2)}, u32[]{:S(2)}) collective-permute-start(bf16[80,384]{1,0:T(8,128)(2,1)S(1)} %collective-permute-done.3), channel_id=1, source_target_pairs={{0,480},{32,0},{64,32},{96,64},{128,96},{160,128},{192,160},{224,1... | collective-permute-start | bytes 184328 | tf_op jit(solution)/shard_map/ppermute | solution.py:107
  49.5 7.8 %collective-permute-start.6 = (bf16[80,384]{1,0:T(8,128)(2,1)S(1)}, bf16[80,384]{1,0:T(8,128)(2,1)S(1)}, u32[]{:S(2)}, u32[]{:S(2)}) collective-permute-start(bf16[80,384]{1,0:T(8,128)(2,1)S(1)} %collective-permute-done.4), channel_id=1, source_target_pairs={{0,32},{32,64},{64,96},{96,128},{128,160},{160,192},{192,224},{224... | collective-permute-start | bytes 184328 | tf_op jit(solution)/shard_map/ppermute | solution.py:104
  51.4 7.8 %collective-permute-start.7 = (bf16[80,384]{1,0:T(8,128)(2,1)S(1)}, bf16[80,384]{1,0:T(8,128)(2,1)S(1)}, u32[]{:S(2)}, u32[]{:S(2)}) collective-permute-start(bf16[80,384]{1,0:T(8,128)(2,1)S(1)} %collective-permute-done.5), channel_id=1, source_target_pairs={{0,480},{32,0},{64,32},{96,64},{128,96},{160,128},{192,160},{224,1... | collective-permute-start | bytes 184328 | tf_op jit(solution)/shard_map/ppermute | solution.py:107
  57.2 7.8 %collective-permute-start.8 = (bf16[80,384]{1,0:T(8,128)(2,1)S(1)}, bf16[80,384]{1,0:T(8,128)(2,1)S(1)}, u32[]{:S(2)}, u32[]{:S(2)}) collective-permute-start(bf16[80,384]{1,0:T(8,128)(2,1)S(1)} %collective-permute-done.6), channel_id=1, source_target_pairs={{0,32},{32,64},{64,96},{96,128},{128,160},{160,192},{192,224},{224... | collective-permute-start | bytes 184328 | tf_op jit(solution)/shard_map/ppermute | solution.py:104
  59.2 7.8 %collective-permute-start.9 = (bf16[80,384]{1,0:T(8,128)(2,1)S(1)}, bf16[80,384]{1,0:T(8,128)(2,1)S(1)}, u32[]{:S(2)}, u32[]{:S(2)}) collective-permute-start(bf16[80,384]{1,0:T(8,128)(2,1)S(1)} %collective-permute-done.7), channel_id=1, source_target_pairs={{0,480},{32,0},{64,32},{96,64},{128,96},{160,128},{192,160},{224,1... | collective-permute-start | bytes 184328 | tf_op jit(solution)/shard_map/ppermute | solution.py:107
  65.0 7.8 %collective-permute-start.10 = (bf16[80,384]{1,0:T(8,128)(2,1)S(1)}, bf16[80,384]{1,0:T(8,128)(2,1)S(1)}, u32[]{:S(2)}, u32[]{:S(2)}) collective-permute-start(bf16[80,384]{1,0:T(8,128)(2,1)S(1)} %collective-permute-done.8), channel_id=1, source_target_pairs={{0,32},{32,64},{64,96},{96,128},{128,160},{160,192},{192,224},{224... | collective-permute-start | bytes 184328 | tf_op jit(solution)/shard_map/ppermute | solution.py:104
  67.0 7.8 %collective-permute-start.11 = (bf16[80,384]{1,0:T(8,128)(2,1)S(1)}, bf16[80,384]{1,0:T(8,128)(2,1)S(1)}, u32[]{:S(2)}, u32[]{:S(2)}) collective-permute-start(bf16[80,384]{1,0:T(8,128)(2,1)S(1)} %collective-permute-done.9), channel_id=1, source_target_pairs={{0,480},{32,0},{64,32},{96,64},{128,96},{160,128},{192,160},{224,1... | collective-permute-start | bytes 184328 | tf_op jit(solution)/shard_map/ppermute | solution.py:107
  72.8 7.8 %collective-permute-start.12 = (bf16[80,384]{1,0:T(8,128)(2,1)S(1)}, bf16[80,384]{1,0:T(8,128)(2,1)S(1)}, u32[]{:S(2)}, u32[]{:S(2)}) collective-permute-start(bf16[80,384]{1,0:T(8,128)(2,1)S(1)} %collective-permute-done.10), channel_id=1, source_target_pairs={{0,32},{32,64},{64,96},{96,128},{128,160},{160,192},{192,224},{224... | collective-permute-start | bytes 184328 | tf_op jit(solution)/shard_map/ppermute | solution.py:104
  74.7 7.8 %collective-permute-start.13 = (bf16[80,384]{1,0:T(8,128)(2,1)S(1)}, bf16[80,384]{1,0:T(8,128)(2,1)S(1)}, u32[]{:S(2)}, u32[]{:S(2)}) collective-permute-start(bf16[80,384]{1,0:T(8,128)(2,1)S(1)} %collective-permute-done.11), channel_id=1, source_target_pairs={{0,480},{32,0},{64,32},{96,64},{128,96},{160,128},{192,160},{224,1... | collective-permute-start | bytes 184328 | tf_op jit(solution)/shard_map/ppermute | solution.py:107
  80.6 7.8 %collective-permute-start.14 = (bf16[40,384]{1,0:T(8,128)(2,1)S(1)}, bf16[40,384]{1,0:T(8,128)(2,1)S(1)}, u32[]{:S(2)}, u32[]{:S(2)}) collective-permute-start(bf16[40,384]{1,0:T(8,128)(2,1)S(1)} %slice.129), channel_id=1, source_target_pairs={{0,32},{32,64},{64,96},{96,128},{128,160},{160,192},{192,224},{224... | collective-permute-start | bytes 92168 | tf_op jit(solution)/shard_map/ppermute | solution.py:101
  82.5 6.4 %collective-permute-start.15 = (bf16[40,384]{1,0:T(8,128)(2,1)S(1)}, bf16[40,384]{1,0:T(8,128)(2,1)S(1)}, u32[]{:S(2)}, u32[]{:S(2)}) collective-permute-start(bf16[40,384]{1,0:T(8,128)(2,1)S(1)} %slice.130), channel_id=1, source_target_pairs={{0,480},{32,0},{64,32},{96,64},{128,96},{160,128},{192,160},{224,1... | collective-permute-start | bytes 92168 | tf_op jit(solution)/shard_map/ppermute | solution.py:102
  95.2 20.9 %collective-permute-start.17 = (bf16[16,80,384]{2,1,0:T(8,128)(2,1)}, bf16[16,80,384]{2,1,0:T(8,128)(2,1)S(1)}, u32[]{:S(2)}, u32[]{:S(2)}) collective-permute-start(bf16[16,80,384]{2,1,0:T(8,128)(2,1)} %bitcast_dynamic-update-slice_fusion.20), channel_id=1, source_target_pairs={{0,24},{8,0},{16,8},{24,16},{1,25},{9,1},{17,9},{25,17},{2,26},{10... | collective-permute-start | bytes 2949128 | tf_op jit(solution)/shard_map/ppermute | solution.py:107
  99.5 21.8 %collective-permute-start.16 = (bf16[16,80,384]{2,1,0:T(8,128)(2,1)}, bf16[16,80,384]{2,1,0:T(8,128)(2,1)S(1)}, u32[]{:S(2)}, u32[]{:S(2)}) collective-permute-start(bf16[16,80,384]{2,1,0:T(8,128)(2,1)} %bitcast_dynamic-update-slice_fusion.20), channel_id=1, source_target_pairs={{0,8},{8,16},{16,24},{24,0},{1,9},{9,17},{17,25},{25,1},{2,10},{10... | collective-permute-start | bytes 2949128 | tf_op jit(solution)/shard_map/ppermute | solution.py:104
  101.5 59.3 %copy-start.13 = (pred[64]{0:T(512)(128)(4,1)}, pred[64]{0:T(512)(128)(4,1)S(1)}, u32[]{:S(2)}) copy-start(pred[64]{0:T(512)(128)(4,1)S(1)} %compare_bitcast_fusion.1) | copy-start | bytes 196
  101.7 59.1 %copy-start.15 = (s32[64]{0:T(128)}, s32[64]{0:T(128)S(1)}, u32[]{:S(2)}) copy-start(s32[64]{0:T(128)S(1)} %add_convert_fusion.2) | copy-start | bytes 772
  116.1 16.2 %collective-permute-start.19 = (bf16[8,80,384]{2,1,0:T(8,128)(2,1)S(1)}, bf16[8,80,384]{2,1,0:T(8,128)(2,1)S(1)}, u32[]{:S(2)}, u32[]{:S(2)}) collective-permute-start(bf16[8,80,384]{2,1,0:T(8,128)(2,1)S(1)} %slice.132), channel_id=1, source_target_pairs={{0,24},{8,0},{16,8},{24,16},{1,25},{9,1},{17,9},{25,17},{2,26},{10... | collective-permute-start | bytes 1474568 | tf_op jit(solution)/shard_map/ppermute | solution.py:102
  121.4 10.8 %collective-permute-start.18 = (bf16[8,80,384]{2,1,0:T(8,128)(2,1)S(1)}, bf16[8,80,384]{2,1,0:T(8,128)(2,1)S(1)}, u32[]{:S(2)}, u32[]{:S(2)}) collective-permute-start(bf16[8,80,384]{2,1,0:T(8,128)(2,1)S(1)} %slice.131), channel_id=1, source_target_pairs={{0,8},{8,16},{16,24},{24,0},{1,9},{9,17},{17,25},{25,1},{2,10},{10... | collective-permute-start | bytes 1474568 | tf_op jit(solution)/shard_map/ppermute | solution.py:101
  132.4 1.7 copy-start.2
  136.5 23.8 %all-to-all-start = ((f32[8,64,384]{2,1,0:T(8,128)}), f32[8,64,384]{2,1,0:T(8,128)S(1)}, u32[]{:S(2)}, u32[]{:S(2)}) async-start(f32[8,64,384]{2,1,0:T(8,128)} %fusion.50), calls=%async_computation | async-start | bytes 1572864 | tf_op jit(solution)/shard_map/all_to_all | solution.py:177
  148.2 50.7 %all-gather.5.cloned.1.call-start = ((), (), s32[]{:S(2)}) async-start(), calls=%async_computation.2 | async-start | bytes 2949120 | tf_op jit(solution)/shard_map/all_gather | solution.py:206
  160.7 2.5 %copy-start.5 = (f32[64,512]{1,0:T(8,128)}, f32[64,512]{1,0:T(8,128)S(1)}, u32[]{:S(2)}) copy-start(f32[64,512]{1,0:T(8,128)S(1)} %reshape.349) | copy-start | bytes 393220
  160.8 2.5 %copy-start.7 = (bf16[64,512]{1,0:T(8,128)(2,1)}, bf16[64,512]{1,0:T(8,128)(2,1)S(1)}, u32[]{:S(2)}) copy-start(bf16[64,512]{1,0:T(8,128)(2,1)S(1)} %convert.35) | copy-start | bytes 196612
  164.8 0.9 copy-start.6
  164.8 0.9 copy-start.17
  164.8 0.9 copy-start.21
  164.8 1.1 copy-start.12
  164.8 1.1 copy-start.14
  164.8 1.1 copy-start.16
  164.8 1.4 copy-start.3
  164.9 1.4 copy-start.4
  164.9 1.4 copy-start.20
  164.9 1.4 copy-start.24
  166.3 1.3 copy-start.10
  167.3 0.8 copy-start.9
  167.6 1.5 copy-start.8
  169.4 1.2 copy-start.19
  169.4 1.2 copy-start.23
  198.9 5.2 %copy-start.1 = (bf16[4,2,128,256]{3,2,1,0:T(8,128)(2,1)S(1)}, bf16[4,2,128,256]{3,2,1,0:T(8,128)(2,1)}, u32[]{:S(2)}) copy-start(bf16[4,2,128,256]{3,2,1,0:T(8,128)(2,1)} %param.15) | copy-start | bytes 1572868
Sparse Core Ops, SparseCore 0:
  26.9 32.5 all-gather.2
  170.8 28.0 all-gather.4
